TPU v7x, 256 devices: a whole 4x4x8 slice. The times are simulated.
256 devices in a mesh: grp: 16 (over x_hi, y, core), dom: 16 (over z, x_lo).
Axes of the slice: x: 4 (x_hi: 2, x_lo: 2; x = x_hi * 2 + x_lo), y: 4, z: 8, core: 2. Of those that a mesh axis runs over, the one named last changes fastest.
Arguments:
- positions: float32 [11264, 4096], P('grp', 'dom'), may hold values from 0 to 32
- energies: float32 [11264, 4096], P('grp', 'dom'), may hold values from -6 to 6
- bucket: int32 [11264], P('grp'), may hold values from 0 to 8191, as said below
- impedance: float32 [3, 2, 128, 128, 256], P(None, None, 'dom', 'grp'), may hold values from -6 to 6
- history: float32 [2, 2, 128, 128, 256], P(None, None, 'dom', 'grp'), may hold values from -1.8 to 1.8
Outputs:
- positions_out: float32 [11264, 4096], P('grp', 'dom')
- energies_out: float32 [11264, 4096], P('grp', 'dom')
- spectrum: float32 [2, 128, 128, 256], P(None, 'dom', 'grp')
Inputs may be any that keep to these rules, and one draw needn't show every extreme that they name: Within one train group no two bunches share a bucket; the first bunch of each group sits in bucket 0 and its last bunch in bucket 8192 - 1.
All inputs are finite; a program needn't handle non-finite values.
Results may differ from a plain program's by a relative error of at most 0.00013.
Values sent between devices are 32-bit elements; how exact they have to be, the bound alone decides.
No kernel may reach another device: no remote copies, remote signals or barrier semaphores. Data moves between devices by JAX's collectives and lax.ppermute only.
A program may use at most 64 MiB of HBM per device.

v0:
```python
import math

import jax
import jax.numpy as jnp
from jax import lax
from jax.sharding import PartitionSpec as P
from jax.experimental import pallas as pl
from jax.experimental.pallas import tpu as pltpu

BINS = 32
N3 = 256
R1 = 8
R2 = 8
HIST = 2
BUNCH_GRP = 704
P_DEV = 256


highest = lax.Precision.HIGHEST
two_pi = 2.0 * math.pi


def kernel_table(places):
    centers = jnp.arange(BINS, dtype=jnp.float32) + 0.5
    offset = places[:, None, :] - centers[None, :, None]
    return jnp.exp(-0.5 * offset * offset)


def dft_tables(length):
    series = jnp.arange(length, dtype=jnp.int32)
    windings = series[:, None] * series[None, :] % length
    angles = windings.astype(jnp.float32) * (two_pi / length)
    return (jnp.cos(angles), jnp.sin(angles))


def rotation(windings, modulus):
    angles = (windings % modulus).astype(jnp.float32) * (two_pi / modulus)
    return (jnp.cos(angles), jnp.sin(angles))


def contract(pattern, operand, matrix):
    return jnp.einsum(pattern, operand, matrix, precision=highest)


def block_table(length):
    cos_t, sin_t = dft_tables(length)
    return jnp.stack([jnp.stack([cos_t, -sin_t], axis=1), jnp.stack([sin_t, cos_t], axis=1)])


def conjugate(table):
    return table * jnp.array([1.0, -1.0], jnp.float32)[None, None, :, None] * jnp.array(
        [1.0, -1.0], jnp.float32
    )[:, None, None, None]


def turn(pair, cos_t, sin_t):
    return jnp.stack([pair[0] * cos_t - pair[1] * sin_t, pair[0] * sin_t + pair[1] * cos_t])


def dom_sum(rows, domains):
    chunk = rows.shape[0] // domains
    pieces = lax.all_to_all(rows.reshape(domains, chunk, BINS), "dom", 0, 0, tiled=True)
    mine = jnp.sum(pieces, axis=0)
    spread = jnp.broadcast_to(mine[None], (domains, chunk, BINS))
    return lax.all_to_all(spread, "dom", 0, 0, tiled=True).reshape(rows.shape)


KICK_ROWS = 64
SUB_ROWS = 8


def kick_kernel(pos_ref, drift_ref, volt_ref, pos_out, en_out):
    def sub_block(i, carry):
        rows = pl.ds(pl.multiple_of(i * SUB_ROWS, SUB_ROWS), SUB_ROWS)
        place = pos_ref[rows, :]
        volts = volt_ref[rows, :]
        weighted = jnp.zeros_like(place)
        norm = jnp.zeros_like(place)
        for j in range(BINS):
            offset = place - (j + 0.5)
            table = jnp.exp(-0.5 * offset * offset)
            weighted = weighted + table * volts[:, j : j + 1]
            norm = norm + table
        energy = drift_ref[rows, :] - weighted / norm
        en_out[rows, :] = energy
        pos_out[rows, :] = place + 0.25 * energy
        return carry

    lax.fori_loop(0, KICK_ROWS // SUB_ROWS, sub_block, 0)


def kick_call(positions, drifted, volt_rows):
    bunches, width = positions.shape
    wide = pl.BlockSpec((KICK_ROWS, width), lambda i: (i, 0))
    narrow = pl.BlockSpec((KICK_ROWS, BINS), lambda i: (i, 0))
    shape = jax.ShapeDtypeStruct(positions.shape, jnp.float32)
    return pl.pallas_call(
        kick_kernel,
        grid=(bunches // KICK_ROWS,),
        in_specs=[wide, wide, narrow],
        out_specs=[wide, wide],
        out_shape=[shape, shape],
        cost_estimate=pl.CostEstimate(
            flops=12 * bunches * width * BINS,
            transcendentals=bunches * width * BINS,
            bytes_accessed=4 * bunches * (4 * width + BINS),
        ),
    )(positions, drifted, volt_rows)


def on_device(positions, energies, bucket, impedance, history):
    groups = lax.axis_size("grp")
    domains = lax.axis_size("dom")
    group_index = lax.axis_index("grp")
    domain_index = lax.axis_index("dom")
    first_len = R1 * groups
    second_len = R2 * domains
    cycle_len = first_len * second_len * N3
    plane_len = second_len * N3
    depth_len = N3 // groups
    first_part = first_len // domains
    second_part = second_len // groups
    per_row = N3 // BINS
    row_buckets = second_len * per_row
    own_rows = R2 * per_row
    partial_value = jnp.sum(kernel_table(positions), axis=2) / float(P_DEV * domains)
    first_row = bucket // row_buckets
    within = bucket % row_buckets
    owner_dom = within // own_rows
    owned_here = owner_dom == domain_index
    slot = jnp.where(owned_here, first_row * own_rows + within - owner_dom * own_rows, -1)
    picker = (slot[None, :] == jnp.arange(R1 * own_rows, dtype=jnp.int32)[:, None]).astype(jnp.float32)
    totals = dom_sum(partial_value, domains)
    line_slab = contract("sb,bj->sj", picker, totals)
    density = line_slab.reshape(R1, R2, N3)
    first_table = block_table(first_len)
    second_table = block_table(second_len)
    third_table = block_table(N3)
    received = lax.all_to_all(density, "grp", split_axis=2, concat_axis=0, tiled=True)
    rows = contract("nab,nok->oabk", received, first_table[0])
    second_global = domain_index * R2 + jnp.arange(R2, dtype=jnp.int32)
    depth_global = group_index * depth_len + jnp.arange(depth_len, dtype=jnp.int32)
    first_freq = jnp.arange(first_len, dtype=jnp.int32)
    cos_turn, sin_turn = rotation(
        first_freq[None, None, :]
        * (second_global[:, None, None] * N3 + depth_global[None, :, None]),
        cycle_len,
    )
    twist = turn(rows, cos_turn, -sin_turn)
    part = lax.all_to_all(twist, "dom", split_axis=3, concat_axis=1, tiled=True)
    cols = contract("inbk,inom->obkm", part, second_table)
    second_freq = jnp.arange(second_len, dtype=jnp.int32)
    cos_turn, sin_turn = rotation(
        depth_global[:, None, None] * second_freq[None, None, :], plane_len
    )
    turned = turn(cols, cos_turn, -sin_turn)
    part = lax.all_to_all(turned, "grp", split_axis=3, concat_axis=1, tiled=True)
    full = contract("inac,inok->oack", part, third_table)
    norm_factor = 1.0 / math.sqrt(BUNCH_GRP * groups)
    spectrum = full * norm_factor
    spec_real = spectrum[0]
    spec_imag = spectrum[1]
    volt_real = impedance[0, 0] * spec_real - impedance[0, 1] * spec_imag
    volt_imag = impedance[0, 0] * spec_imag + impedance[0, 1] * spec_real
    for earlier in range(HIST):
        past_real = history[earlier, 0]
        past_imag = history[earlier, 1]
        volt_real = (
            volt_real
            + impedance[earlier + 1, 0] * past_real
            - impedance[earlier + 1, 1] * past_imag
        )
        volt_imag = (
            volt_imag
            + impedance[earlier + 1, 0] * past_imag
            + impedance[earlier + 1, 1] * past_real
        )
    back = contract("iack,ikon->oacn", jnp.stack([volt_real, volt_imag]), conjugate(third_table))
    second_own = group_index * second_part + jnp.arange(second_part, dtype=jnp.int32)
    depth_all = jnp.arange(N3, dtype=jnp.int32)
    cos_turn, sin_turn = rotation(second_own[None, :, None] * depth_all[None, None, :], plane_len)
    lift = turn(back, cos_turn, sin_turn)
    part = lax.all_to_all(lift, "grp", split_axis=3, concat_axis=2, tiled=True)
    spun = contract("iakb,ikon->oanb", part, conjugate(second_table))
    first_own = domain_index * first_part + jnp.arange(first_part, dtype=jnp.int32)
    cos_turn, sin_turn = rotation(
        first_own[:, None, None] * (second_freq[None, :, None] * N3 + depth_global[None, None, :]),
        cycle_len,
    )
    spin = turn(spun, cos_turn, sin_turn)
    inverse_factor = 1.0 / math.sqrt(cycle_len)
    part = lax.all_to_all(spin, "dom", split_axis=2, concat_axis=1, tiled=True)
    summed = contract("ikab,ikn->nab", part, conjugate(first_table)[:, :, 0, :])
    volt_part = summed * inverse_factor
    volt_slab = lax.all_to_all(volt_part, "grp", split_axis=0, concat_axis=2, tiled=True).reshape(
        R1 * own_rows, BINS
    )
    owned_volts = contract("sb,sj->bj", picker, volt_slab)
    volt_rows = dom_sum(owned_volts, domains)
    drifted = energies - 0.5 * jnp.sin(two_pi * (positions - 0.5 * BINS) / BINS)
    positions_out, energies_out = kick_call(positions, drifted, volt_rows)
    return (positions_out, energies_out, spectrum)


def solution(mesh):
    placed = (
        P("grp", "dom"),
        P("grp", "dom"),
        P("grp"),
        P(None, None, "dom", "grp", None),
        P(None, None, "dom", "grp", None),
    )
    return jax.shard_map(
        on_device,
        mesh=mesh,
        in_specs=placed,
        out_specs=(P("grp", "dom"), P("grp", "dom"), P(None, "dom", "grp", None)),
        check_vma=False,
    )
```

profile of v0, /device:TPU:2, one launch (start us, length us, event | category | flops | bytes accessed | tf_op | source)
XLA Modules:
  0.0 192.0 jit_solution(6633684927721607535)
XLA Ops:
  0.7 5.7 %fusion.1 = f32[704,32]{1,0:T(8,128)S(1)} fusion(f32[32]{0:T(128)S(1)} %iota_add_fusion.3, f32[704,256]{1,0:T(8,128)} %pos_ref.1), kind=kLoop, calls=%fused_computation.2 | loop fusion | flops 23046144 | bytes 811136 | tf_op jit(solution)/shard_map/reduce_sum | solution.py:126
  6.8 0.9 reshape.695
  7.7 9.9 %all-to-all-start = ((f32[16,1,1408]{2,1,0:T(1,128)}), f32[16,1,1408]{2,1,0:T(1,128)S(1)}, u32[]{:S(2)}, u32[]{:S(2)}) async-start(f32[16,1,1408]{2,1,0:T(1,128)} %reshape.695), calls=%async_computation | async-start | bytes 180224 | tf_op jit(solution)/shard_map/all_to_all | solution.py:62
  18.6 1.0 fusion.35
  19.6 6.1 %all-to-all-done = f32[16,1,1408]{2,1,0:T(1,128)S(1)} async-done(((f32[16,1,1408]{2,1,0:T(1,128)}), f32[16,1,1408]{2,1,0:T(1,128)S(1)}, u32[]{:S(2)}, u32[]{:S(2)}) %all-to-all-start) | async-done | bytes 90144 | tf_op jit(solution)/shard_map/all_to_all | solution.py:62
  26.3 0.8 reduce
  27.5 0.9 reshape.697
  28.4 4.6 %all-to-all-start.1 = ((f32[16,1,1408]{2,1,0:T(1,128)}), f32[16,1,1408]{2,1,0:T(1,128)S(1)}, u32[]{:S(2)}, u32[]{:S(2)}) async-start(f32[16,1,1408]{2,1,0:T(1,128)} %reshape.697), calls=%async_computation.1 | async-start | bytes 180224 | tf_op jit(solution)/shard_map/all_to_all | solution.py:65
  33.3 1.8 fusion.33
  35.1 6.0 %all-to-all-done.1 = f32[16,1,1408]{2,1,0:T(1,128)S(1)} async-done(((f32[16,1,1408]{2,1,0:T(1,128)}), f32[16,1,1408]{2,1,0:T(1,128)S(1)}, u32[]{:S(2)}, u32[]{:S(2)}) %all-to-all-start.1) | async-done | bytes 90144 | tf_op jit(solution)/shard_map/all_to_all | solution.py:65
  41.1 0.8 reduce.1
  42.5 0.8 fusion.5
  43.9 1.2 reshape.699
  45.1 6.1 %all-to-all-start.2 = ((f32[16,1,1024]{2,1,0:T(1,128)}), f32[16,1,1024]{2,1,0:T(1,128)S(1)}, u32[]{:S(2)}, u32[]{:S(2)}) async-start(f32[16,1,1024]{2,1,0:T(1,128)} %reshape.699), calls=%async_computation.2 | async-start | bytes 131072 | tf_op jit(solution)/shard_map/all_to_all | solution.py:139
  51.5 7.4 %all-to-all-done.2 = f32[16,1,1024]{2,1,0:T(1,128)S(1)} async-done(((f32[16,1,1024]{2,1,0:T(1,128)}), f32[16,1,1024]{2,1,0:T(1,128)S(1)}, u32[]{:S(2)}, u32[]{:S(2)}) %all-to-all-start.2) | async-done | bytes 65568 | tf_op jit(solution)/shard_map/all_to_all | solution.py:139
  62.0 1.0 reshape.701
  63.0 5.4 %all-to-all-start.3 = ((f32[16,1,2048]{2,1,0:T(1,128)}), f32[16,1,2048]{2,1,0:T(1,128)S(1)}, u32[]{:S(2)}, u32[]{:S(2)}) async-start(f32[16,1,2048]{2,1,0:T(1,128)} %reshape.701), calls=%async_computation.3 | async-start | bytes 262144 | tf_op jit(solution)/shard_map/all_to_all | solution.py:150
  68.4 0.9 multiply_multiply_fusion.1
  69.3 8.1 %all-to-all-done.3 = f32[16,1,2048]{2,1,0:T(1,128)S(1)} async-done(((f32[16,1,2048]{2,1,0:T(1,128)}), f32[16,1,2048]{2,1,0:T(1,128)S(1)}, u32[]{:S(2)}, u32[]{:S(2)}) %all-to-all-start.3) | async-done | bytes 131104 | tf_op jit(solution)/shard_map/all_to_all | solution.py:150
  77.4 0.9 reduce.3
  80.3 1.0 reshape.703
  81.3 3.5 %all-to-all-start.4 = ((f32[16,1,2048]{2,1,0:T(1,128)}), f32[16,1,2048]{2,1,0:T(1,128)S(1)}, u32[]{:S(2)}, u32[]{:S(2)}) async-start(f32[16,1,2048]{2,1,0:T(1,128)} %reshape.703), calls=%async_computation.4 | async-start | bytes 262144 | tf_op jit(solution)/shard_map/all_to_all | solution.py:157
  85.5 7.5 %all-to-all-done.4 = f32[16,1,2048]{2,1,0:T(1,128)S(1)} async-done(((f32[16,1,2048]{2,1,0:T(1,128)}), f32[16,1,2048]{2,1,0:T(1,128)S(1)}, u32[]{:S(2)}, u32[]{:S(2)}) %all-to-all-start.4) | async-done | bytes 131104 | tf_op jit(solution)/shard_map/all_to_all | solution.py:157
  93.0 0.9 reduce.4
  96.3 0.9 convolution_bitcast_fusion.2
  97.4 1.2 copy.122
  98.6 1.7 reshape.705
  100.3 3.7 %all-to-all-start.5 = ((f32[16,1,2048]{2,1,0:T(1,128)}), f32[16,1,2048]{2,1,0:T(1,128)S(1)}, u32[]{:S(2)}, u32[]{:S(2)}) async-start(f32[16,1,2048]{2,1,0:T(1,128)} %reshape.705), calls=%async_computation.5 | async-start | bytes 262144 | tf_op jit(solution)/shard_map/all_to_all | solution.py:183
  104.2 7.9 %all-to-all-done.5 = f32[16,1,2048]{2,1,0:T(1,128)S(1)} async-done(((f32[16,1,2048]{2,1,0:T(1,128)}), f32[16,1,2048]{2,1,0:T(1,128)S(1)}, u32[]{:S(2)}, u32[]{:S(2)}) %all-to-all-start.5) | async-done | bytes 131104 | tf_op jit(solution)/shard_map/all_to_all | solution.py:183
  112.0 0.9 reduce.5
  113.0 1.1 reshape.706
  114.1 1.1 copy.123
  115.2 1.8 convolution_bitcast_fusion.1
  118.2 12.8 %all_to_all.125 = f32[16,1,2048]{2,1,0:T(1,128)S(1)} all-to-all(f32[16,1,2048]{2,1,0:T(1,128)S(1)} %reshape.707), channel_id=1, replica_groups=mesh['grp'=16,'dom'=16] {'dom'}, dimensions={0} | all-to-all | bytes 262144 | tf_op jit(solution)/shard_map/all_to_all | solution.py:192
  131.0 0.9 reduce.6
  132.7 1.8 fusion.8
  134.7 0.9 reshape.709
  135.5 3.5 %all-to-all-start.7 = ((f32[16,1,1024]{2,1,0:T(1,128)}), f32[16,1,1024]{2,1,0:T(1,128)S(1)}, u32[]{:S(2)}, u32[]{:S(2)}) async-start(f32[16,1,1024]{2,1,0:T(1,128)} %reshape.709), calls=%async_computation.7 | async-start | bytes 131072 | tf_op jit(solution)/shard_map/all_to_all | solution.py:195
  139.2 7.5 %all-to-all-done.7 = f32[16,1,1024]{2,1,0:T(1,128)S(1)} async-done(((f32[16,1,1024]{2,1,0:T(1,128)}), f32[16,1,1024]{2,1,0:T(1,128)S(1)}, u32[]{:S(2)}, u32[]{:S(2)}) %all-to-all-start.7) | async-done | bytes 65568 | tf_op jit(solution)/shard_map/all_to_all | solution.py:195
  148.1 1.5 fusion.88
  149.9 12.0 %all_to_all.126 = f32[16,1,1408]{2,1,0:T(1,128)S(1)} all-to-all(f32[16,1,1408]{2,1,0:T(1,128)S(1)} %reshape.711), channel_id=1, replica_groups=mesh['grp'=16,'dom'=16] {'dom'}, dimensions={0} | all-to-all | bytes 180224 | tf_op jit(solution)/shard_map/all_to_all | solution.py:62
  161.9 0.8 reduce.8
  163.1 0.9 reshape.713
  164.1 4.7 %all-to-all-start.9 = ((f32[16,1,1408]{2,1,0:T(1,128)}), f32[16,1,1408]{2,1,0:T(1,128)S(1)}, u32[]{:S(2)}, u32[]{:S(2)}) async-start(f32[16,1,1408]{2,1,0:T(1,128)} %reshape.713), calls=%async_computation.9 | async-start | bytes 180224 | tf_op jit(solution)/shard_map/all_to_all | solution.py:65
  168.8 3.2 %multiply_subtract_fusion.drift_ref = f32[704,256]{1,0:T(8,128)} fusion(f32[704,256]{1,0:T(8,128)S(1)} %copy-done.6, f32[704,256]{1,0:T(8,128)S(1)} %copy-done.7), kind=kLoop, calls=%fused_computation.26 | loop fusion | flops 720896 | bytes 2162688 | tf_op jit(solution)/shard_map/sub | solution.py:200
  172.0 4.9 %all-to-all-done.9 = f32[16,1,1408]{2,1,0:T(1,128)S(1)} async-done(((f32[16,1,1408]{2,1,0:T(1,128)}), f32[16,1,1408]{2,1,0:T(1,128)S(1)}, u32[]{:S(2)}, u32[]{:S(2)}) %all-to-all-start.9) | async-done | bytes 90144 | tf_op jit(solution)/shard_map/all_to_all | solution.py:65
  176.8 0.8 reduce.9
  179.0 13.1 %shard_map.130 = (f32[704,256]{1,0:T(8,128)}, f32[704,256]{1,0:T(8,128)}) custom-call(f32[704,256]{1,0:T(8,128)} %pos_ref.1, f32[704,256]{1,0:T(8,128)} %multiply_subtract_fusion.drift_ref, f32[704,32]{1,0:T(8,128)} %reshape.694.volt_ref), custom_call_target="tpu_custom_call" | custom-call | flops 69206016 | bytes 2973696 | tf_op jit(solution)/shard_map/pallas_call | solution.py:97
  (105 shorter events, 17.5 us)
Async XLA Ops:
  0.6 17.0 %copy-start.13 = (s32[704]{0:T(1024)S(1)}, s32[704]{0:T(1024)}, u32[]{:S(2)}) copy-start(s32[704]{0:T(1024)} %param.13) | copy-start | bytes 8452
  7.7 18.0 %all-to-all-start = ((f32[16,1,1408]{2,1,0:T(1,128)}), f32[16,1,1408]{2,1,0:T(1,128)S(1)}, u32[]{:S(2)}, u32[]{:S(2)}) async-start(f32[16,1,1408]{2,1,0:T(1,128)} %reshape.695), calls=%async_computation | async-start | bytes 180224 | tf_op jit(solution)/shard_map/all_to_all | solution.py:62
  17.7 25.7 %copy-start.9 = (s32[704]{0:T(1024)}, s32[704]{0:T(1024)S(1)}, u32[]{:S(2)}) copy-start(s32[704]{0:T(1024)S(1)} %fusion.77) | copy-start | bytes 8452
  17.7 25.6 %copy-start.11 = (s32[16]{0:T(128)}, s32[16]{0:T(128)S(1)}, u32[]{:S(2)}) copy-start(s32[16]{0:T(128)S(1)} %iota_add_fusion.1) | copy-start | bytes 196
  28.4 12.7 %all-to-all-start.1 = ((f32[16,1,1408]{2,1,0:T(1,128)}), f32[16,1,1408]{2,1,0:T(1,128)S(1)}, u32[]{:S(2)}, u32[]{:S(2)}) async-start(f32[16,1,1408]{2,1,0:T(1,128)} %reshape.697), calls=%async_computation.1 | async-start | bytes 180224 | tf_op jit(solution)/shard_map/all_to_all | solution.py:65
  45.1 13.8 %all-to-all-start.2 = ((f32[16,1,1024]{2,1,0:T(1,128)}), f32[16,1,1024]{2,1,0:T(1,128)S(1)}, u32[]{:S(2)}, u32[]{:S(2)}) async-start(f32[16,1,1024]{2,1,0:T(1,128)} %reshape.699), calls=%async_computation.2 | async-start | bytes 131072 | tf_op jit(solution)/shard_map/all_to_all | solution.py:139
  60.8 7.6 %copy-start.14 = (f32[2]{0:T(128)S(1)}, f32[2]{0:T(128)}, u32[]{:S(2)}) copy-start(f32[2]{0:T(128)} %constant.164.clone) | copy-start | bytes 28
  63.0 14.4 %all-to-all-start.3 = ((f32[16,1,2048]{2,1,0:T(1,128)}), f32[16,1,2048]{2,1,0:T(1,128)S(1)}, u32[]{:S(2)}, u32[]{:S(2)}) async-start(f32[16,1,2048]{2,1,0:T(1,128)} %reshape.701), calls=%async_computation.3 | async-start | bytes 262144 | tf_op jit(solution)/shard_map/all_to_all | solution.py:150
  79.4 5.4 %copy-start.2 = (f32[256,1,256]{2,0,1:T(8,128)S(1)}, f32[256,1,256]{2,0,1:T(8,128)}, u32[]{:S(2)}) copy-start(f32[256,1,256]{2,0,1:T(8,128)} %get-tuple-element.26) | copy-start | bytes 786436
  79.4 5.4 %copy-start.3 = (f32[256,1,256]{2,0,1:T(8,128)S(1)}, f32[256,1,256]{2,0,1:T(8,128)}, u32[]{:S(2)}) copy-start(f32[256,1,256]{2,0,1:T(8,128)} %get-tuple-element.27) | copy-start | bytes 786436
  81.3 11.7 %all-to-all-start.4 = ((f32[16,1,2048]{2,1,0:T(1,128)}), f32[16,1,2048]{2,1,0:T(1,128)S(1)}, u32[]{:S(2)}, u32[]{:S(2)}) async-start(f32[16,1,2048]{2,1,0:T(1,128)} %reshape.703), calls=%async_computation.4 | async-start | bytes 262144 | tf_op jit(solution)/shard_map/all_to_all | solution.py:157
  94.3 1.9 copy-start
  94.9 1.3 copy-start.4
  94.9 1.4 copy-start.15
  96.2 1.1 copy-start.1
  97.3 6.7 %copy-start.12 = (s32[16]{0:T(128)S(1)}, s32[16]{0:T(128)}, u32[]{:S(2)}) copy-start(s32[16]{0:T(128)} %copy-done.11) | copy-start | bytes 196
  97.4 6.7 %copy-start.17 = (s32[128]{0:T(128)S(1)}, s32[128]{0:T(128)}, u32[]{:S(2)}) copy-start(s32[128]{0:T(128)} %iota_multiply_fusion) | copy-start | bytes 1540
  100.3 11.7 %all-to-all-start.5 = ((f32[16,1,2048]{2,1,0:T(1,128)}), f32[16,1,2048]{2,1,0:T(1,128)S(1)}, u32[]{:S(2)}, u32[]{:S(2)}) async-start(f32[16,1,2048]{2,1,0:T(1,128)} %reshape.705), calls=%async_computation.5 | async-start | bytes 262144 | tf_op jit(solution)/shard_map/all_to_all | solution.py:183
  114.1 1.1 copy-start.5
  114.1 2.9 %copy-start.16 = (s32[8]{0:T(128)S(1)}, s32[8]{0:T(128)}, u32[]{:S(2)}) copy-start(s32[8]{0:T(128)} %get-tuple-element.30) | copy-start | bytes 100
  118.2 14.4 %copy-start.8 = (f32[2,128,2,128]{3,1,2,0:T(8,128)S(1)}, f32[2,128,2,128]{3,1,2,0:T(8,128)}, u32[]{:S(2)}) copy-start(f32[2,128,2,128]{3,1,2,0:T(8,128)} %get-tuple-element.7) | copy-start | bytes 786436
  132.3 6.8 %copy-start.10 = (s32[704]{0:T(1024)S(1)}, s32[704]{0:T(1024)}, u32[]{:S(2)}) copy-start(s32[704]{0:T(1024)} %copy-done.9) | copy-start | bytes 8452
  135.5 11.1 %all-to-all-start.7 = ((f32[16,1,1024]{2,1,0:T(1,128)}), f32[16,1,1024]{2,1,0:T(1,128)S(1)}, u32[]{:S(2)}, u32[]{:S(2)}) async-start(f32[16,1,1024]{2,1,0:T(1,128)} %reshape.709), calls=%async_computation.7 | async-start | bytes 131072 | tf_op jit(solution)/shard_map/all_to_all | solution.py:195
  147.7 21.1 %copy-start.6 = (f32[704,256]{1,0:T(8,128)S(1)}, f32[704,256]{1,0:T(8,128)}, u32[]{:S(2)}) copy-start(f32[704,256]{1,0:T(8,128)} %param.12) | copy-start | bytes 2162692
  147.7 21.1 %copy-start.7 = (f32[704,256]{1,0:T(8,128)S(1)}, f32[704,256]{1,0:T(8,128)}, u32[]{:S(2)}) copy-start(f32[704,256]{1,0:T(8,128)} %pos_ref.1) | copy-start | bytes 2162692
  164.1 12.8 %all-to-all-start.9 = ((f32[16,1,1408]{2,1,0:T(1,128)}), f32[16,1,1408]{2,1,0:T(1,128)S(1)}, u32[]{:S(2)}, u32[]{:S(2)}) async-start(f32[16,1,1408]{2,1,0:T(1,128)} %reshape.713), calls=%async_computation.9 | async-start | bytes 180224 | tf_op jit(solution)/shard_map/all_to_all | solution.py:65
where the time goes:
time: 193 us; the launch traced here: 192 us
  waiting for transfers between devices  55.3 us (29%)
  starting transfers between devices  41.6 us (22%)
  blocking collectives  24.7 us (13%)
  other arithmetic  24.2 us (13%)
  local copies, waits for them, and re-layouts  23.5 us (12%)
  Pallas kernels  13.1 us (7%)
  matrix products  8.21 us (4%)
    unnamed x58, local copies, waits for them, and re-layouts  13.6 us
    pallas_call x1, Pallas kernels, kick_call(): pl.pallas_call(kick_kernel, grid=(bunches // KICK_ROWS,), in_specs=[wide,...  13.1 us
    all_to_all x1, blocking collectives, on_device(): part = lax.all_to_all(spin, 'dom', split_axis=2, concat_axis=1, tiled=True)  12.8 us
    all_to_all x1, blocking collectives, dom_sum(): lax.all_to_all(rows.reshape(domains, chunk, BINS), 'dom', 0, 0, tiled=True)  12 us
    all_to_all x2, waiting for transfers between devices, dom_sum(): return lax.all_to_all(spread, 'dom', 0, 0, tiled=True).reshape(rows.shape)  10.9 us
    all_to_all x1, starting transfers between devices, dom_sum(): lax.all_to_all(rows.reshape(domains, chunk, BINS), 'dom', 0, 0, tiled=True)  9.94 us
    all_to_all x2, starting transfers between devices, dom_sum(): return lax.all_to_all(spread, 'dom', 0, 0, tiled=True).reshape(rows.shape)  9.35 us
    dot_general x8, matrix products, contract(): return jnp.einsum(pattern, operand, matrix, precision=highest)  8.21 us
  transfers between devices with their start and end apart: 8, of which 8 were waited for; matrix products, arithmetic and copies ran while one was open for 5% of the time, Pallas kernels for 0%

commit v1 on v0

--- a/solution.py
+++ b/solution.py
@@ -55,6 +55,21 @@
 
 def turn(pair, cos_t, sin_t):
     return jnp.stack([pair[0] * cos_t - pair[1] * sin_t, pair[0] * sin_t + pair[1] * cos_t])
+
+
+def exchange(x, axis_name, split_axis, concat_axis):
+    count = lax.axis_size(axis_name)
+    front = jnp.moveaxis(x, split_axis, 0)
+    rest = front.shape[1:]
+    piece = (front.shape[0] // count,) + rest
+    sent = front.reshape(count, -1, 128)
+    got = lax.all_to_all(sent, axis_name, 0, 0, tiled=True).reshape((count,) + piece)
+    got = jnp.moveaxis(got, 1, split_axis + 1)
+    got = jnp.moveaxis(got, 0, concat_axis)
+    shape = list(x.shape)
+    shape[split_axis] //= count
+    shape[concat_axis] *= count
+    return got.reshape(shape)
 
 
 def dom_sum(rows, domains):
@@ -136,7 +151,7 @@
     first_table = block_table(first_len)
     second_table = block_table(second_len)
     third_table = block_table(N3)
-    received = lax.all_to_all(density, "grp", split_axis=2, concat_axis=0, tiled=True)
+    received = exchange(density, "grp", 2, 0)
     rows = contract("nab,nok->oabk", received, first_table[0])
     second_global = domain_index * R2 + jnp.arange(R2, dtype=jnp.int32)
     depth_global = group_index * depth_len + jnp.arange(depth_len, dtype=jnp.int32)
@@ -147,14 +162,14 @@
         cycle_len,
     )
     twist = turn(rows, cos_turn, -sin_turn)
-    part = lax.all_to_all(twist, "dom", split_axis=3, concat_axis=1, tiled=True)
+    part = exchange(twist, "dom", 3, 1)
     cols = contract("inbk,inom->obkm", part, second_table)
     second_freq = jnp.arange(second_len, dtype=jnp.int32)
     cos_turn, sin_turn = rotation(
         depth_global[:, None, None] * second_freq[None, None, :], plane_len
     )
     turned = turn(cols, cos_turn, -sin_turn)
-    part = lax.all_to_all(turned, "grp", split_axis=3, concat_axis=1, tiled=True)
+    part = exchange(turned, "grp", 3, 1)
     full = contract("inac,inok->oack", part, third_table)
     norm_factor = 1.0 / math.sqrt(BUNCH_GRP * groups)
     spectrum = full * norm_factor
@@ -180,7 +195,7 @@
     depth_all = jnp.arange(N3, dtype=jnp.int32)
     cos_turn, sin_turn = rotation(second_own[None, :, None] * depth_all[None, None, :], plane_len)
     lift = turn(back, cos_turn, sin_turn)
-    part = lax.all_to_all(lift, "grp", split_axis=3, concat_axis=2, tiled=True)
+    part = exchange(lift, "grp", 3, 2)
     spun = contract("iakb,ikon->oanb", part, conjugate(second_table))
     first_own = domain_index * first_part + jnp.arange(first_part, dtype=jnp.int32)
     cos_turn, sin_turn = rotation(
@@ -189,10 +204,10 @@
     )
     spin = turn(spun, cos_turn, sin_turn)
     inverse_factor = 1.0 / math.sqrt(cycle_len)
-    part = lax.all_to_all(spin, "dom", split_axis=2, concat_axis=1, tiled=True)
+    part = exchange(spin, "dom", 2, 1)
     summed = contract("ikab,ikn->nab", part, conjugate(first_table)[:, :, 0, :])
     volt_part = summed * inverse_factor
-    volt_slab = lax.all_to_all(volt_part, "grp", split_axis=0, concat_axis=2, tiled=True).reshape(
+    volt_slab = exchange(volt_part, "grp", 0, 2).reshape(
         R1 * own_rows, BINS
     )
     owned_volts = contract("sb,sj->bj", picker, volt_slab)

time: 193 us -> 185 us (0.959)
  other arithmetic: 24.2 us -> 20.4 us
  local copies, waits for them, and re-layouts: 23.5 us -> 21.2 us
    unnamed x58 -> x42, local copies, waits for them, and re-layouts: 13.6 us -> 4.35 us
    reshape x1 -> x14, local copies, waits for them, and re-layouts: 0.13 us -> 8.26 us  [the longest x7 6.16 us: exchange(): sent = front.reshape(count, -1, 128)]
    all_to_all x6 -> x0, other arithmetic: 5.24 us -> none  [the longest x1 0.92 us: on_device(): lax.all_to_all(turned, 'grp', split_axis=3, concat_axis=1, tiled=True)]
    transpose x0 -> x5, local copies, waits for them, and re-layouts: none -> 3.78 us  [the longest x4 3.21 us: exchange(): front = jnp.moveaxis(x, split_axis, 0)]
    all_to_all x9 -> x3, local copies, waits for them, and re-layouts: 3.99 us -> 0.87 us  [exchange(): lax.all_to_all(sent, axis_name, 0, 0, tiled=True).reshape((count,) + piece)]
  transfers between devices with their start and end apart: 8 -> 8, of which waited for: 8 -> 8; matrix products, arithmetic and copies ran while one was open for 5% -> 6% of each run, Pallas kernels for 0% -> 0%
where the time goes in v1:
time: 185 us
  waiting for transfers between devices  54.1 us (29%)
  starting transfers between devices  41.6 us (22%)
  blocking collectives  24.6 us (13%)
  local copies, waits for them, and re-layouts  21.2 us (11%)
  other arithmetic  20.4 us (11%)
  Pallas kernels  13.1 us (7%)
  matrix products  8.21 us (4%)
    all_to_all x5, waiting for transfers between devices, exchange(): lax.all_to_all(sent, axis_name, 0, 0, tiled=True).reshape((count,) + piece)  37.2 us
    all_to_all x5, starting transfers between devices, exchange(): lax.all_to_all(sent, axis_name, 0, 0, tiled=True).reshape((count,) + piece)  22.3 us
    pallas_call x1, Pallas kernels, kick_call(): pl.pallas_call(kick_kernel, grid=(bunches // KICK_ROWS,), in_specs=[wide,...  13.1 us
    all_to_all x1, blocking collectives, exchange(): lax.all_to_all(sent, axis_name, 0, 0, tiled=True).reshape((count,) + piece)  12.6 us
    all_to_all x1, blocking collectives, dom_sum(): lax.all_to_all(rows.reshape(domains, chunk, BINS), 'dom', 0, 0, tiled=True)  12 us
    all_to_all x2, waiting for transfers between devices, dom_sum(): return lax.all_to_all(spread, 'dom', 0, 0, tiled=True).reshape(rows.shape)  10.8 us
    all_to_all x1, starting transfers between devices, dom_sum(): lax.all_to_all(rows.reshape(domains, chunk, BINS), 'dom', 0, 0, tiled=True)  9.94 us
    all_to_all x2, starting transfers between devices, dom_sum(): return lax.all_to_all(spread, 'dom', 0, 0, tiled=True).reshape(rows.shape)  9.35 us
  transfers between devices with their start and end apart: 8, of which 8 were waited for; matrix products, arithmetic and copies ran while one was open for 6% of the time, Pallas kernels for 0%

profile of v1, /device:TPU:2, one launch (start us, length us, event | category | flops | bytes accessed | tf_op | source)
XLA Modules:
  0.0 184.6 jit_solution(5848371353099650647)
XLA Ops:
  0.7 5.7 %fusion.1 = f32[704,32]{1,0:T(8,128)S(1)} fusion(f32[32]{0:T(128)S(1)} %iota_add_fusion.3, f32[704,256]{1,0:T(8,128)} %pos_ref.1), kind=kLoop, calls=%fused_computation.2 | loop fusion | flops 23046144 | bytes 811136 | tf_op jit(solution)/shard_map/reduce_sum | solution.py:141
  6.8 0.9 reshape.758
  7.7 9.9 %all-to-all-start = ((f32[16,1,1408]{2,1,0:T(1,128)}), f32[16,1,1408]{2,1,0:T(1,128)S(1)}, u32[]{:S(2)}, u32[]{:S(2)}) async-start(f32[16,1,1408]{2,1,0:T(1,128)} %reshape.758), calls=%async_computation | async-start | bytes 180224 | tf_op jit(solution)/shard_map/all_to_all | solution.py:77
  17.8 0.6 iota_add_fusion.2
  18.7 1.0 fusion.35
  19.7 6.0 %all-to-all-done = f32[16,1,1408]{2,1,0:T(1,128)S(1)} async-done(((f32[16,1,1408]{2,1,0:T(1,128)}), f32[16,1,1408]{2,1,0:T(1,128)S(1)}, u32[]{:S(2)}, u32[]{:S(2)}) %all-to-all-start) | async-done | bytes 90144 | tf_op jit(solution)/shard_map/all_to_all | solution.py:77
  25.7 0.6 broadcast.739
  26.3 0.9 reduce
  27.5 0.9 reshape.760
  28.5 4.6 %all-to-all-start.1 = ((f32[16,1,1408]{2,1,0:T(1,128)}), f32[16,1,1408]{2,1,0:T(1,128)S(1)}, u32[]{:S(2)}, u32[]{:S(2)}) async-start(f32[16,1,1408]{2,1,0:T(1,128)} %reshape.760), calls=%async_computation.1 | async-start | bytes 180224 | tf_op jit(solution)/shard_map/all_to_all | solution.py:80
  33.4 1.8 fusion.33
  35.2 6.0 %all-to-all-done.1 = f32[16,1,1408]{2,1,0:T(1,128)S(1)} async-done(((f32[16,1,1408]{2,1,0:T(1,128)}), f32[16,1,1408]{2,1,0:T(1,128)S(1)}, u32[]{:S(2)}, u32[]{:S(2)}) %all-to-all-start.1) | async-done | bytes 90144 | tf_op jit(solution)/shard_map/all_to_all | solution.py:80
  41.2 0.9 reduce.1
  42.7 0.8 fusion.5
  44.1 1.1 reshape.721
  45.2 6.1 %all-to-all-start.2 = ((f32[16,8,128]{2,1,0:T(8,128)}), f32[16,8,128]{2,1,0:T(8,128)S(1)}, u32[]{:S(2)}, u32[]{:S(2)}) async-start(f32[16,8,128]{2,1,0:T(8,128)} %reshape.721), calls=%async_computation.2 | async-start | bytes 131072 | tf_op jit(solution)/shard_map/all_to_all | solution.py:66
  51.6 7.4 %all-to-all-done.2 = f32[16,8,128]{2,1,0:T(8,128)S(1)} async-done(((f32[16,8,128]{2,1,0:T(8,128)}), f32[16,8,128]{2,1,0:T(8,128)S(1)}, u32[]{:S(2)}, u32[]{:S(2)}) %all-to-all-start.2) | async-done | bytes 65568 | tf_op jit(solution)/shard_map/all_to_all | solution.py:66
  61.1 1.0 reshape.724
  62.1 5.4 %all-to-all-start.3 = ((f32[16,16,128]{2,1,0:T(8,128)}), f32[16,16,128]{2,1,0:T(8,128)S(1)}, u32[]{:S(2)}, u32[]{:S(2)}) async-start(f32[16,16,128]{2,1,0:T(8,128)} %reshape.724), calls=%async_computation.3 | async-start | bytes 262144 | tf_op jit(solution)/shard_map/all_to_all | solution.py:66
  67.5 0.9 multiply_multiply_fusion.1
  68.4 8.1 %all-to-all-done.3 = f32[16,16,128]{2,1,0:T(8,128)S(1)} async-done(((f32[16,16,128]{2,1,0:T(8,128)}), f32[16,16,128]{2,1,0:T(8,128)S(1)}, u32[]{:S(2)}, u32[]{:S(2)}) %all-to-all-start.3) | async-done | bytes 131104 | tf_op jit(solution)/shard_map/all_to_all | solution.py:66
  77.8 1.8 copy.143
  79.7 1.6 reshape.727
  81.3 3.5 %all-to-all-start.4 = ((f32[16,16,128]{2,1,0:T(8,128)}), f32[16,16,128]{2,1,0:T(8,128)S(1)}, u32[]{:S(2)}, u32[]{:S(2)}) async-start(f32[16,16,128]{2,1,0:T(8,128)} %reshape.727), calls=%async_computation.4 | async-start | bytes 262144 | tf_op jit(solution)/shard_map/all_to_all | solution.py:66
  84.8 1.2 maximum_bitcast_fusion
  86.0 0.6 iota_multiply_fusion
  86.6 6.4 %all-to-all-done.4 = f32[16,16,128]{2,1,0:T(8,128)S(1)} async-done(((f32[16,16,128]{2,1,0:T(8,128)}), f32[16,16,128]{2,1,0:T(8,128)S(1)}, u32[]{:S(2)}, u32[]{:S(2)}) %all-to-all-start.4) | async-done | bytes 131104 | tf_op jit(solution)/shard_map/all_to_all | solution.py:66
  94.2 0.8 fusion.7
  95.2 0.9 convolution_bitcast_fusion.2
  96.5 1.1 copy.147
  97.6 3.7 %all-to-all-start.5 = ((f32[16,16,128]{2,1,0:T(8,128)}), f32[16,16,128]{2,1,0:T(8,128)S(1)}, u32[]{:S(2)}, u32[]{:S(2)}) async-start(f32[16,16,128]{2,1,0:T(8,128)} %copy.147), calls=%async_computation.5 | async-start | bytes 262144 | tf_op jit(solution)/shard_map/all_to_all | solution.py:66
  101.4 7.9 %all-to-all-done.5 = f32[16,16,128]{2,1,0:T(8,128)S(1)} async-done(((f32[16,16,128]{2,1,0:T(8,128)}), f32[16,16,128]{2,1,0:T(8,128)S(1)}, u32[]{:S(2)}, u32[]{:S(2)}) %all-to-all-start.5) | async-done | bytes 131104 | tf_op jit(solution)/shard_map/all_to_all | solution.py:66
  109.6 1.8 convolution_bitcast_fusion.1
  112.6 12.6 %all_to_all.50 = f32[16,16,128]{2,1,0:T(8,128)S(1)} all-to-all(f32[16,16,128]{2,1,0:T(8,128)S(1)} %reshape.733), channel_id=1, replica_groups=mesh['grp'=16,'dom'=16] {'dom'}, dimensions={0} | all-to-all | bytes 262144 | tf_op jit(solution)/shard_map/all_to_all | solution.py:66
  125.9 1.8 fusion.8
  127.9 0.8 reshape.736
  128.8 3.5 %all-to-all-start.7 = ((f32[16,8,128]{2,1,0:T(8,128)}), f32[16,8,128]{2,1,0:T(8,128)S(1)}, u32[]{:S(2)}, u32[]{:S(2)}) async-start(f32[16,8,128]{2,1,0:T(8,128)} %reshape.736), calls=%async_computation.7 | async-start | bytes 131072 | tf_op jit(solution)/shard_map/all_to_all | solution.py:66
  132.4 7.5 %all-to-all-done.7 = f32[16,8,128]{2,1,0:T(8,128)S(1)} async-done(((f32[16,8,128]{2,1,0:T(8,128)}), f32[16,8,128]{2,1,0:T(8,128)S(1)}, u32[]{:S(2)}, u32[]{:S(2)}) %all-to-all-start.7) | async-done | bytes 65568 | tf_op jit(solution)/shard_map/all_to_all | solution.py:66
  140.6 1.5 fusion.88
  142.4 12.0 %all_to_all.51 = f32[16,1,1408]{2,1,0:T(1,128)S(1)} all-to-all(f32[16,1,1408]{2,1,0:T(1,128)S(1)} %reshape.762), channel_id=1, replica_groups=mesh['grp'=16,'dom'=16] {'dom'}, dimensions={0} | all-to-all | bytes 180224 | tf_op jit(solution)/shard_map/all_to_all | solution.py:77
  154.3 0.9 reduce.2
  155.6 0.9 reshape.764
  156.5 4.7 %all-to-all-start.9 = ((f32[16,1,1408]{2,1,0:T(1,128)}), f32[16,1,1408]{2,1,0:T(1,128)S(1)}, u32[]{:S(2)}, u32[]{:S(2)}) async-start(f32[16,1,1408]{2,1,0:T(1,128)} %reshape.764), calls=%async_computation.9 | async-start | bytes 180224 | tf_op jit(solution)/shard_map/all_to_all | solution.py:80
  161.3 3.2 %multiply_subtract_fusion.drift_ref = f32[704,256]{1,0:T(8,128)} fusion(f32[704,256]{1,0:T(8,128)S(1)} %copy-done.4, f32[704,256]{1,0:T(8,128)S(1)} %copy-done.5), kind=kLoop, calls=%fused_computation.27 | loop fusion | flops 720896 | bytes 2162688 | tf_op jit(solution)/shard_map/sub | solution.py:215
  164.4 4.9 %all-to-all-done.9 = f32[16,1,1408]{2,1,0:T(1,128)S(1)} async-done(((f32[16,1,1408]{2,1,0:T(1,128)}), f32[16,1,1408]{2,1,0:T(1,128)S(1)}, u32[]{:S(2)}, u32[]{:S(2)}) %all-to-all-start.9) | async-done | bytes 90144 | tf_op jit(solution)/shard_map/all_to_all | solution.py:80
  169.3 0.9 reduce.3
  170.7 0.8 reshape.757.volt_ref
  171.5 13.1 %shard_map.130 = (f32[704,256]{1,0:T(8,128)}, f32[704,256]{1,0:T(8,128)}) custom-call(f32[704,256]{1,0:T(8,128)} %pos_ref.1, f32[704,256]{1,0:T(8,128)} %multiply_subtract_fusion.drift_ref, f32[704,32]{1,0:T(8,128)} %reshape.757.volt_ref), custom_call_target="tpu_custom_call" | custom-call | flops 69206016 | bytes 2973696 | tf_op jit(solution)/shard_map/pallas_call | solution.py:112
  (94 shorter events, 12.3 us)
Async XLA Ops:
  0.6 17.0 %copy-start.11 = (s32[704]{0:T(1024)S(1)}, s32[704]{0:T(1024)}, u32[]{:S(2)}) copy-start(s32[704]{0:T(1024)} %param.13) | copy-start | bytes 8452
  7.7 18.0 %all-to-all-start = ((f32[16,1,1408]{2,1,0:T(1,128)}), f32[16,1,1408]{2,1,0:T(1,128)S(1)}, u32[]{:S(2)}, u32[]{:S(2)}) async-start(f32[16,1,1408]{2,1,0:T(1,128)} %reshape.758), calls=%async_computation | async-start | bytes 180224 | tf_op jit(solution)/shard_map/all_to_all | solution.py:77
  17.7 25.8 %copy-start.7 = (s32[704]{0:T(1024)}, s32[704]{0:T(1024)S(1)}, u32[]{:S(2)}) copy-start(s32[704]{0:T(1024)S(1)} %fusion.77) | copy-start | bytes 8452
  17.7 25.8 %copy-start.9 = (s32[16]{0:T(128)}, s32[16]{0:T(128)S(1)}, u32[]{:S(2)}) copy-start(s32[16]{0:T(128)S(1)} %iota_add_fusion.1) | copy-start | bytes 196
  28.5 12.7 %all-to-all-start.1 = ((f32[16,1,1408]{2,1,0:T(1,128)}), f32[16,1,1408]{2,1,0:T(1,128)S(1)}, u32[]{:S(2)}, u32[]{:S(2)}) async-start(f32[16,1,1408]{2,1,0:T(1,128)} %reshape.760), calls=%async_computation.1 | async-start | bytes 180224 | tf_op jit(solution)/shard_map/all_to_all | solution.py:80
  45.2 13.8 %all-to-all-start.2 = ((f32[16,8,128]{2,1,0:T(8,128)}), f32[16,8,128]{2,1,0:T(8,128)S(1)}, u32[]{:S(2)}, u32[]{:S(2)}) async-start(f32[16,8,128]{2,1,0:T(8,128)} %reshape.721), calls=%async_computation.2 | async-start | bytes 131072 | tf_op jit(solution)/shard_map/all_to_all | solution.py:66
  60.0 7.5 %copy-start.12 = (f32[2]{0:T(128)S(1)}, f32[2]{0:T(128)}, u32[]{:S(2)}) copy-start(f32[2]{0:T(128)} %constant.164.clone) | copy-start | bytes 28
  62.1 14.4 %all-to-all-start.3 = ((f32[16,16,128]{2,1,0:T(8,128)}), f32[16,16,128]{2,1,0:T(8,128)S(1)}, u32[]{:S(2)}, u32[]{:S(2)}) async-start(f32[16,16,128]{2,1,0:T(8,128)} %reshape.724), calls=%async_computation.3 | async-start | bytes 262144 | tf_op jit(solution)/shard_map/all_to_all | solution.py:66
  81.3 11.7 %all-to-all-start.4 = ((f32[16,16,128]{2,1,0:T(8,128)}), f32[16,16,128]{2,1,0:T(8,128)S(1)}, u32[]{:S(2)}, u32[]{:S(2)}) async-start(f32[16,16,128]{2,1,0:T(8,128)} %reshape.727), calls=%async_computation.4 | async-start | bytes 262144 | tf_op jit(solution)/shard_map/all_to_all | solution.py:66
  93.3 1.7 copy-start
  93.7 1.3 copy-start.2
  93.8 1.4 copy-start.13
  95.0 1.5 copy-start.1
  95.2 6.2 %copy-start.10 = (s32[16]{0:T(128)S(1)}, s32[16]{0:T(128)}, u32[]{:S(2)}) copy-start(s32[16]{0:T(128)} %copy-done.9) | copy-start | bytes 196
  95.2 6.2 %copy-start.15 = (s32[128]{0:T(128)S(1)}, s32[128]{0:T(128)}, u32[]{:S(2)}) copy-start(s32[128]{0:T(128)} %iota_multiply_fusion) | copy-start | bytes 1540
  96.1 13.5 %copy-start.3 = (f32[2,128,2,128,1]{3,1,2,0,4:T(8,128)S(1)}, f32[2,128,2,128,1]{3,1,2,0,4:T(8,128)}, u32[]{:S(2)}) copy-start(f32[2,128,2,128,1]{3,1,2,0,4:T(8,128)} %get-tuple-element.8) | copy-start | bytes 786436
  96.5 14.9 %copy-start.14 = (s32[8]{0:T(128)S(1)}, s32[8]{0:T(128)}, u32[]{:S(2)}) copy-start(s32[8]{0:T(128)} %get-tuple-element.30) | copy-start | bytes 100
  97.6 11.7 %all-to-all-start.5 = ((f32[16,16,128]{2,1,0:T(8,128)}), f32[16,16,128]{2,1,0:T(8,128)S(1)}, u32[]{:S(2)}, u32[]{:S(2)}) async-start(f32[16,16,128]{2,1,0:T(8,128)} %copy.147), calls=%async_computation.5 | async-start | bytes 262144 | tf_op jit(solution)/shard_map/all_to_all | solution.py:66
  112.3 13.6 %copy-start.6 = (f32[2,128,2,128]{3,1,2,0:T(8,128)S(1)}, f32[2,128,2,128]{3,1,2,0:T(8,128)}, u32[]{:S(2)}) copy-start(f32[2,128,2,128]{3,1,2,0:T(8,128)} %get-tuple-element.7) | copy-start | bytes 786436
  125.5 6.7 %copy-start.8 = (s32[704]{0:T(1024)S(1)}, s32[704]{0:T(1024)}, u32[]{:S(2)}) copy-start(s32[704]{0:T(1024)} %copy-done.7) | copy-start | bytes 8452
  128.8 11.1 %all-to-all-start.7 = ((f32[16,8,128]{2,1,0:T(8,128)}), f32[16,8,128]{2,1,0:T(8,128)S(1)}, u32[]{:S(2)}, u32[]{:S(2)}) async-start(f32[16,8,128]{2,1,0:T(8,128)} %reshape.736), calls=%async_computation.7 | async-start | bytes 131072 | tf_op jit(solution)/shard_map/all_to_all | solution.py:66
  140.1 21.2 %copy-start.4 = (f32[704,256]{1,0:T(8,128)S(1)}, f32[704,256]{1,0:T(8,128)}, u32[]{:S(2)}) copy-start(f32[704,256]{1,0:T(8,128)} %param.12) | copy-start | bytes 2162692
  140.1 21.2 %copy-start.5 = (f32[704,256]{1,0:T(8,128)S(1)}, f32[704,256]{1,0:T(8,128)}, u32[]{:S(2)}) copy-start(f32[704,256]{1,0:T(8,128)} %pos_ref.1) | copy-start | bytes 2162692
  156.5 12.8 %all-to-all-start.9 = ((f32[16,1,1408]{2,1,0:T(1,128)}), f32[16,1,1408]{2,1,0:T(1,128)S(1)}, u32[]{:S(2)}, u32[]{:S(2)}) async-start(f32[16,1,1408]{2,1,0:T(1,128)} %reshape.764), calls=%async_computation.9 | async-start | bytes 180224 | tf_op jit(solution)/shard_map/all_to_all | solution.py:80

commit v2 on v1

--- a/solution.py
+++ b/solution.py
@@ -74,9 +74,9 @@
 
 def dom_sum(rows, domains):
     chunk = rows.shape[0] // domains
-    pieces = lax.all_to_all(rows.reshape(domains, chunk, BINS), "dom", 0, 0, tiled=True)
+    pieces = lax.all_to_all(rows.reshape(domains, -1, 128), "dom", 0, 0, tiled=True)
     mine = jnp.sum(pieces, axis=0)
-    spread = jnp.broadcast_to(mine[None], (domains, chunk, BINS))
+    spread = jnp.broadcast_to(mine[None], (domains,) + mine.shape)
     return lax.all_to_all(spread, "dom", 0, 0, tiled=True).reshape(rows.shape)
 
 

time: 185 us -> 179 us (0.968)
  blocking collectives: 24.6 us -> 35.7 us
  waiting for transfers between devices: 54.1 us -> 48.2 us
  local copies, waits for them, and re-layouts: 21.2 us -> 17.2 us
  starting transfers between devices: 41.6 us -> 37.9 us
  other arithmetic: 20.4 us -> 16.7 us
    all_to_all x1 -> x2, blocking collectives: 12.6 us -> 22.7 us  [exchange(): lax.all_to_all(sent, axis_name, 0, 0, tiled=True).reshape((count,) + piece)]
    all_to_all x5 -> x4, waiting for transfers between devices: 37.2 us -> 30 us  [exchange(): lax.all_to_all(sent, axis_name, 0, 0, tiled=True).reshape((count,) + piece)]
    unnamed x42 -> x32, local copies, waits for them, and re-layouts: 4.35 us -> 0.08 us
    all_to_all x5 -> x4, starting transfers between devices: 22.3 us -> 18.6 us  [exchange(): lax.all_to_all(sent, axis_name, 0, 0, tiled=True).reshape((count,) + piece)]
    all_to_all x4 -> x0, other arithmetic: 3.56 us -> none  [the longest x2 1.78 us: dom_sum(): return lax.all_to_all(spread, 'dom', 0, 0, tiled=True).reshape(rows.shape)]
  transfers between devices with their start and end apart: 8 -> 7, of which waited for: 8 -> 7; matrix products, arithmetic and copies ran while one was open for 6% -> 6% of each run, Pallas kernels for 0% -> 0%
where the time goes in v2:
time: 179 us; the launch traced here: 178 us
  waiting for transfers between devices  48.2 us (27%)
  starting transfers between devices  37.9 us (21%)
  blocking collectives  35.7 us (20%)
  local copies, waits for them, and re-layouts  17.2 us (10%)
  other arithmetic  16.7 us (9%)
  Pallas kernels  13.1 us (7%)
  matrix products  8.15 us (5%)
    all_to_all x4, waiting for transfers between devices, exchange(): lax.all_to_all(sent, axis_name, 0, 0, tiled=True).reshape((count,) + piece)  30 us
    all_to_all x2, blocking collectives, exchange(): lax.all_to_all(sent, axis_name, 0, 0, tiled=True).reshape((count,) + piece)  22.7 us
    all_to_all x4, starting transfers between devices, exchange(): lax.all_to_all(sent, axis_name, 0, 0, tiled=True).reshape((count,) + piece)  18.6 us
    pallas_call x1, Pallas kernels, kick_call(): pl.pallas_call(kick_kernel, grid=(bunches // KICK_ROWS,), in_specs=[wide,...  13.1 us
    all_to_all x1, blocking collectives, dom_sum(): lax.all_to_all(rows.reshape(domains, -1, 128), 'dom', 0, 0, tiled=True)  13 us
    all_to_all x2, waiting for transfers between devices, dom_sum(): return lax.all_to_all(spread, 'dom', 0, 0, tiled=True).reshape(rows.shape)  11.7 us
    all_to_all x1, starting transfers between devices, dom_sum(): lax.all_to_all(rows.reshape(domains, -1, 128), 'dom', 0, 0, tiled=True)  9.94 us
    all_to_all x2, starting transfers between devices, dom_sum(): return lax.all_to_all(spread, 'dom', 0, 0, tiled=True).reshape(rows.shape)  9.34 us
  transfers between devices with their start and end apart: 7, of which 7 were waited for; matrix products, arithmetic and copies ran while one was open for 6% of the time, Pallas kernels for 0%

profile of v2, /device:TPU:2, one launch (start us, length us, event | category | flops | bytes accessed | tf_op | source)
XLA Modules:
  0.0 178.2 jit_solution(1635964347221708047)
XLA Ops:
  0.7 5.7 %fusion.1 = f32[704,32]{1,0:T(8,128)S(1)} fusion(f32[32]{0:T(128)S(1)} %iota_add_fusion.3, f32[704,256]{1,0:T(8,128)} %pos_ref.1), kind=kLoop, calls=%fused_computation.2 | loop fusion | flops 23046144 | bytes 811136 | tf_op jit(solution)/shard_map/reduce_sum | solution.py:141
  6.4 0.8 div.48
  7.2 9.9 %all-to-all-start = ((f32[16,11,128]{2,1,0:T(8,128)}), f32[16,11,128]{2,1,0:T(8,128)S(1)}, u32[]{:S(2)}, u32[]{:S(2)}) async-start(f32[16,11,128]{2,1,0:T(8,128)} %div.48), calls=%async_computation | async-start | bytes 262144 | tf_op jit(solution)/shard_map/all_to_all | solution.py:77
  17.2 0.5 iota_add_fusion.2
  18.0 1.0 fusion.32
  19.0 6.6 %all-to-all-done = f32[16,11,128]{2,1,0:T(8,128)S(1)} async-done(((f32[16,11,128]{2,1,0:T(8,128)}), f32[16,11,128]{2,1,0:T(8,128)S(1)}, u32[]{:S(2)}, u32[]{:S(2)}) %all-to-all-start) | async-done | bytes 90144 | tf_op jit(solution)/shard_map/all_to_all | solution.py:77
  25.6 0.7 broadcast_in_dim.6
  26.3 4.6 %all-to-all-start.1 = ((f32[16,11,128]{2,1,0:T(8,128)}), f32[16,11,128]{2,1,0:T(8,128)S(1)}, u32[]{:S(2)}, u32[]{:S(2)}) async-start(f32[16,11,128]{2,1,0:T(8,128)} %broadcast_in_dim.6), calls=%async_computation.1 | async-start | bytes 262144 | tf_op jit(solution)/shard_map/all_to_all | solution.py:80
  31.1 1.8 fusion.30
  32.9 6.4 %all-to-all-done.1 = f32[16,11,128]{2,1,0:T(8,128)S(1)} async-done(((f32[16,11,128]{2,1,0:T(8,128)}), f32[16,11,128]{2,1,0:T(8,128)S(1)}, u32[]{:S(2)}, u32[]{:S(2)}) %all-to-all-start.1) | async-done | bytes 90144 | tf_op jit(solution)/shard_map/all_to_all | solution.py:80
  39.5 0.9 fusion.3
  40.5 0.4 copy.93
  40.9 1.1 reshape.706
  42.0 6.1 %all-to-all-start.2 = ((f32[16,8,128]{2,1,0:T(8,128)}), f32[16,8,128]{2,1,0:T(8,128)S(1)}, u32[]{:S(2)}, u32[]{:S(2)}) async-start(f32[16,8,128]{2,1,0:T(8,128)} %reshape.706), calls=%async_computation.2 | async-start | bytes 131072 | tf_op jit(solution)/shard_map/all_to_all | solution.py:66
  48.4 7.4 %all-to-all-done.2 = f32[16,8,128]{2,1,0:T(8,128)S(1)} async-done(((f32[16,8,128]{2,1,0:T(8,128)}), f32[16,8,128]{2,1,0:T(8,128)S(1)}, u32[]{:S(2)}, u32[]{:S(2)}) %all-to-all-start.2) | async-done | bytes 65568 | tf_op jit(solution)/shard_map/all_to_all | solution.py:66
  56.0 0.6 copy.95
  57.4 0.5 copy.97
  57.9 1.0 reshape.709
  58.9 5.5 %all-to-all-start.3 = ((f32[16,16,128]{2,1,0:T(8,128)}), f32[16,16,128]{2,1,0:T(8,128)S(1)}, u32[]{:S(2)}, u32[]{:S(2)}) async-start(f32[16,16,128]{2,1,0:T(8,128)} %reshape.709), calls=%async_computation.3 | async-start | bytes 262144 | tf_op jit(solution)/shard_map/all_to_all | solution.py:66
  64.4 0.9 multiply_multiply_fusion.1
  65.3 8.1 %all-to-all-done.3 = f32[16,16,128]{2,1,0:T(8,128)S(1)} async-done(((f32[16,16,128]{2,1,0:T(8,128)}), f32[16,16,128]{2,1,0:T(8,128)S(1)}, u32[]{:S(2)}, u32[]{:S(2)}) %all-to-all-start.3) | async-done | bytes 131104 | tf_op jit(solution)/shard_map/all_to_all | solution.py:66
  74.7 1.8 %copy.101 = f32[128,2,16,8]{3,2,1,0:T(8,128)S(1)} copy(f32[128,2,16,8]{0,2,3,1:T(8,128)S(1)} %maximum_bitcast_fusion.4) | data formatting | bytes 262144 | tf_op jit(solution)/shard_map/transpose | solution.py:62
  76.6 1.6 reshape.712
  78.2 3.5 %all-to-all-start.4 = ((f32[16,16,128]{2,1,0:T(8,128)}), f32[16,16,128]{2,1,0:T(8,128)S(1)}, u32[]{:S(2)}, u32[]{:S(2)}) async-start(f32[16,16,128]{2,1,0:T(8,128)} %reshape.712), calls=%async_computation.4 | async-start | bytes 262144 | tf_op jit(solution)/shard_map/all_to_all | solution.py:66
  81.7 1.2 maximum_bitcast_fusion
  82.9 0.5 iota_multiply_fusion
  83.4 6.5 %all-to-all-done.4 = f32[16,16,128]{2,1,0:T(8,128)S(1)} async-done(((f32[16,16,128]{2,1,0:T(8,128)}), f32[16,16,128]{2,1,0:T(8,128)S(1)}, u32[]{:S(2)}, u32[]{:S(2)}) %all-to-all-start.4) | async-done | bytes 131104 | tf_op jit(solution)/shard_map/all_to_all | solution.py:66
  90.3 0.4 copy.103
  90.7 0.4 reshape.731
  91.1 0.8 fusion.5
  92.1 0.9 convolution_bitcast_fusion.2
  93.4 1.1 copy.105
  94.5 3.5 %all-to-all-start.5 = ((f32[16,16,128]{2,1,0:T(8,128)}), f32[16,16,128]{2,1,0:T(8,128)S(1)}, u32[]{:S(2)}, u32[]{:S(2)}) async-start(f32[16,16,128]{2,1,0:T(8,128)} %copy.105), calls=%async_computation.5 | async-start | bytes 262144 | tf_op jit(solution)/shard_map/all_to_all | solution.py:66
  98.1 8.1 %all-to-all-done.5 = f32[16,16,128]{2,1,0:T(8,128)S(1)} async-done(((f32[16,16,128]{2,1,0:T(8,128)}), f32[16,16,128]{2,1,0:T(8,128)S(1)}, u32[]{:S(2)}, u32[]{:S(2)}) %all-to-all-start.5) | async-done | bytes 131104 | tf_op jit(solution)/shard_map/all_to_all | solution.py:66
  106.5 1.8 convolution_bitcast_fusion.1
  108.3 0.4 multiply_subtract_fusion.1
  108.7 0.5 copy.110
  109.5 12.4 %all_to_all.50 = f32[16,16,128]{2,1,0:T(8,128)S(1)} all-to-all(f32[16,16,128]{2,1,0:T(8,128)S(1)} %reshape.718), channel_id=1, replica_groups=mesh['grp'=16,'dom'=16] {'dom'}, dimensions={0} | all-to-all | bytes 262144 | tf_op jit(solution)/shard_map/all_to_all | solution.py:66
  122.6 1.8 fusion.6
  124.8 10.2 %all_to_all.51 = f32[16,8,128]{2,1,0:T(8,128)S(1)} all-to-all(f32[16,8,128]{2,1,0:T(8,128)S(1)} %reshape.721), channel_id=1, replica_groups=mesh['grp'=16,'dom'=16] {'grp'}, dimensions={0} | all-to-all | bytes 131072 | tf_op jit(solution)/shard_map/all_to_all | solution.py:66
  135.7 1.4 fusion.2
  137.3 13.0 %all_to_all.52 = f32[16,11,128]{2,1,0:T(8,128)S(1)} all-to-all(f32[16,11,128]{2,1,0:T(8,128)S(1)} %reshape.723), channel_id=1, replica_groups=mesh['grp'=16,'dom'=16] {'dom'}, dimensions={0} | all-to-all | bytes 180224 | tf_op jit(solution)/shard_map/all_to_all | solution.py:77
  150.3 0.7 broadcast_in_dim.7
  151.0 4.8 %all-to-all-start.9 = ((f32[16,11,128]{2,1,0:T(8,128)}), f32[16,11,128]{2,1,0:T(8,128)S(1)}, u32[]{:S(2)}, u32[]{:S(2)}) async-start(f32[16,11,128]{2,1,0:T(8,128)} %broadcast_in_dim.7), calls=%async_computation.9 | async-start | bytes 262144 | tf_op jit(solution)/shard_map/all_to_all | solution.py:80
  155.8 3.2 %multiply_subtract_fusion.drift_ref = f32[704,256]{1,0:T(8,128)} fusion(f32[704,256]{1,0:T(8,128)S(1)} %copy-done.4, f32[704,256]{1,0:T(8,128)S(1)} %copy-done.5), kind=kLoop, calls=%fused_computation.25 | loop fusion | flops 720896 | bytes 2162688 | tf_op jit(solution)/shard_map/sub | solution.py:215
  159.0 5.3 %all-to-all-done.9 = f32[16,11,128]{2,1,0:T(8,128)S(1)} async-done(((f32[16,11,128]{2,1,0:T(8,128)}), f32[16,11,128]{2,1,0:T(8,128)S(1)}, u32[]{:S(2)}, u32[]{:S(2)}) %all-to-all-start.9) | async-done | bytes 90144 | tf_op jit(solution)/shard_map/all_to_all | solution.py:80
  164.2 0.9 reshape.724.volt_ref
  165.1 13.1 %shard_map.130 = (f32[704,256]{1,0:T(8,128)}, f32[704,256]{1,0:T(8,128)}) custom-call(f32[704,256]{1,0:T(8,128)} %pos_ref.1, f32[704,256]{1,0:T(8,128)} %multiply_subtract_fusion.drift_ref, f32[704,32]{1,0:T(8,128)} %reshape.724.volt_ref), custom_call_target="tpu_custom_call" | custom-call | flops 69206016 | bytes 2973696 | tf_op jit(solution)/shard_map/pallas_call | solution.py:112
  (76 shorter events, 7.1 us)
Async XLA Ops:
  0.6 17.0 %copy-start.9 = (s32[704]{0:T(1024)S(1)}, s32[704]{0:T(1024)}, u32[]{:S(2)}) copy-start(s32[704]{0:T(1024)} %param.13) | copy-start | bytes 8452
  7.2 18.4 %all-to-all-start = ((f32[16,11,128]{2,1,0:T(8,128)}), f32[16,11,128]{2,1,0:T(8,128)S(1)}, u32[]{:S(2)}, u32[]{:S(2)}) async-start(f32[16,11,128]{2,1,0:T(8,128)} %div.48), calls=%async_computation | async-start | bytes 262144 | tf_op jit(solution)/shard_map/all_to_all | solution.py:77
  17.2 24.8 %copy-start.7 = (s32[16]{0:T(128)}, s32[16]{0:T(128)S(1)}, u32[]{:S(2)}) copy-start(s32[16]{0:T(128)S(1)} %iota_add_fusion.1) | copy-start | bytes 196
  17.7 24.3 %copy-start.10 = (s32[704]{0:T(1024)}, s32[704]{0:T(1024)S(1)}, u32[]{:S(2)}) copy-start(s32[704]{0:T(1024)S(1)} %fusion.74) | copy-start | bytes 8452
  26.3 13.0 %all-to-all-start.1 = ((f32[16,11,128]{2,1,0:T(8,128)}), f32[16,11,128]{2,1,0:T(8,128)S(1)}, u32[]{:S(2)}, u32[]{:S(2)}) async-start(f32[16,11,128]{2,1,0:T(8,128)} %broadcast_in_dim.6), calls=%async_computation.1 | async-start | bytes 262144 | tf_op jit(solution)/shard_map/all_to_all | solution.py:80
  42.0 13.8 %all-to-all-start.2 = ((f32[16,8,128]{2,1,0:T(8,128)}), f32[16,8,128]{2,1,0:T(8,128)S(1)}, u32[]{:S(2)}, u32[]{:S(2)}) async-start(f32[16,8,128]{2,1,0:T(8,128)} %reshape.706), calls=%async_computation.2 | async-start | bytes 131072 | tf_op jit(solution)/shard_map/all_to_all | solution.py:66
  56.8 7.6 %copy-start.12 = (f32[2]{0:T(128)S(1)}, f32[2]{0:T(128)}, u32[]{:S(2)}) copy-start(f32[2]{0:T(128)} %constant.164.clone) | copy-start | bytes 28
  58.9 14.4 %all-to-all-start.3 = ((f32[16,16,128]{2,1,0:T(8,128)}), f32[16,16,128]{2,1,0:T(8,128)S(1)}, u32[]{:S(2)}, u32[]{:S(2)}) async-start(f32[16,16,128]{2,1,0:T(8,128)} %reshape.709), calls=%async_computation.3 | async-start | bytes 262144 | tf_op jit(solution)/shard_map/all_to_all | solution.py:66
  78.2 11.7 %all-to-all-start.4 = ((f32[16,16,128]{2,1,0:T(8,128)}), f32[16,16,128]{2,1,0:T(8,128)S(1)}, u32[]{:S(2)}, u32[]{:S(2)}) async-start(f32[16,16,128]{2,1,0:T(8,128)} %reshape.712), calls=%async_computation.4 | async-start | bytes 262144 | tf_op jit(solution)/shard_map/all_to_all | solution.py:66
  90.2 1.7 copy-start
  90.6 1.3 copy-start.2
  90.7 1.4 copy-start.13
  91.9 1.5 copy-start.1
  92.1 5.9 %copy-start.8 = (s32[16]{0:T(128)S(1)}, s32[16]{0:T(128)}, u32[]{:S(2)}) copy-start(s32[16]{0:T(128)} %copy-done.7) | copy-start | bytes 196
  92.1 5.9 %copy-start.15 = (s32[128]{0:T(128)S(1)}, s32[128]{0:T(128)}, u32[]{:S(2)}) copy-start(s32[128]{0:T(128)} %iota_multiply_fusion) | copy-start | bytes 1540
  93.0 13.5 %copy-start.3 = (f32[2,128,2,128,1]{3,1,2,0,4:T(8,128)S(1)}, f32[2,128,2,128,1]{3,1,2,0,4:T(8,128)}, u32[]{:S(2)}) copy-start(f32[2,128,2,128,1]{3,1,2,0,4:T(8,128)} %get-tuple-element.8) | copy-start | bytes 786436
  93.4 14.9 %copy-start.14 = (s32[8]{0:T(128)S(1)}, s32[8]{0:T(128)}, u32[]{:S(2)}) copy-start(s32[8]{0:T(128)} %get-tuple-element.30) | copy-start | bytes 100
  94.5 11.7 %all-to-all-start.5 = ((f32[16,16,128]{2,1,0:T(8,128)}), f32[16,16,128]{2,1,0:T(8,128)S(1)}, u32[]{:S(2)}, u32[]{:S(2)}) async-start(f32[16,16,128]{2,1,0:T(8,128)} %copy.105), calls=%async_computation.5 | async-start | bytes 262144 | tf_op jit(solution)/shard_map/all_to_all | solution.py:66
  109.2 13.4 %copy-start.6 = (f32[2,128,2,128]{3,1,2,0:T(8,128)S(1)}, f32[2,128,2,128]{3,1,2,0:T(8,128)}, u32[]{:S(2)}) copy-start(f32[2,128,2,128]{3,1,2,0:T(8,128)} %get-tuple-element.7) | copy-start | bytes 786436
  124.4 11.3 %copy-start.11 = (s32[704]{0:T(1024)S(1)}, s32[704]{0:T(1024)}, u32[]{:S(2)}) copy-start(s32[704]{0:T(1024)} %copy-done.10) | copy-start | bytes 8452
  135.1 20.7 %copy-start.4 = (f32[704,256]{1,0:T(8,128)S(1)}, f32[704,256]{1,0:T(8,128)}, u32[]{:S(2)}) copy-start(f32[704,256]{1,0:T(8,128)} %param.12) | copy-start | bytes 2162692
  135.1 20.7 %copy-start.5 = (f32[704,256]{1,0:T(8,128)S(1)}, f32[704,256]{1,0:T(8,128)}, u32[]{:S(2)}) copy-start(f32[704,256]{1,0:T(8,128)} %pos_ref.1) | copy-start | bytes 2162692
  151.0 13.2 %all-to-all-start.9 = ((f32[16,11,128]{2,1,0:T(8,128)}), f32[16,11,128]{2,1,0:T(8,128)S(1)}, u32[]{:S(2)}, u32[]{:S(2)}) async-start(f32[16,11,128]{2,1,0:T(8,128)} %broadcast_in_dim.7), calls=%async_computation.9 | async-start | bytes 262144 | tf_op jit(solution)/shard_map/all_to_all | solution.py:80

commit v3 on v2

--- a/solution.py
+++ b/solution.py
@@ -80,47 +80,78 @@
     return lax.all_to_all(spread, "dom", 0, 0, tiled=True).reshape(rows.shape)
 
 
-KICK_ROWS = 64
+KICK_ROWS = 88
 SUB_ROWS = 8
-
-
-def kick_kernel(pos_ref, drift_ref, volt_ref, pos_out, en_out):
+CHUNKS = 4
+
+
+def weight_kernel(pos_ref, out_ref):
     def sub_block(i, carry):
         rows = pl.ds(pl.multiple_of(i * SUB_ROWS, SUB_ROWS), SUB_ROWS)
         place = pos_ref[rows, :]
-        volts = volt_ref[rows, :]
-        weighted = jnp.zeros_like(place)
         norm = jnp.zeros_like(place)
         for j in range(BINS):
             offset = place - (j + 0.5)
             table = jnp.exp(-0.5 * offset * offset)
-            weighted = weighted + table * volts[:, j : j + 1]
+            out_ref[rows, j, :] = table
             norm = norm + table
-        energy = drift_ref[rows, :] - weighted / norm
+        scale = 1.0 / norm
+        for j in range(BINS):
+            out_ref[rows, j, :] = out_ref[rows, j, :] * scale
+        return carry
+
+    lax.fori_loop(0, KICK_ROWS // SUB_ROWS, sub_block, 0)
+
+
+def weight_call(positions):
+    bunches, width = positions.shape
+    return pl.pallas_call(
+        weight_kernel,
+        grid=(bunches // KICK_ROWS,),
+        in_specs=[pl.BlockSpec((KICK_ROWS, width), lambda i: (i, 0))],
+        out_specs=pl.BlockSpec((KICK_ROWS, BINS, width), lambda i: (i, 0, 0)),
+        out_shape=jax.ShapeDtypeStruct((bunches, BINS, width), jnp.float32),
+        cost_estimate=pl.CostEstimate(
+            flops=10 * bunches * width * BINS,
+            transcendentals=bunches * width * BINS,
+            bytes_accessed=4 * bunches * width * (BINS + 1),
+        ),
+    )(positions)
+
+
+def kick_kernel(pos_ref, drift_ref, volt_ref, weight_ref, pos_out, en_out):
+    def sub_block(i, carry):
+        rows = pl.ds(pl.multiple_of(i * SUB_ROWS, SUB_ROWS), SUB_ROWS)
+        volts = volt_ref[rows, :]
+        kick = weight_ref[rows, 0, :] * volts[:, 0:1]
+        for j in range(1, BINS):
+            kick = kick + weight_ref[rows, j, :] * volts[:, j : j + 1]
+        energy = drift_ref[rows, :] - kick
         en_out[rows, :] = energy
-        pos_out[rows, :] = place + 0.25 * energy
+        pos_out[rows, :] = pos_ref[rows, :] + 0.25 * energy
         return carry
 
     lax.fori_loop(0, KICK_ROWS // SUB_ROWS, sub_block, 0)
 
 
-def kick_call(positions, drifted, volt_rows):
+def kick_call(positions, drifted, volt_rows, weights):
     bunches, width = positions.shape
     wide = pl.BlockSpec((KICK_ROWS, width), lambda i: (i, 0))
     narrow = pl.BlockSpec((KICK_ROWS, BINS), lambda i: (i, 0))
+    table = pl.BlockSpec((KICK_ROWS, BINS, width), lambda i: (i, 0, 0))
     shape = jax.ShapeDtypeStruct(positions.shape, jnp.float32)
     return pl.pallas_call(
         kick_kernel,
         grid=(bunches // KICK_ROWS,),
-        in_specs=[wide, wide, narrow],
+        in_specs=[wide, wide, narrow, table],
         out_specs=[wide, wide],
         out_shape=[shape, shape],
         cost_estimate=pl.CostEstimate(
-            flops=12 * bunches * width * BINS,
-            transcendentals=bunches * width * BINS,
-            bytes_accessed=4 * bunches * (4 * width + BINS),
+            flops=2 * bunches * width * BINS,
+            transcendentals=0,
+            bytes_accessed=4 * bunches * (width * (BINS + 4) + BINS),
         ),
-    )(positions, drifted, volt_rows)
+    )(positions, drifted, volt_rows, weights)
 
 
 def on_device(positions, energies, bucket, impedance, history):
@@ -139,6 +170,17 @@
     row_buckets = second_len * per_row
     own_rows = R2 * per_row
     partial_value = jnp.sum(kernel_table(positions), axis=2) / float(P_DEV * domains)
+    span = BUNCH_GRP // CHUNKS
+    pieces = [slice(c * span, (c + 1) * span) for c in range(CHUNKS)]
+    weights = []
+
+    def covered(operand, axis_name, split_axis, concat_axis):
+        piece = pieces[len(weights)]
+        place, operand = lax.optimization_barrier((positions[piece], operand))
+        got = exchange(operand, axis_name, split_axis, concat_axis)
+        got, weight = lax.optimization_barrier((got, weight_call(place)))
+        weights.append(weight)
+        return got
     first_row = bucket // row_buckets
     within = bucket % row_buckets
     owner_dom = within // own_rows
@@ -151,7 +193,7 @@
     first_table = block_table(first_len)
     second_table = block_table(second_len)
     third_table = block_table(N3)
-    received = exchange(density, "grp", 2, 0)
+    received = covered(density, "grp", 2, 0)
     rows = contract("nab,nok->oabk", received, first_table[0])
     second_global = domain_index * R2 + jnp.arange(R2, dtype=jnp.int32)
     depth_global = group_index * depth_len + jnp.arange(depth_len, dtype=jnp.int32)
@@ -162,14 +204,14 @@
         cycle_len,
     )
     twist = turn(rows, cos_turn, -sin_turn)
-    part = exchange(twist, "dom", 3, 1)
+    part = covered(twist, "dom", 3, 1)
     cols = contract("inbk,inom->obkm", part, second_table)
     second_freq = jnp.arange(second_len, dtype=jnp.int32)
     cos_turn, sin_turn = rotation(
         depth_global[:, None, None] * second_freq[None, None, :], plane_len
     )
     turned = turn(cols, cos_turn, -sin_turn)
-    part = exchange(turned, "grp", 3, 1)
+    part = covered(turned, "grp", 3, 1)
     full = contract("inac,inok->oack", part, third_table)
     norm_factor = 1.0 / math.sqrt(BUNCH_GRP * groups)
     spectrum = full * norm_factor
@@ -195,7 +237,7 @@
     depth_all = jnp.arange(N3, dtype=jnp.int32)
     cos_turn, sin_turn = rotation(second_own[None, :, None] * depth_all[None, None, :], plane_len)
     lift = turn(back, cos_turn, sin_turn)
-    part = exchange(lift, "grp", 3, 2)
+    part = covered(lift, "grp", 3, 2)
     spun = contract("iakb,ikon->oanb", part, conjugate(second_table))
     first_own = domain_index * first_part + jnp.arange(first_part, dtype=jnp.int32)
     cos_turn, sin_turn = rotation(
@@ -213,7 +255,12 @@
     owned_volts = contract("sb,sj->bj", picker, volt_slab)
     volt_rows = dom_sum(owned_volts, domains)
     drifted = energies - 0.5 * jnp.sin(two_pi * (positions - 0.5 * BINS) / BINS)
-    positions_out, energies_out = kick_call(positions, drifted, volt_rows)
+    outs = [
+        kick_call(positions[piece], drifted[piece], volt_rows[piece], weights[c])
+        for c, piece in enumerate(pieces)
+    ]
+    positions_out = jnp.concatenate([o[0] for o in outs])
+    energies_out = jnp.concatenate([o[1] for o in outs])
     return (positions_out, energies_out, spectrum)
 
 

time: 179 us -> 223 us (1.25)
  Pallas kernels: 13.1 us -> 58.2 us
  waiting for transfers between devices: 48.2 us -> 26.8 us
  starting transfers between devices: 37.9 us -> 49.7 us
  other arithmetic: 16.7 us -> 21.7 us
  local copies, waits for them, and re-layouts: 17.2 us -> 21.7 us
  blocking collectives: 35.7 us -> 31.4 us
  matrix products: 8.15 us -> 11.2 us
    pallas_call x0 -> x4, Pallas kernels: none -> 35.5 us  [weight_call(): pl.pallas_call(weight_kernel, grid=(bunches // KICK_ROWS,), in_specs=[pl....]
    all_to_all x4, waiting for transfers between devices: 30 us -> 0.01 us  [exchange(): lax.all_to_all(sent, axis_name, 0, 0, tiled=True).reshape((count,) + piece)]
    all_to_all x1 -> x0, blocking collectives: 13 us -> none  [dom_sum(): lax.all_to_all(rows.reshape(domains, -1, 128), 'dom', 0, 0, tiled=True)]
    pallas_call x1 -> x4, Pallas kernels: 13.1 us -> 22.7 us  [kick_call(): pl.pallas_call(kick_kernel, grid=(bunches // KICK_ROWS,), in_specs=[wide,...]
    all_to_all x2, blocking collectives: 22.7 us -> 31.4 us  [exchange(): lax.all_to_all(sent, axis_name, 0, 0, tiled=True).reshape((count,) + piece)]
    all_to_all x4, starting transfers between devices: 18.6 us -> 25.2 us  [exchange(): lax.all_to_all(sent, axis_name, 0, 0, tiled=True).reshape((count,) + piece)]
    all_to_all x1 -> x2, waiting for transfers between devices: 6.58 us -> 12.7 us  [dom_sum(): lax.all_to_all(rows.reshape(domains, -1, 128), 'dom', 0, 0, tiled=True)]
    all_to_all x1 -> x2, starting transfers between devices: 9.94 us -> 15.1 us  [dom_sum(): lax.all_to_all(rows.reshape(domains, -1, 128), 'dom', 0, 0, tiled=True)]
  transfers between devices with their start and end apart: 7 -> 8, of which waited for: 7 -> 4; matrix products, arithmetic and copies ran while one was open for 6% -> 5% of each run, Pallas kernels for 0% -> 16%
where the time goes in v3:
time: 223 us; the launch traced here: 222 us
  Pallas kernels  58.2 us (26%)
  starting transfers between devices  49.7 us (22%)
  blocking collectives  31.4 us (14%)
  waiting for transfers between devices  26.8 us (12%)
  other arithmetic  21.7 us (10%)
  local copies, waits for them, and re-layouts  21.7 us (10%)
  matrix products  11.2 us (5%)
    pallas_call x4, Pallas kernels, weight_call(): pl.pallas_call(weight_kernel, grid=(bunches // KICK_ROWS,), in_specs=[pl....  35.5 us
    all_to_all x2, blocking collectives, exchange(): lax.all_to_all(sent, axis_name, 0, 0, tiled=True).reshape((count,) + piece)  31.4 us
    all_to_all x4, starting transfers between devices, exchange(): lax.all_to_all(sent, axis_name, 0, 0, tiled=True).reshape((count,) + piece)  25.2 us
    pallas_call x4, Pallas kernels, kick_call(): pl.pallas_call(kick_kernel, grid=(bunches // KICK_ROWS,), in_specs=[wide,...  22.7 us
    all_to_all x2, starting transfers between devices, dom_sum(): lax.all_to_all(rows.reshape(domains, -1, 128), 'dom', 0, 0, tiled=True)  15.1 us
    all_to_all x2, waiting for transfers between devices, dom_sum(): return lax.all_to_all(spread, 'dom', 0, 0, tiled=True).reshape(rows.shape)  14.1 us
    all_to_all x2, waiting for transfers between devices, dom_sum(): lax.all_to_all(rows.reshape(domains, -1, 128), 'dom', 0, 0, tiled=True)  12.7 us
    dot_general x8, matrix products, contract(): return jnp.einsum(pattern, operand, matrix, precision=highest)  11.2 us
  transfers between devices with their start and end apart: 8, of which 4 were waited for; matrix products, arithmetic and copies ran while one was open for 5% of the time, Pallas kernels for 16%

profile of v3, /device:TPU:2, one launch (start us, length us, event | category | flops | bytes accessed | tf_op | source)
XLA Modules:
  0.0 221.8 jit_solution(15260968001622762100)
XLA Ops:
  0.7 5.8 %fusion.1 = f32[704,32]{1,0:T(8,128)S(1)} fusion(f32[32]{0:T(128)S(1)} %iota_add_fusion.3, f32[704,256]{1,0:T(8,128)} %param.11), kind=kLoop, calls=%fused_computation.2 | loop fusion | flops 23046144 | bytes 811136 | tf_op jit(solution)/shard_map/reduce_sum | solution.py:172
  6.5 0.8 div.48
  7.3 9.9 %all-to-all-start = ((f32[16,11,128]{2,1,0:T(8,128)}), f32[16,11,128]{2,1,0:T(8,128)S(1)}, u32[]{:S(2)}, u32[]{:S(2)}) async-start(f32[16,11,128]{2,1,0:T(8,128)} %div.48), calls=%async_computation | async-start | bytes 262144 | tf_op jit(solution)/shard_map/all_to_all | solution.py:77
  17.2 0.9 fusion.88
  18.5 1.0 fusion.34
  19.5 6.2 %all-to-all-done = f32[16,11,128]{2,1,0:T(8,128)S(1)} async-done(((f32[16,11,128]{2,1,0:T(8,128)}), f32[16,11,128]{2,1,0:T(8,128)S(1)}, u32[]{:S(2)}, u32[]{:S(2)}) %all-to-all-start) | async-done | bytes 90144 | tf_op jit(solution)/shard_map/all_to_all | solution.py:77
  26.4 4.6 %all-to-all-start.1 = ((f32[16,11,128]{2,1,0:T(8,128)}), f32[16,11,128]{2,1,0:T(8,128)S(1)}, u32[]{:S(2)}, u32[]{:S(2)}) async-start(f32[16,11,128]{2,1,0:T(8,128)} %broadcast_in_dim.6), calls=%async_computation.1 | async-start | bytes 262144 | tf_op jit(solution)/shard_map/all_to_all | solution.py:80
  31.2 1.7 fusion.32
  32.9 6.5 %all-to-all-done.1 = f32[16,11,128]{2,1,0:T(8,128)S(1)} async-done(((f32[16,11,128]{2,1,0:T(8,128)}), f32[16,11,128]{2,1,0:T(8,128)S(1)}, u32[]{:S(2)}, u32[]{:S(2)}) %all-to-all-start.1) | async-done | bytes 90144 | tf_op jit(solution)/shard_map/all_to_all | solution.py:80
  39.5 0.9 fusion.3
  41.0 1.1 reshape.708
  42.1 6.1 %all-to-all-start.2 = ((f32[16,8,128]{2,1,0:T(8,128)}), f32[16,8,128]{2,1,0:T(8,128)S(1)}, u32[]{:S(2)}, u32[]{:S(2)}) async-start(f32[16,8,128]{2,1,0:T(8,128)} %reshape.708), calls=%async_computation.2 | async-start | bytes 131072 | tf_op jit(solution)/shard_map/all_to_all | solution.py:66
  48.5 8.9 %shard_map.130.weight_ref = f32[176,32,256]{2,1,0:T(8,128)} custom-call(f32[176,256]{1,0:T(8,128)} %get-tuple-element.28.pos_ref), custom_call_target="tpu_custom_call" | custom-call | flops 14417920 | bytes 5947392 | tf_op jit(solution)/shard_map/pallas_call | solution.py:108
  59.5 1.0 reshape.711
  60.4 5.3 %all-to-all-start.3 = ((f32[16,16,128]{2,1,0:T(8,128)}), f32[16,16,128]{2,1,0:T(8,128)S(1)}, u32[]{:S(2)}, u32[]{:S(2)}) async-start(f32[16,16,128]{2,1,0:T(8,128)} %reshape.711), calls=%async_computation.3 | async-start | bytes 262144 | tf_op jit(solution)/shard_map/all_to_all | solution.py:66
  65.8 1.0 multiply_multiply_fusion.1
  66.7 8.9 %shard_map.131.weight_ref = f32[176,32,256]{2,1,0:T(8,128)} custom-call(f32[176,256]{1,0:T(8,128)} %get-tuple-element.31.pos_ref), custom_call_target="tpu_custom_call" | custom-call | flops 14417920 | bytes 5947392 | tf_op jit(solution)/shard_map/pallas_call | solution.py:108
  76.6 1.3 convolution_bitcast_fusion
  78.0 1.8 copy.126
  79.8 1.6 reshape.714
  81.4 6.6 %all-to-all-start.4 = ((f32[16,16,128]{2,1,0:T(8,128)}), f32[16,16,128]{2,1,0:T(8,128)S(1)}, u32[]{:S(2)}, u32[]{:S(2)}) async-start(f32[16,16,128]{2,1,0:T(8,128)} %reshape.714), calls=%async_computation.4 | async-start | bytes 262144 | tf_op jit(solution)/shard_map/all_to_all | solution.py:66
  88.0 1.9 maximum_bitcast_fusion
  90.0 8.9 %shard_map.132.weight_ref = f32[176,32,256]{2,1,0:T(8,128)} custom-call(f32[176,256]{1,0:T(8,128)} %get-tuple-element.34.pos_ref), custom_call_target="tpu_custom_call" | custom-call | flops 14417920 | bytes 5947392 | tf_op jit(solution)/shard_map/pallas_call | solution.py:108
  100.0 1.8 fusion.5
  101.8 1.2 bitcast_add_fusion
  103.0 1.2 bitcast_subtract_fusion
  104.2 2.0 convolution_bitcast_fusion.2
  106.6 1.1 copy.131
  107.6 7.2 %all-to-all-start.5 = ((f32[16,16,128]{2,1,0:T(8,128)}), f32[16,16,128]{2,1,0:T(8,128)S(1)}, u32[]{:S(2)}, u32[]{:S(2)}) async-start(f32[16,16,128]{2,1,0:T(8,128)} %copy.131), calls=%async_computation.5 | async-start | bytes 262144 | tf_op jit(solution)/shard_map/all_to_all | solution.py:66
  114.9 8.9 %shard_map.133.weight_ref = f32[176,32,256]{2,1,0:T(8,128)} custom-call(f32[176,256]{1,0:T(8,128)} %get-tuple-element.37.pos_ref), custom_call_target="tpu_custom_call" | custom-call | flops 14417920 | bytes 5947392 | tf_op jit(solution)/shard_map/pallas_call | solution.py:108
  124.3 1.8 convolution_bitcast_fusion.1
  127.3 17.0 %all_to_all.50 = f32[16,16,128]{2,1,0:T(8,128)S(1)} all-to-all(f32[16,16,128]{2,1,0:T(8,128)S(1)} %reshape.720), channel_id=1, replica_groups=mesh['grp'=16,'dom'=16] {'dom'}, dimensions={0} | all-to-all | bytes 262144 | tf_op jit(solution)/shard_map/all_to_all | solution.py:66
  144.9 1.8 fusion.6
  147.2 14.4 %all_to_all.51 = f32[16,8,128]{2,1,0:T(8,128)S(1)} all-to-all(f32[16,8,128]{2,1,0:T(8,128)S(1)} %reshape.723), channel_id=1, replica_groups=mesh['grp'=16,'dom'=16] {'grp'}, dimensions={0} | all-to-all | bytes 131072 | tf_op jit(solution)/shard_map/all_to_all | solution.py:66
  162.2 1.4 fusion.2
  163.6 0.8 reshape.725
  164.4 5.2 %all-to-all-start.8 = ((f32[16,11,128]{2,1,0:T(8,128)}), f32[16,11,128]{2,1,0:T(8,128)S(1)}, u32[]{:S(2)}, u32[]{:S(2)}) async-start(f32[16,11,128]{2,1,0:T(8,128)} %reshape.725), calls=%async_computation.8 | async-start | bytes 262144 | tf_op jit(solution)/shard_map/all_to_all | solution.py:77
  169.6 2.4 %multiply_subtract_fusion = f32[704,256]{1,0:T(8,128)S(1)} fusion(f32[704,256]{1,0:T(8,128)S(1)} %copy-done.3, f32[704,256]{1,0:T(8,128)S(1)} %copy-done), kind=kLoop, calls=%fused_computation.27 | loop fusion | flops 720896 | bytes 2162688 | tf_op jit(solution)/shard_map/sub | solution.py:257
  172.1 6.5 %all-to-all-done.8 = f32[16,11,128]{2,1,0:T(8,128)S(1)} async-done(((f32[16,11,128]{2,1,0:T(8,128)}), f32[16,11,128]{2,1,0:T(8,128)S(1)}, u32[]{:S(2)}, u32[]{:S(2)}) %all-to-all-start.8) | async-done | bytes 90144 | tf_op jit(solution)/shard_map/all_to_all | solution.py:77
  179.3 4.8 %all-to-all-start.9 = ((f32[16,11,128]{2,1,0:T(8,128)}), f32[16,11,128]{2,1,0:T(8,128)S(1)}, u32[]{:S(2)}, u32[]{:S(2)}) async-start(f32[16,11,128]{2,1,0:T(8,128)} %broadcast_in_dim.7), calls=%async_computation.9 | async-start | bytes 262144 | tf_op jit(solution)/shard_map/all_to_all | solution.py:80
  184.0 0.9 fusion.87
  184.9 7.6 %all-to-all-done.9 = f32[16,11,128]{2,1,0:T(8,128)S(1)} async-done(((f32[16,11,128]{2,1,0:T(8,128)}), f32[16,11,128]{2,1,0:T(8,128)S(1)}, u32[]{:S(2)}, u32[]{:S(2)}) %all-to-all-start.9) | async-done | bytes 90144 | tf_op jit(solution)/shard_map/all_to_all | solution.py:80
  195.4 5.7 %shard_map.134 = (f32[176,256]{1,0:T(8,128)}, f32[176,256]{1,0:T(8,128)}) custom-call(f32[176,256]{1,0:T(8,128)} %get-tuple-element.28.pos_ref, f32[176,256]{1,0:T(8,128)} %get-tuple-element.51.drift_ref, f32[176,32]{1,0:T(8,128)} %slice.156.volt_ref, f32[176,32,256]{2,1,0:T(8,128)} %shard_map.130.weight_ref), custom_call_target="tpu_custom_call" | custom-call | flops 2883584 | bytes 6510592 | tf_op jit(solution)/shard_map/pallas_call | solution.py:143
  201.1 5.6 %shard_map.135 = (f32[176,256]{1,0:T(8,128)}, f32[176,256]{1,0:T(8,128)}) custom-call(f32[176,256]{1,0:T(8,128)} %get-tuple-element.31.pos_ref, f32[176,256]{1,0:T(8,128)} %get-tuple-element.54.drift_ref, f32[176,32]{1,0:T(8,128)} %slice.159.volt_ref, f32[176,32,256]{2,1,0:T(8,128)} %shard_map.131.weight_ref), custom_call_target="tpu_custom_call" | custom-call | flops 2883584 | bytes 6510592 | tf_op jit(solution)/shard_map/pallas_call | solution.py:143
  206.7 5.7 %shard_map.136 = (f32[176,256]{1,0:T(8,128)}, f32[176,256]{1,0:T(8,128)}) custom-call(f32[176,256]{1,0:T(8,128)} %get-tuple-element.34.pos_ref, f32[176,256]{1,0:T(8,128)} %get-tuple-element.53.drift_ref, f32[176,32]{1,0:T(8,128)} %slice.162.volt_ref, f32[176,32,256]{2,1,0:T(8,128)} %shard_map.132.weight_ref), custom_call_target="tpu_custom_call" | custom-call | flops 2883584 | bytes 6510592 | tf_op jit(solution)/shard_map/pallas_call | solution.py:143
  212.4 5.7 %shard_map.137 = (f32[176,256]{1,0:T(8,128)}, f32[176,256]{1,0:T(8,128)}) custom-call(f32[176,256]{1,0:T(8,128)} %get-tuple-element.37.pos_ref, f32[176,256]{1,0:T(8,128)} %get-tuple-element.52.drift_ref, f32[176,32]{1,0:T(8,128)} %slice.165.volt_ref, f32[176,32,256]{2,1,0:T(8,128)} %shard_map.133.weight_ref), custom_call_target="tpu_custom_call" | custom-call | flops 2883584 | bytes 6510592 | tf_op jit(solution)/shard_map/pallas_call | solution.py:143
  218.1 1.8 pad_maximum_fusion.4
  220.0 1.8 pad_maximum_fusion.3
  (87 shorter events, 14.0 us)
Async XLA Ops:
  0.6 16.6 %copy-start = (f32[704,256]{1,0:T(8,128)S(1)}, f32[704,256]{1,0:T(8,128)}, u32[]{:S(2)}) copy-start(f32[704,256]{1,0:T(8,128)} %param.11) | copy-start | bytes 2162692
  0.7 17.5 %copy-start.11 = (s32[704]{0:T(1024)S(1)}, s32[704]{0:T(1024)}, u32[]{:S(2)}) copy-start(s32[704]{0:T(1024)} %param.13) | copy-start | bytes 8452
  7.3 18.4 %all-to-all-start = ((f32[16,11,128]{2,1,0:T(8,128)}), f32[16,11,128]{2,1,0:T(8,128)S(1)}, u32[]{:S(2)}, u32[]{:S(2)}) async-start(f32[16,11,128]{2,1,0:T(8,128)} %div.48), calls=%async_computation | async-start | bytes 262144 | tf_op jit(solution)/shard_map/all_to_all | solution.py:77
  26.4 13.0 %all-to-all-start.1 = ((f32[16,11,128]{2,1,0:T(8,128)}), f32[16,11,128]{2,1,0:T(8,128)S(1)}, u32[]{:S(2)}, u32[]{:S(2)}) async-start(f32[16,11,128]{2,1,0:T(8,128)} %broadcast_in_dim.6), calls=%async_computation.1 | async-start | bytes 262144 | tf_op jit(solution)/shard_map/all_to_all | solution.py:80
  42.1 15.3 %all-to-all-start.2 = ((f32[16,8,128]{2,1,0:T(8,128)}), f32[16,8,128]{2,1,0:T(8,128)S(1)}, u32[]{:S(2)}, u32[]{:S(2)}) async-start(f32[16,8,128]{2,1,0:T(8,128)} %reshape.708), calls=%async_computation.2 | async-start | bytes 131072 | tf_op jit(solution)/shard_map/all_to_all | solution.py:66
  48.5 17.3 %copy-start.12 = (f32[2]{0:T(128)S(1)}, f32[2]{0:T(128)}, u32[]{:S(2)}) copy-start(f32[2]{0:T(128)} %constant.164.clone) | copy-start | bytes 28
  60.4 15.2 %all-to-all-start.3 = ((f32[16,16,128]{2,1,0:T(8,128)}), f32[16,16,128]{2,1,0:T(8,128)S(1)}, u32[]{:S(2)}, u32[]{:S(2)}) async-start(f32[16,16,128]{2,1,0:T(8,128)} %reshape.711), calls=%async_computation.3 | async-start | bytes 262144 | tf_op jit(solution)/shard_map/all_to_all | solution.py:66
  81.4 17.4 %all-to-all-start.4 = ((f32[16,16,128]{2,1,0:T(8,128)}), f32[16,16,128]{2,1,0:T(8,128)S(1)}, u32[]{:S(2)}, u32[]{:S(2)}) async-start(f32[16,16,128]{2,1,0:T(8,128)} %reshape.714), calls=%async_computation.4 | async-start | bytes 262144 | tf_op jit(solution)/shard_map/all_to_all | solution.py:66
  101.8 22.0 %copy-start.1 = (f32[2,8,8,256]{3,2,1,0:T(8,128)}, f32[2,8,8,256]{3,2,1,0:T(8,128)S(1)}, u32[]{:S(2)}) copy-start(f32[2,8,8,256]{3,2,1,0:T(8,128)S(1)} %fusion.5) | copy-start | bytes 393220
  106.2 18.1 %copy-start.2 = (f32[2,128,2,128,1]{3,1,2,0,4:T(8,128)S(1)}, f32[2,128,2,128,1]{3,1,2,0,4:T(8,128)}, u32[]{:S(2)}) copy-start(f32[2,128,2,128,1]{3,1,2,0,4:T(8,128)} %get-tuple-element.60) | copy-start | bytes 786436
  107.6 16.2 %all-to-all-start.5 = ((f32[16,16,128]{2,1,0:T(8,128)}), f32[16,16,128]{2,1,0:T(8,128)S(1)}, u32[]{:S(2)}, u32[]{:S(2)}) async-start(f32[16,16,128]{2,1,0:T(8,128)} %copy.131), calls=%async_computation.5 | async-start | bytes 262144 | tf_op jit(solution)/shard_map/all_to_all | solution.py:66
  123.8 21.1 %copy-start.4 = (f32[2,128,2,128]{3,1,2,0:T(8,128)S(1)}, f32[2,128,2,128]{3,1,2,0:T(8,128)}, u32[]{:S(2)}) copy-start(f32[2,128,2,128]{3,1,2,0:T(8,128)} %get-tuple-element.59) | copy-start | bytes 786436
  127.0 42.7 %copy-start.3 = (f32[704,256]{1,0:T(8,128)S(1)}, f32[704,256]{1,0:T(8,128)}, u32[]{:S(2)}) copy-start(f32[704,256]{1,0:T(8,128)} %param.12) | copy-start | bytes 2162692
  164.4 14.2 %all-to-all-start.8 = ((f32[16,11,128]{2,1,0:T(8,128)}), f32[16,11,128]{2,1,0:T(8,128)S(1)}, u32[]{:S(2)}, u32[]{:S(2)}) async-start(f32[16,11,128]{2,1,0:T(8,128)} %reshape.725), calls=%async_computation.8 | async-start | bytes 262144 | tf_op jit(solution)/shard_map/all_to_all | solution.py:77
  179.3 13.2 %all-to-all-start.9 = ((f32[16,11,128]{2,1,0:T(8,128)}), f32[16,11,128]{2,1,0:T(8,128)S(1)}, u32[]{:S(2)}, u32[]{:S(2)}) async-start(f32[16,11,128]{2,1,0:T(8,128)} %broadcast_in_dim.7), calls=%async_computation.9 | async-start | bytes 262144 | tf_op jit(solution)/shard_map/all_to_all | solution.py:80
  206.7 11.4 %copy-start.7 = (f32[176,256]{1,0:T(8,128)S(1)}, f32[176,256]{1,0:T(8,128)}, u32[]{:S(2)}) copy-start(f32[176,256]{1,0:T(8,128)} %get-tuple-element.47) | copy-start | bytes 540676
  206.7 11.4 %copy-start.9 = (f32[176,256]{1,0:T(8,128)S(1)}, f32[176,256]{1,0:T(8,128)}, u32[]{:S(2)}) copy-start(f32[176,256]{1,0:T(8,128)} %get-tuple-element.48) | copy-start | bytes 540676
  206.7 13.3 %copy-start.5 = (f32[176,256]{1,0:T(8,128)S(1)}, f32[176,256]{1,0:T(8,128)}, u32[]{:S(2)}) copy-start(f32[176,256]{1,0:T(8,128)} %get-tuple-element.40) | copy-start | bytes 540676
  206.7 13.3 %copy-start.6 = (f32[176,256]{1,0:T(8,128)S(1)}, f32[176,256]{1,0:T(8,128)}, u32[]{:S(2)}) copy-start(f32[176,256]{1,0:T(8,128)} %get-tuple-element.42) | copy-start | bytes 540676
  212.4 5.7 %copy-start.10 = (f32[176,256]{1,0:T(8,128)S(1)}, f32[176,256]{1,0:T(8,128)}, u32[]{:S(2)}) copy-start(f32[176,256]{1,0:T(8,128)} %get-tuple-element.49) | copy-start | bytes 540676
  212.4 7.5 %copy-start.8 = (f32[176,256]{1,0:T(8,128)S(1)}, f32[176,256]{1,0:T(8,128)}, u32[]{:S(2)}) copy-start(f32[176,256]{1,0:T(8,128)} %get-tuple-element.44) | copy-start | bytes 540676

commit v4 on v3

--- a/solution.py
+++ b/solution.py
@@ -85,7 +85,7 @@
 CHUNKS = 4
 
 
-def weight_kernel(pos_ref, out_ref):
+def weight_kernel(pos_ref, table_ref, norm_ref):
     def sub_block(i, carry):
         rows = pl.ds(pl.multiple_of(i * SUB_ROWS, SUB_ROWS), SUB_ROWS)
         place = pos_ref[rows, :]
@@ -93,11 +93,9 @@
         for j in range(BINS):
             offset = place - (j + 0.5)
             table = jnp.exp(-0.5 * offset * offset)
-            out_ref[rows, j, :] = table
+            table_ref[j, rows, :] = table
             norm = norm + table
-        scale = 1.0 / norm
-        for j in range(BINS):
-            out_ref[rows, j, :] = out_ref[rows, j, :] * scale
+        norm_ref[rows, :] = norm
         return carry
 
     lax.fori_loop(0, KICK_ROWS // SUB_ROWS, sub_block, 0)
@@ -105,28 +103,32 @@
 
 def weight_call(positions):
     bunches, width = positions.shape
+    wide = pl.BlockSpec((KICK_ROWS, width), lambda i: (i, 0))
     return pl.pallas_call(
         weight_kernel,
         grid=(bunches // KICK_ROWS,),
-        in_specs=[pl.BlockSpec((KICK_ROWS, width), lambda i: (i, 0))],
-        out_specs=pl.BlockSpec((KICK_ROWS, BINS, width), lambda i: (i, 0, 0)),
-        out_shape=jax.ShapeDtypeStruct((bunches, BINS, width), jnp.float32),
+        in_specs=[wide],
+        out_specs=[pl.BlockSpec((BINS, KICK_ROWS, width), lambda i: (0, i, 0)), wide],
+        out_shape=[
+            jax.ShapeDtypeStruct((BINS, bunches, width), jnp.float32),
+            jax.ShapeDtypeStruct((bunches, width), jnp.float32),
+        ],
         cost_estimate=pl.CostEstimate(
-            flops=10 * bunches * width * BINS,
+            flops=6 * bunches * width * BINS,
             transcendentals=bunches * width * BINS,
-            bytes_accessed=4 * bunches * width * (BINS + 1),
+            bytes_accessed=4 * bunches * width * (BINS + 2),
         ),
     )(positions)
 
 
-def kick_kernel(pos_ref, drift_ref, volt_ref, weight_ref, pos_out, en_out):
+def kick_kernel(pos_ref, drift_ref, volt_ref, table_ref, norm_ref, pos_out, en_out):
     def sub_block(i, carry):
         rows = pl.ds(pl.multiple_of(i * SUB_ROWS, SUB_ROWS), SUB_ROWS)
         volts = volt_ref[rows, :]
-        kick = weight_ref[rows, 0, :] * volts[:, 0:1]
+        weighted = table_ref[0, rows, :] * volts[:, 0:1]
         for j in range(1, BINS):
-            kick = kick + weight_ref[rows, j, :] * volts[:, j : j + 1]
-        energy = drift_ref[rows, :] - kick
+            weighted = weighted + table_ref[j, rows, :] * volts[:, j : j + 1]
+        energy = drift_ref[rows, :] - weighted / norm_ref[rows, :]
         en_out[rows, :] = energy
         pos_out[rows, :] = pos_ref[rows, :] + 0.25 * energy
         return carry
@@ -135,23 +137,24 @@
 
 
 def kick_call(positions, drifted, volt_rows, weights):
+    table, norm = weights
     bunches, width = positions.shape
     wide = pl.BlockSpec((KICK_ROWS, width), lambda i: (i, 0))
     narrow = pl.BlockSpec((KICK_ROWS, BINS), lambda i: (i, 0))
-    table = pl.BlockSpec((KICK_ROWS, BINS, width), lambda i: (i, 0, 0))
+    tall = pl.BlockSpec((BINS, KICK_ROWS, width), lambda i: (0, i, 0))
     shape = jax.ShapeDtypeStruct(positions.shape, jnp.float32)
     return pl.pallas_call(
         kick_kernel,
         grid=(bunches // KICK_ROWS,),
-        in_specs=[wide, wide, narrow, table],
+        in_specs=[wide, wide, narrow, tall, wide],
         out_specs=[wide, wide],
         out_shape=[shape, shape],
         cost_estimate=pl.CostEstimate(
             flops=2 * bunches * width * BINS,
             transcendentals=0,
-            bytes_accessed=4 * bunches * (width * (BINS + 4) + BINS),
+            bytes_accessed=4 * bunches * (width * (BINS + 5) + BINS),
         ),
-    )(positions, drifted, volt_rows, weights)
+    )(positions, drifted, volt_rows, table, norm)
 
 
 def on_device(positions, energies, bucket, impedance, history):

time: 223 us -> 204 us (0.915)
  Pallas kernels: 58.2 us -> 38.5 us
  waiting for transfers between devices: 26.8 us -> 40 us
  blocking collectives: 31.4 us -> 23.6 us
  starting transfers between devices: 49.7 us -> 44.6 us
    pallas_call x4, Pallas kernels: 35.5 us -> 16.5 us  [weight_call(): pl.pallas_call(weight_kernel, grid=(bunches // KICK_ROWS,), in_specs=[wid...]
    all_to_all x4, waiting for transfers between devices: 0.01 us -> 13.3 us  [exchange(): lax.all_to_all(sent, axis_name, 0, 0, tiled=True).reshape((count,) + piece)]
    all_to_all x2, blocking collectives: 31.4 us -> 23.6 us  [exchange(): lax.all_to_all(sent, axis_name, 0, 0, tiled=True).reshape((count,) + piece)]
    all_to_all x4, starting transfers between devices: 25.2 us -> 19.9 us  [exchange(): lax.all_to_all(sent, axis_name, 0, 0, tiled=True).reshape((count,) + piece)]
  transfers between devices with their start and end apart: 8 -> 8, of which waited for: 4 -> 8; matrix products, arithmetic and copies ran while one was open for 5% -> 5% of each run, Pallas kernels for 16% -> 8%
where the time goes in v4:
time: 204 us; the launch traced here: 203 us
  starting transfers between devices  44.6 us (22%)
  waiting for transfers between devices  40 us (20%)
  Pallas kernels  38.5 us (19%)
  blocking collectives  23.6 us (12%)
  other arithmetic  21.8 us (11%)
  local copies, waits for them, and re-layouts  21.7 us (11%)
  matrix products  11.2 us (5%)
    all_to_all x2, blocking collectives, exchange(): lax.all_to_all(sent, axis_name, 0, 0, tiled=True).reshape((count,) + piece)  23.6 us
    pallas_call x4, Pallas kernels, kick_call(): pl.pallas_call(kick_kernel, grid=(bunches // KICK_ROWS,), in_specs=[wide,...  22.1 us
    all_to_all x4, starting transfers between devices, exchange(): lax.all_to_all(sent, axis_name, 0, 0, tiled=True).reshape((count,) + piece)  19.9 us
    pallas_call x4, Pallas kernels, weight_call(): pl.pallas_call(weight_kernel, grid=(bunches // KICK_ROWS,), in_specs=[wid...  16.5 us
    all_to_all x2, starting transfers between devices, dom_sum(): lax.all_to_all(rows.reshape(domains, -1, 128), 'dom', 0, 0, tiled=True)  15.3 us
    all_to_all x2, waiting for transfers between devices, dom_sum(): return lax.all_to_all(spread, 'dom', 0, 0, tiled=True).reshape(rows.shape)  14.1 us
    all_to_all x4, waiting for transfers between devices, exchange(): lax.all_to_all(sent, axis_name, 0, 0, tiled=True).reshape((count,) + piece)  13.3 us
    all_to_all x2, waiting for transfers between devices, dom_sum(): lax.all_to_all(rows.reshape(domains, -1, 128), 'dom', 0, 0, tiled=True)  12.7 us
  transfers between devices with their start and end apart: 8, of which 8 were waited for; matrix products, arithmetic and copies ran while one was open for 5% of the time, Pallas kernels for 8%

profile of v4, /device:TPU:2, one launch (start us, length us, event | category | flops | bytes accessed | tf_op | source)
XLA Modules:
  0.0 202.5 jit_solution(8889041673164852460)
XLA Ops:
  0.7 5.8 %fusion.1 = f32[704,32]{1,0:T(8,128)S(1)} fusion(f32[32]{0:T(128)S(1)} %iota_add_fusion.3, f32[704,256]{1,0:T(8,128)} %param.11), kind=kLoop, calls=%fused_computation.2 | loop fusion | flops 23046144 | bytes 811136 | tf_op jit(solution)/shard_map/reduce_sum | solution.py:175
  7.3 9.9 %all-to-all-start = ((f32[16,11,128]{2,1,0:T(8,128)}), f32[16,11,128]{2,1,0:T(8,128)S(1)}, u32[]{:S(2)}, u32[]{:S(2)}) async-start(f32[16,11,128]{2,1,0:T(8,128)} %div.48), calls=%async_computation | async-start | bytes 262144 | tf_op jit(solution)/shard_map/all_to_all | solution.py:77
  17.2 0.9 fusion.88
  18.5 1.0 fusion.34
  19.5 6.2 %all-to-all-done = f32[16,11,128]{2,1,0:T(8,128)S(1)} async-done(((f32[16,11,128]{2,1,0:T(8,128)}), f32[16,11,128]{2,1,0:T(8,128)S(1)}, u32[]{:S(2)}, u32[]{:S(2)}) %all-to-all-start) | async-done | bytes 90144 | tf_op jit(solution)/shard_map/all_to_all | solution.py:77
  26.4 4.6 %all-to-all-start.1 = ((f32[16,11,128]{2,1,0:T(8,128)}), f32[16,11,128]{2,1,0:T(8,128)S(1)}, u32[]{:S(2)}, u32[]{:S(2)}) async-start(f32[16,11,128]{2,1,0:T(8,128)} %broadcast_in_dim.6), calls=%async_computation.1 | async-start | bytes 262144 | tf_op jit(solution)/shard_map/all_to_all | solution.py:80
  31.2 1.7 fusion.32
  32.9 6.5 %all-to-all-done.1 = f32[16,11,128]{2,1,0:T(8,128)S(1)} async-done(((f32[16,11,128]{2,1,0:T(8,128)}), f32[16,11,128]{2,1,0:T(8,128)S(1)}, u32[]{:S(2)}, u32[]{:S(2)}) %all-to-all-start.1) | async-done | bytes 90144 | tf_op jit(solution)/shard_map/all_to_all | solution.py:80
  41.0 1.1 reshape.708
  42.1 6.1 %all-to-all-start.2 = ((f32[16,8,128]{2,1,0:T(8,128)}), f32[16,8,128]{2,1,0:T(8,128)S(1)}, u32[]{:S(2)}, u32[]{:S(2)}) async-start(f32[16,8,128]{2,1,0:T(8,128)} %reshape.708), calls=%async_computation.2 | async-start | bytes 131072 | tf_op jit(solution)/shard_map/all_to_all | solution.py:66
  48.5 4.2 %shard_map.130 = (f32[32,176,256]{2,1,0:T(8,128)}, f32[176,256]{1,0:T(8,128)}) custom-call(f32[176,256]{1,0:T(8,128)} %get-tuple-element.40.pos_ref), custom_call_target="tpu_custom_call" | custom-call | flops 8650752 | bytes 6127616 | tf_op jit(solution)/shard_map/pallas_call | solution.py:107
  52.7 3.2 %all-to-all-done.2 = f32[16,8,128]{2,1,0:T(8,128)S(1)} async-done(((f32[16,8,128]{2,1,0:T(8,128)}), f32[16,8,128]{2,1,0:T(8,128)S(1)}, u32[]{:S(2)}, u32[]{:S(2)}) %all-to-all-start.2) | async-done | bytes 65568 | tf_op jit(solution)/shard_map/all_to_all | solution.py:66
  58.0 1.0 reshape.711
  59.0 5.3 %all-to-all-start.3 = ((f32[16,16,128]{2,1,0:T(8,128)}), f32[16,16,128]{2,1,0:T(8,128)S(1)}, u32[]{:S(2)}, u32[]{:S(2)}) async-start(f32[16,16,128]{2,1,0:T(8,128)} %reshape.711), calls=%async_computation.3 | async-start | bytes 262144 | tf_op jit(solution)/shard_map/all_to_all | solution.py:66
  64.3 1.0 multiply_multiply_fusion.1
  65.3 4.1 %shard_map.131 = (f32[32,176,256]{2,1,0:T(8,128)}, f32[176,256]{1,0:T(8,128)}) custom-call(f32[176,256]{1,0:T(8,128)} %get-tuple-element.45.pos_ref), custom_call_target="tpu_custom_call" | custom-call | flops 8650752 | bytes 6127616 | tf_op jit(solution)/shard_map/pallas_call | solution.py:107
  69.3 3.9 %all-to-all-done.3 = f32[16,16,128]{2,1,0:T(8,128)S(1)} async-done(((f32[16,16,128]{2,1,0:T(8,128)}), f32[16,16,128]{2,1,0:T(8,128)S(1)}, u32[]{:S(2)}, u32[]{:S(2)}) %all-to-all-start.3) | async-done | bytes 131104 | tf_op jit(solution)/shard_map/all_to_all | solution.py:66
  74.2 1.3 convolution_bitcast_fusion
  75.6 1.8 copy.126
  77.4 1.6 reshape.714
  79.0 3.5 %all-to-all-start.4 = ((f32[16,16,128]{2,1,0:T(8,128)}), f32[16,16,128]{2,1,0:T(8,128)S(1)}, u32[]{:S(2)}, u32[]{:S(2)}) async-start(f32[16,16,128]{2,1,0:T(8,128)} %reshape.714), calls=%async_computation.4 | async-start | bytes 262144 | tf_op jit(solution)/shard_map/all_to_all | solution.py:66
  82.6 1.9 maximum_bitcast_fusion
  84.5 4.1 %shard_map.132 = (f32[32,176,256]{2,1,0:T(8,128)}, f32[176,256]{1,0:T(8,128)}) custom-call(f32[176,256]{1,0:T(8,128)} %get-tuple-element.50.pos_ref), custom_call_target="tpu_custom_call" | custom-call | flops 8650752 | bytes 6127616 | tf_op jit(solution)/shard_map/pallas_call | solution.py:107
  88.5 2.2 %all-to-all-done.4 = f32[16,16,128]{2,1,0:T(8,128)S(1)} async-done(((f32[16,16,128]{2,1,0:T(8,128)}), f32[16,16,128]{2,1,0:T(8,128)S(1)}, u32[]{:S(2)}, u32[]{:S(2)}) %all-to-all-start.4) | async-done | bytes 131104 | tf_op jit(solution)/shard_map/all_to_all | solution.py:66
  91.9 1.8 fusion.5
  93.7 1.2 bitcast_add_fusion
  95.0 1.2 bitcast_subtract_fusion
  96.2 2.0 convolution_bitcast_fusion.2
  98.5 1.1 copy.131
  99.6 5.0 %all-to-all-start.5 = ((f32[16,16,128]{2,1,0:T(8,128)}), f32[16,16,128]{2,1,0:T(8,128)S(1)}, u32[]{:S(2)}, u32[]{:S(2)}) async-start(f32[16,16,128]{2,1,0:T(8,128)} %copy.131), calls=%async_computation.5 | async-start | bytes 262144 | tf_op jit(solution)/shard_map/all_to_all | solution.py:66
  104.7 4.1 %shard_map.133 = (f32[32,176,256]{2,1,0:T(8,128)}, f32[176,256]{1,0:T(8,128)}) custom-call(f32[176,256]{1,0:T(8,128)} %get-tuple-element.55.pos_ref), custom_call_target="tpu_custom_call" | custom-call | flops 8650752 | bytes 6127616 | tf_op jit(solution)/shard_map/pallas_call | solution.py:107
  108.8 4.0 %all-to-all-done.5 = f32[16,16,128]{2,1,0:T(8,128)S(1)} async-done(((f32[16,16,128]{2,1,0:T(8,128)}), f32[16,16,128]{2,1,0:T(8,128)S(1)}, u32[]{:S(2)}, u32[]{:S(2)}) %all-to-all-start.5) | async-done | bytes 131104 | tf_op jit(solution)/shard_map/all_to_all | solution.py:66
  113.3 1.8 convolution_bitcast_fusion.1
  116.2 13.2 %all_to_all.50 = f32[16,16,128]{2,1,0:T(8,128)S(1)} all-to-all(f32[16,16,128]{2,1,0:T(8,128)S(1)} %reshape.720), channel_id=1, replica_groups=mesh['grp'=16,'dom'=16] {'dom'}, dimensions={0} | all-to-all | bytes 262144 | tf_op jit(solution)/shard_map/all_to_all | solution.py:66
  130.1 1.8 fusion.6
  132.4 10.4 %all_to_all.51 = f32[16,8,128]{2,1,0:T(8,128)S(1)} all-to-all(f32[16,8,128]{2,1,0:T(8,128)S(1)} %reshape.723), channel_id=1, replica_groups=mesh['grp'=16,'dom'=16] {'grp'}, dimensions={0} | all-to-all | bytes 131072 | tf_op jit(solution)/shard_map/all_to_all | solution.py:66
  143.4 1.4 fusion.2
  145.6 5.4 %all-to-all-start.8 = ((f32[16,11,128]{2,1,0:T(8,128)}), f32[16,11,128]{2,1,0:T(8,128)S(1)}, u32[]{:S(2)}, u32[]{:S(2)}) async-start(f32[16,11,128]{2,1,0:T(8,128)} %reshape.725), calls=%async_computation.8 | async-start | bytes 262144 | tf_op jit(solution)/shard_map/all_to_all | solution.py:77
  151.0 2.4 %multiply_subtract_fusion = f32[704,256]{1,0:T(8,128)S(1)} fusion(f32[704,256]{1,0:T(8,128)S(1)} %copy-done.3, f32[704,256]{1,0:T(8,128)S(1)} %copy-done), kind=kLoop, calls=%fused_computation.27 | loop fusion | flops 720896 | bytes 2162688 | tf_op jit(solution)/shard_map/sub | solution.py:260
  153.4 6.5 %all-to-all-done.8 = f32[16,11,128]{2,1,0:T(8,128)S(1)} async-done(((f32[16,11,128]{2,1,0:T(8,128)}), f32[16,11,128]{2,1,0:T(8,128)S(1)}, u32[]{:S(2)}, u32[]{:S(2)}) %all-to-all-start.8) | async-done | bytes 90144 | tf_op jit(solution)/shard_map/all_to_all | solution.py:77
  160.6 4.8 %all-to-all-start.9 = ((f32[16,11,128]{2,1,0:T(8,128)}), f32[16,11,128]{2,1,0:T(8,128)S(1)}, u32[]{:S(2)}, u32[]{:S(2)}) async-start(f32[16,11,128]{2,1,0:T(8,128)} %broadcast_in_dim.7), calls=%async_computation.9 | async-start | bytes 262144 | tf_op jit(solution)/shard_map/all_to_all | solution.py:80
  166.3 7.6 %all-to-all-done.9 = f32[16,11,128]{2,1,0:T(8,128)S(1)} async-done(((f32[16,11,128]{2,1,0:T(8,128)}), f32[16,11,128]{2,1,0:T(8,128)S(1)}, u32[]{:S(2)}, u32[]{:S(2)}) %all-to-all-start.9) | async-done | bytes 90144 | tf_op jit(solution)/shard_map/all_to_all | solution.py:80
  176.7 5.5 %shard_map.134 = (f32[176,256]{1,0:T(8,128)}, f32[176,256]{1,0:T(8,128)}) custom-call(f32[176,256]{1,0:T(8,128)} %get-tuple-element.40.pos_ref, f32[176,256]{1,0:T(8,128)} %get-tuple-element.75.drift_ref, f32[176,32]{1,0:T(8,128)} %slice.156.volt_ref, f32[32,176,256]{2,1,0:T(8,128)} %get-tuple-element.59.table_ref, f32[176,256]{1,0:T(8,128)} %get-tuple-element.60.norm_ref), custom_call_target="tpu_custom_call" | custom-call | flops 2883584 | bytes 6690816 | tf_op jit(solution)/shard_map/pallas_call | solution.py:146
  182.2 5.5 %shard_map.135 = (f32[176,256]{1,0:T(8,128)}, f32[176,256]{1,0:T(8,128)}) custom-call(f32[176,256]{1,0:T(8,128)} %get-tuple-element.45.pos_ref, f32[176,256]{1,0:T(8,128)} %get-tuple-element.78.drift_ref, f32[176,32]{1,0:T(8,128)} %slice.159.volt_ref, f32[32,176,256]{2,1,0:T(8,128)} %get-tuple-element.62.table_ref, f32[176,256]{1,0:T(8,128)} %get-tuple-element.63.norm_ref), custom_call_target="tpu_custom_call" | custom-call | flops 2883584 | bytes 6690816 | tf_op jit(solution)/shard_map/pallas_call | solution.py:146
  187.7 5.5 %shard_map.136 = (f32[176,256]{1,0:T(8,128)}, f32[176,256]{1,0:T(8,128)}) custom-call(f32[176,256]{1,0:T(8,128)} %get-tuple-element.50.pos_ref, f32[176,256]{1,0:T(8,128)} %get-tuple-element.77.drift_ref, f32[176,32]{1,0:T(8,128)} %slice.162.volt_ref, f32[32,176,256]{2,1,0:T(8,128)} %get-tuple-element.65.table_ref, f32[176,256]{1,0:T(8,128)} %get-tuple-element.66.norm_ref), custom_call_target="tpu_custom_call" | custom-call | flops 2883584 | bytes 6690816 | tf_op jit(solution)/shard_map/pallas_call | solution.py:146
  193.3 5.5 %shard_map.137 = (f32[176,256]{1,0:T(8,128)}, f32[176,256]{1,0:T(8,128)}) custom-call(f32[176,256]{1,0:T(8,128)} %get-tuple-element.55.pos_ref, f32[176,256]{1,0:T(8,128)} %get-tuple-element.76.drift_ref, f32[176,32]{1,0:T(8,128)} %slice.165.volt_ref, f32[32,176,256]{2,1,0:T(8,128)} %get-tuple-element.68.table_ref, f32[176,256]{1,0:T(8,128)} %get-tuple-element.69.norm_ref), custom_call_target="tpu_custom_call" | custom-call | flops 2883584 | bytes 6690816 | tf_op jit(solution)/shard_map/pallas_call | solution.py:146
  198.8 1.8 pad_maximum_fusion.4
  200.7 1.8 pad_maximum_fusion.3
  (87 shorter events, 17.3 us)
Async XLA Ops:
  0.6 16.6 %copy-start = (f32[704,256]{1,0:T(8,128)S(1)}, f32[704,256]{1,0:T(8,128)}, u32[]{:S(2)}) copy-start(f32[704,256]{1,0:T(8,128)} %param.11) | copy-start | bytes 2162692
  0.7 17.5 %copy-start.11 = (s32[704]{0:T(1024)S(1)}, s32[704]{0:T(1024)}, u32[]{:S(2)}) copy-start(s32[704]{0:T(1024)} %param.13) | copy-start | bytes 8452
  7.3 18.4 %all-to-all-start = ((f32[16,11,128]{2,1,0:T(8,128)}), f32[16,11,128]{2,1,0:T(8,128)S(1)}, u32[]{:S(2)}, u32[]{:S(2)}) async-start(f32[16,11,128]{2,1,0:T(8,128)} %div.48), calls=%async_computation | async-start | bytes 262144 | tf_op jit(solution)/shard_map/all_to_all | solution.py:77
  26.4 13.0 %all-to-all-start.1 = ((f32[16,11,128]{2,1,0:T(8,128)}), f32[16,11,128]{2,1,0:T(8,128)S(1)}, u32[]{:S(2)}, u32[]{:S(2)}) async-start(f32[16,11,128]{2,1,0:T(8,128)} %broadcast_in_dim.6), calls=%async_computation.1 | async-start | bytes 262144 | tf_op jit(solution)/shard_map/all_to_all | solution.py:80
  40.4 23.8 %copy-start.12 = (f32[2]{0:T(128)S(1)}, f32[2]{0:T(128)}, u32[]{:S(2)}) copy-start(f32[2]{0:T(128)} %constant.164.clone) | copy-start | bytes 28
  42.1 13.8 %all-to-all-start.2 = ((f32[16,8,128]{2,1,0:T(8,128)}), f32[16,8,128]{2,1,0:T(8,128)S(1)}, u32[]{:S(2)}, u32[]{:S(2)}) async-start(f32[16,8,128]{2,1,0:T(8,128)} %reshape.708), calls=%async_computation.2 | async-start | bytes 131072 | tf_op jit(solution)/shard_map/all_to_all | solution.py:66
  59.0 14.3 %all-to-all-start.3 = ((f32[16,16,128]{2,1,0:T(8,128)}), f32[16,16,128]{2,1,0:T(8,128)S(1)}, u32[]{:S(2)}, u32[]{:S(2)}) async-start(f32[16,16,128]{2,1,0:T(8,128)} %reshape.711), calls=%async_computation.3 | async-start | bytes 262144 | tf_op jit(solution)/shard_map/all_to_all | solution.py:66
  79.0 11.7 %all-to-all-start.4 = ((f32[16,16,128]{2,1,0:T(8,128)}), f32[16,16,128]{2,1,0:T(8,128)S(1)}, u32[]{:S(2)}, u32[]{:S(2)}) async-start(f32[16,16,128]{2,1,0:T(8,128)} %reshape.714), calls=%async_computation.4 | async-start | bytes 262144 | tf_op jit(solution)/shard_map/all_to_all | solution.py:66
  93.7 19.5 %copy-start.1 = (f32[2,8,8,256]{3,2,1,0:T(8,128)}, f32[2,8,8,256]{3,2,1,0:T(8,128)S(1)}, u32[]{:S(2)}) copy-start(f32[2,8,8,256]{3,2,1,0:T(8,128)S(1)} %fusion.5) | copy-start | bytes 393220
  94.9 18.3 %copy-start.2 = (f32[2,128,2,128,1]{3,1,2,0,4:T(8,128)S(1)}, f32[2,128,2,128,1]{3,1,2,0,4:T(8,128)}, u32[]{:S(2)}) copy-start(f32[2,128,2,128,1]{3,1,2,0,4:T(8,128)} %get-tuple-element.84) | copy-start | bytes 786436
  99.6 13.2 %all-to-all-start.5 = ((f32[16,16,128]{2,1,0:T(8,128)}), f32[16,16,128]{2,1,0:T(8,128)S(1)}, u32[]{:S(2)}, u32[]{:S(2)}) async-start(f32[16,16,128]{2,1,0:T(8,128)} %copy.131), calls=%async_computation.5 | async-start | bytes 262144 | tf_op jit(solution)/shard_map/all_to_all | solution.py:66
  108.8 21.3 %copy-start.4 = (f32[2,128,2,128]{3,1,2,0:T(8,128)S(1)}, f32[2,128,2,128]{3,1,2,0:T(8,128)}, u32[]{:S(2)}) copy-start(f32[2,128,2,128]{3,1,2,0:T(8,128)} %get-tuple-element.83) | copy-start | bytes 786436
  115.9 35.1 %copy-start.3 = (f32[704,256]{1,0:T(8,128)S(1)}, f32[704,256]{1,0:T(8,128)}, u32[]{:S(2)}) copy-start(f32[704,256]{1,0:T(8,128)} %param.12) | copy-start | bytes 2162692
  145.6 14.3 %all-to-all-start.8 = ((f32[16,11,128]{2,1,0:T(8,128)}), f32[16,11,128]{2,1,0:T(8,128)S(1)}, u32[]{:S(2)}, u32[]{:S(2)}) async-start(f32[16,11,128]{2,1,0:T(8,128)} %reshape.725), calls=%async_computation.8 | async-start | bytes 262144 | tf_op jit(solution)/shard_map/all_to_all | solution.py:77
  160.6 13.2 %all-to-all-start.9 = ((f32[16,11,128]{2,1,0:T(8,128)}), f32[16,11,128]{2,1,0:T(8,128)S(1)}, u32[]{:S(2)}, u32[]{:S(2)}) async-start(f32[16,11,128]{2,1,0:T(8,128)} %broadcast_in_dim.7), calls=%async_computation.9 | async-start | bytes 262144 | tf_op jit(solution)/shard_map/all_to_all | solution.py:80
  187.7 11.1 %copy-start.6 = (f32[176,256]{1,0:T(8,128)S(1)}, f32[176,256]{1,0:T(8,128)}, u32[]{:S(2)}) copy-start(f32[176,256]{1,0:T(8,128)} %get-tuple-element.71) | copy-start | bytes 540676
  187.7 11.1 %copy-start.8 = (f32[176,256]{1,0:T(8,128)S(1)}, f32[176,256]{1,0:T(8,128)}, u32[]{:S(2)}) copy-start(f32[176,256]{1,0:T(8,128)} %get-tuple-element.72) | copy-start | bytes 540676
  187.7 13.0 %copy-start.5 = (f32[176,256]{1,0:T(8,128)S(1)}, f32[176,256]{1,0:T(8,128)}, u32[]{:S(2)}) copy-start(f32[176,256]{1,0:T(8,128)} %get-tuple-element.61) | copy-start | bytes 540676
  187.7 13.0 %copy-start.7 = (f32[176,256]{1,0:T(8,128)S(1)}, f32[176,256]{1,0:T(8,128)}, u32[]{:S(2)}) copy-start(f32[176,256]{1,0:T(8,128)} %get-tuple-element.64) | copy-start | bytes 540676
  193.3 5.6 %copy-start.10 = (f32[176,256]{1,0:T(8,128)S(1)}, f32[176,256]{1,0:T(8,128)}, u32[]{:S(2)}) copy-start(f32[176,256]{1,0:T(8,128)} %get-tuple-element.73) | copy-start | bytes 540676
  193.3 7.4 %copy-start.9 = (f32[176,256]{1,0:T(8,128)S(1)}, f32[176,256]{1,0:T(8,128)}, u32[]{:S(2)}) copy-start(f32[176,256]{1,0:T(8,128)} %get-tuple-element.67) | copy-start | bytes 540676

commit v5 on v2

--- a/solution.py
+++ b/solution.py
@@ -18,6 +18,7 @@
 
 highest = lax.Precision.HIGHEST
 two_pi = 2.0 * math.pi
+HALF_LOG2E = -0.5 / math.log(2.0)
 
 
 def kernel_table(places):
@@ -93,7 +94,7 @@
         norm = jnp.zeros_like(place)
         for j in range(BINS):
             offset = place - (j + 0.5)
-            table = jnp.exp(-0.5 * offset * offset)
+            table = jnp.exp2(offset * offset * HALF_LOG2E)
             weighted = weighted + table * volts[:, j : j + 1]
             norm = norm + table
         energy = drift_ref[rows, :] - weighted / norm

time: 179 us -> 179 us (level)
  no operation moved by 1% of the time
where the time goes in v5:
time: 179 us; the launch traced here: 178 us
  waiting for transfers between devices  48.2 us (27%)
  starting transfers between devices  37.9 us (21%)
  blocking collectives  35.7 us (20%)
  local copies, waits for them, and re-layouts  17.2 us (10%)
  other arithmetic  16.7 us (9%)
  Pallas kernels  13.1 us (7%)
  matrix products  8.15 us (5%)
    all_to_all x4, waiting for transfers between devices, exchange(): lax.all_to_all(sent, axis_name, 0, 0, tiled=True).reshape((count,) + piece)  30 us
    all_to_all x2, blocking collectives, exchange(): lax.all_to_all(sent, axis_name, 0, 0, tiled=True).reshape((count,) + piece)  22.7 us
    all_to_all x4, starting transfers between devices, exchange(): lax.all_to_all(sent, axis_name, 0, 0, tiled=True).reshape((count,) + piece)  18.6 us
    pallas_call x1, Pallas kernels, kick_call(): pl.pallas_call(kick_kernel, grid=(bunches // KICK_ROWS,), in_specs=[wide,...  13.1 us
    all_to_all x1, blocking collectives, dom_sum(): lax.all_to_all(rows.reshape(domains, -1, 128), 'dom', 0, 0, tiled=True)  13 us
    all_to_all x2, waiting for transfers between devices, dom_sum(): return lax.all_to_all(spread, 'dom', 0, 0, tiled=True).reshape(rows.shape)  11.7 us
    all_to_all x1, starting transfers between devices, dom_sum(): lax.all_to_all(rows.reshape(domains, -1, 128), 'dom', 0, 0, tiled=True)  9.94 us
    all_to_all x2, starting transfers between devices, dom_sum(): return lax.all_to_all(spread, 'dom', 0, 0, tiled=True).reshape(rows.shape)  9.34 us
  transfers between devices with their start and end apart: 7, of which 7 were waited for; matrix products, arithmetic and copies ran while one was open for 6% of the time, Pallas kernels for 0%

profile of v5, /device:TPU:2, one launch (start us, length us, event | category | flops | bytes accessed | tf_op | source)
XLA Modules:
  0.0 178.2 jit_solution(2031190692598042001)
XLA Ops:
  0.7 5.7 %fusion.1 = f32[704,32]{1,0:T(8,128)S(1)} fusion(f32[32]{0:T(128)S(1)} %iota_add_fusion.3, f32[704,256]{1,0:T(8,128)} %pos_ref.1), kind=kLoop, calls=%fused_computation.2 | loop fusion | flops 23046144 | bytes 811136 | tf_op jit(solution)/shard_map/reduce_sum | solution.py:142
  6.4 0.8 div.48
  7.2 9.9 %all-to-all-start = ((f32[16,11,128]{2,1,0:T(8,128)}), f32[16,11,128]{2,1,0:T(8,128)S(1)}, u32[]{:S(2)}, u32[]{:S(2)}) async-start(f32[16,11,128]{2,1,0:T(8,128)} %div.48), calls=%async_computation | async-start | bytes 262144 | tf_op jit(solution)/shard_map/all_to_all | solution.py:78
  17.2 0.5 iota_add_fusion.2
  18.0 1.0 fusion.32
  19.0 6.6 %all-to-all-done = f32[16,11,128]{2,1,0:T(8,128)S(1)} async-done(((f32[16,11,128]{2,1,0:T(8,128)}), f32[16,11,128]{2,1,0:T(8,128)S(1)}, u32[]{:S(2)}, u32[]{:S(2)}) %all-to-all-start) | async-done | bytes 90144 | tf_op jit(solution)/shard_map/all_to_all | solution.py:78
  25.6 0.7 broadcast_in_dim.6
  26.3 4.6 %all-to-all-start.1 = ((f32[16,11,128]{2,1,0:T(8,128)}), f32[16,11,128]{2,1,0:T(8,128)S(1)}, u32[]{:S(2)}, u32[]{:S(2)}) async-start(f32[16,11,128]{2,1,0:T(8,128)} %broadcast_in_dim.6), calls=%async_computation.1 | async-start | bytes 262144 | tf_op jit(solution)/shard_map/all_to_all | solution.py:81
  31.1 1.8 fusion.30
  32.9 6.4 %all-to-all-done.1 = f32[16,11,128]{2,1,0:T(8,128)S(1)} async-done(((f32[16,11,128]{2,1,0:T(8,128)}), f32[16,11,128]{2,1,0:T(8,128)S(1)}, u32[]{:S(2)}, u32[]{:S(2)}) %all-to-all-start.1) | async-done | bytes 90144 | tf_op jit(solution)/shard_map/all_to_all | solution.py:81
  39.5 0.9 fusion.3
  40.5 0.4 copy.93
  40.9 1.1 reshape.706
  42.0 6.1 %all-to-all-start.2 = ((f32[16,8,128]{2,1,0:T(8,128)}), f32[16,8,128]{2,1,0:T(8,128)S(1)}, u32[]{:S(2)}, u32[]{:S(2)}) async-start(f32[16,8,128]{2,1,0:T(8,128)} %reshape.706), calls=%async_computation.2 | async-start | bytes 131072 | tf_op jit(solution)/shard_map/all_to_all | solution.py:67
  48.4 7.4 %all-to-all-done.2 = f32[16,8,128]{2,1,0:T(8,128)S(1)} async-done(((f32[16,8,128]{2,1,0:T(8,128)}), f32[16,8,128]{2,1,0:T(8,128)S(1)}, u32[]{:S(2)}, u32[]{:S(2)}) %all-to-all-start.2) | async-done | bytes 65568 | tf_op jit(solution)/shard_map/all_to_all | solution.py:67
  56.0 0.6 copy.95
  57.4 0.5 copy.97
  57.9 1.0 reshape.709
  58.9 5.5 %all-to-all-start.3 = ((f32[16,16,128]{2,1,0:T(8,128)}), f32[16,16,128]{2,1,0:T(8,128)S(1)}, u32[]{:S(2)}, u32[]{:S(2)}) async-start(f32[16,16,128]{2,1,0:T(8,128)} %reshape.709), calls=%async_computation.3 | async-start | bytes 262144 | tf_op jit(solution)/shard_map/all_to_all | solution.py:67
  64.4 0.9 multiply_multiply_fusion.1
  65.3 8.1 %all-to-all-done.3 = f32[16,16,128]{2,1,0:T(8,128)S(1)} async-done(((f32[16,16,128]{2,1,0:T(8,128)}), f32[16,16,128]{2,1,0:T(8,128)S(1)}, u32[]{:S(2)}, u32[]{:S(2)}) %all-to-all-start.3) | async-done | bytes 131104 | tf_op jit(solution)/shard_map/all_to_all | solution.py:67
  74.7 1.8 %copy.101 = f32[128,2,16,8]{3,2,1,0:T(8,128)S(1)} copy(f32[128,2,16,8]{0,2,3,1:T(8,128)S(1)} %maximum_bitcast_fusion.4) | data formatting | bytes 262144 | tf_op jit(solution)/shard_map/transpose | solution.py:63
  76.6 1.6 reshape.712
  78.2 3.5 %all-to-all-start.4 = ((f32[16,16,128]{2,1,0:T(8,128)}), f32[16,16,128]{2,1,0:T(8,128)S(1)}, u32[]{:S(2)}, u32[]{:S(2)}) async-start(f32[16,16,128]{2,1,0:T(8,128)} %reshape.712), calls=%async_computation.4 | async-start | bytes 262144 | tf_op jit(solution)/shard_map/all_to_all | solution.py:67
  81.7 1.2 maximum_bitcast_fusion
  82.9 0.5 iota_multiply_fusion
  83.4 6.5 %all-to-all-done.4 = f32[16,16,128]{2,1,0:T(8,128)S(1)} async-done(((f32[16,16,128]{2,1,0:T(8,128)}), f32[16,16,128]{2,1,0:T(8,128)S(1)}, u32[]{:S(2)}, u32[]{:S(2)}) %all-to-all-start.4) | async-done | bytes 131104 | tf_op jit(solution)/shard_map/all_to_all | solution.py:67
  90.3 0.4 copy.103
  90.7 0.4 reshape.731
  91.1 0.8 fusion.5
  92.1 0.9 convolution_bitcast_fusion.2
  93.4 1.1 copy.105
  94.5 3.5 %all-to-all-start.5 = ((f32[16,16,128]{2,1,0:T(8,128)}), f32[16,16,128]{2,1,0:T(8,128)S(1)}, u32[]{:S(2)}, u32[]{:S(2)}) async-start(f32[16,16,128]{2,1,0:T(8,128)} %copy.105), calls=%async_computation.5 | async-start | bytes 262144 | tf_op jit(solution)/shard_map/all_to_all | solution.py:67
  98.1 8.1 %all-to-all-done.5 = f32[16,16,128]{2,1,0:T(8,128)S(1)} async-done(((f32[16,16,128]{2,1,0:T(8,128)}), f32[16,16,128]{2,1,0:T(8,128)S(1)}, u32[]{:S(2)}, u32[]{:S(2)}) %all-to-all-start.5) | async-done | bytes 131104 | tf_op jit(solution)/shard_map/all_to_all | solution.py:67
  106.5 1.8 convolution_bitcast_fusion.1
  108.3 0.4 multiply_subtract_fusion.1
  108.7 0.5 copy.110
  109.5 12.4 %all_to_all.50 = f32[16,16,128]{2,1,0:T(8,128)S(1)} all-to-all(f32[16,16,128]{2,1,0:T(8,128)S(1)} %reshape.718), channel_id=1, replica_groups=mesh['grp'=16,'dom'=16] {'dom'}, dimensions={0} | all-to-all | bytes 262144 | tf_op jit(solution)/shard_map/all_to_all | solution.py:67
  122.6 1.8 fusion.6
  124.8 10.2 %all_to_all.51 = f32[16,8,128]{2,1,0:T(8,128)S(1)} all-to-all(f32[16,8,128]{2,1,0:T(8,128)S(1)} %reshape.721), channel_id=1, replica_groups=mesh['grp'=16,'dom'=16] {'grp'}, dimensions={0} | all-to-all | bytes 131072 | tf_op jit(solution)/shard_map/all_to_all | solution.py:67
  135.7 1.4 fusion.2
  137.3 13.0 %all_to_all.52 = f32[16,11,128]{2,1,0:T(8,128)S(1)} all-to-all(f32[16,11,128]{2,1,0:T(8,128)S(1)} %reshape.723), channel_id=1, replica_groups=mesh['grp'=16,'dom'=16] {'dom'}, dimensions={0} | all-to-all | bytes 180224 | tf_op jit(solution)/shard_map/all_to_all | solution.py:78
  150.3 0.7 broadcast_in_dim.7
  151.0 4.8 %all-to-all-start.9 = ((f32[16,11,128]{2,1,0:T(8,128)}), f32[16,11,128]{2,1,0:T(8,128)S(1)}, u32[]{:S(2)}, u32[]{:S(2)}) async-start(f32[16,11,128]{2,1,0:T(8,128)} %broadcast_in_dim.7), calls=%async_computation.9 | async-start | bytes 262144 | tf_op jit(solution)/shard_map/all_to_all | solution.py:81
  155.8 3.2 %multiply_subtract_fusion.drift_ref = f32[704,256]{1,0:T(8,128)} fusion(f32[704,256]{1,0:T(8,128)S(1)} %copy-done.4, f32[704,256]{1,0:T(8,128)S(1)} %copy-done.5), kind=kLoop, calls=%fused_computation.25 | loop fusion | flops 720896 | bytes 2162688 | tf_op jit(solution)/shard_map/sub | solution.py:216
  159.0 5.3 %all-to-all-done.9 = f32[16,11,128]{2,1,0:T(8,128)S(1)} async-done(((f32[16,11,128]{2,1,0:T(8,128)}), f32[16,11,128]{2,1,0:T(8,128)S(1)}, u32[]{:S(2)}, u32[]{:S(2)}) %all-to-all-start.9) | async-done | bytes 90144 | tf_op jit(solution)/shard_map/all_to_all | solution.py:81
  164.2 0.9 reshape.724.volt_ref
  165.1 13.1 %shard_map.130 = (f32[704,256]{1,0:T(8,128)}, f32[704,256]{1,0:T(8,128)}) custom-call(f32[704,256]{1,0:T(8,128)} %pos_ref.1, f32[704,256]{1,0:T(8,128)} %multiply_subtract_fusion.drift_ref, f32[704,32]{1,0:T(8,128)} %reshape.724.volt_ref), custom_call_target="tpu_custom_call" | custom-call | flops 69206016 | bytes 2973696 | tf_op jit(solution)/shard_map/pallas_call | solution.py:113
  (76 shorter events, 7.1 us)
Async XLA Ops:
  0.6 17.0 %copy-start.9 = (s32[704]{0:T(1024)S(1)}, s32[704]{0:T(1024)}, u32[]{:S(2)}) copy-start(s32[704]{0:T(1024)} %param.13) | copy-start | bytes 8452
  7.2 18.4 %all-to-all-start = ((f32[16,11,128]{2,1,0:T(8,128)}), f32[16,11,128]{2,1,0:T(8,128)S(1)}, u32[]{:S(2)}, u32[]{:S(2)}) async-start(f32[16,11,128]{2,1,0:T(8,128)} %div.48), calls=%async_computation | async-start | bytes 262144 | tf_op jit(solution)/shard_map/all_to_all | solution.py:78
  17.2 24.8 %copy-start.7 = (s32[16]{0:T(128)}, s32[16]{0:T(128)S(1)}, u32[]{:S(2)}) copy-start(s32[16]{0:T(128)S(1)} %iota_add_fusion.1) | copy-start | bytes 196
  17.7 24.3 %copy-start.10 = (s32[704]{0:T(1024)}, s32[704]{0:T(1024)S(1)}, u32[]{:S(2)}) copy-start(s32[704]{0:T(1024)S(1)} %fusion.74) | copy-start | bytes 8452
  26.3 13.0 %all-to-all-start.1 = ((f32[16,11,128]{2,1,0:T(8,128)}), f32[16,11,128]{2,1,0:T(8,128)S(1)}, u32[]{:S(2)}, u32[]{:S(2)}) async-start(f32[16,11,128]{2,1,0:T(8,128)} %broadcast_in_dim.6), calls=%async_computation.1 | async-start | bytes 262144 | tf_op jit(solution)/shard_map/all_to_all | solution.py:81
  42.0 13.8 %all-to-all-start.2 = ((f32[16,8,128]{2,1,0:T(8,128)}), f32[16,8,128]{2,1,0:T(8,128)S(1)}, u32[]{:S(2)}, u32[]{:S(2)}) async-start(f32[16,8,128]{2,1,0:T(8,128)} %reshape.706), calls=%async_computation.2 | async-start | bytes 131072 | tf_op jit(solution)/shard_map/all_to_all | solution.py:67
  56.8 7.6 %copy-start.12 = (f32[2]{0:T(128)S(1)}, f32[2]{0:T(128)}, u32[]{:S(2)}) copy-start(f32[2]{0:T(128)} %constant.164.clone) | copy-start | bytes 28
  58.9 14.4 %all-to-all-start.3 = ((f32[16,16,128]{2,1,0:T(8,128)}), f32[16,16,128]{2,1,0:T(8,128)S(1)}, u32[]{:S(2)}, u32[]{:S(2)}) async-start(f32[16,16,128]{2,1,0:T(8,128)} %reshape.709), calls=%async_computation.3 | async-start | bytes 262144 | tf_op jit(solution)/shard_map/all_to_all | solution.py:67
  78.2 11.7 %all-to-all-start.4 = ((f32[16,16,128]{2,1,0:T(8,128)}), f32[16,16,128]{2,1,0:T(8,128)S(1)}, u32[]{:S(2)}, u32[]{:S(2)}) async-start(f32[16,16,128]{2,1,0:T(8,128)} %reshape.712), calls=%async_computation.4 | async-start | bytes 262144 | tf_op jit(solution)/shard_map/all_to_all | solution.py:67
  90.2 1.7 copy-start
  90.6 1.3 copy-start.2
  90.7 1.4 copy-start.13
  91.9 1.5 copy-start.1
  92.1 5.9 %copy-start.8 = (s32[16]{0:T(128)S(1)}, s32[16]{0:T(128)}, u32[]{:S(2)}) copy-start(s32[16]{0:T(128)} %copy-done.7) | copy-start | bytes 196
  92.1 5.9 %copy-start.15 = (s32[128]{0:T(128)S(1)}, s32[128]{0:T(128)}, u32[]{:S(2)}) copy-start(s32[128]{0:T(128)} %iota_multiply_fusion) | copy-start | bytes 1540
  93.0 13.5 %copy-start.3 = (f32[2,128,2,128,1]{3,1,2,0,4:T(8,128)S(1)}, f32[2,128,2,128,1]{3,1,2,0,4:T(8,128)}, u32[]{:S(2)}) copy-start(f32[2,128,2,128,1]{3,1,2,0,4:T(8,128)} %get-tuple-element.8) | copy-start | bytes 786436
  93.4 14.9 %copy-start.14 = (s32[8]{0:T(128)S(1)}, s32[8]{0:T(128)}, u32[]{:S(2)}) copy-start(s32[8]{0:T(128)} %get-tuple-element.30) | copy-start | bytes 100
  94.5 11.7 %all-to-all-start.5 = ((f32[16,16,128]{2,1,0:T(8,128)}), f32[16,16,128]{2,1,0:T(8,128)S(1)}, u32[]{:S(2)}, u32[]{:S(2)}) async-start(f32[16,16,128]{2,1,0:T(8,128)} %copy.105), calls=%async_computation.5 | async-start | bytes 262144 | tf_op jit(solution)/shard_map/all_to_all | solution.py:67
  109.2 13.4 %copy-start.6 = (f32[2,128,2,128]{3,1,2,0:T(8,128)S(1)}, f32[2,128,2,128]{3,1,2,0:T(8,128)}, u32[]{:S(2)}) copy-start(f32[2,128,2,128]{3,1,2,0:T(8,128)} %get-tuple-element.7) | copy-start | bytes 786436
  124.4 11.3 %copy-start.11 = (s32[704]{0:T(1024)S(1)}, s32[704]{0:T(1024)}, u32[]{:S(2)}) copy-start(s32[704]{0:T(1024)} %copy-done.10) | copy-start | bytes 8452
  135.1 20.7 %copy-start.4 = (f32[704,256]{1,0:T(8,128)S(1)}, f32[704,256]{1,0:T(8,128)}, u32[]{:S(2)}) copy-start(f32[704,256]{1,0:T(8,128)} %param.12) | copy-start | bytes 2162692
  135.1 20.7 %copy-start.5 = (f32[704,256]{1,0:T(8,128)S(1)}, f32[704,256]{1,0:T(8,128)}, u32[]{:S(2)}) copy-start(f32[704,256]{1,0:T(8,128)} %pos_ref.1) | copy-start | bytes 2162692
  151.0 13.2 %all-to-all-start.9 = ((f32[16,11,128]{2,1,0:T(8,128)}), f32[16,11,128]{2,1,0:T(8,128)S(1)}, u32[]{:S(2)}, u32[]{:S(2)}) async-start(f32[16,11,128]{2,1,0:T(8,128)} %broadcast_in_dim.7), calls=%async_computation.9 | async-start | bytes 262144 | tf_op jit(solution)/shard_map/all_to_all | solution.py:81

commit v6 on v5

--- a/solution.py
+++ b/solution.py
@@ -81,8 +81,8 @@
     return lax.all_to_all(spread, "dom", 0, 0, tiled=True).reshape(rows.shape)
 
 
-KICK_ROWS = 64
-SUB_ROWS = 8
+KICK_ROWS = 352
+SUB_ROWS = 32
 
 
 def kick_kernel(pos_ref, drift_ref, volt_ref, pos_out, en_out):

time: 179 us -> 174 us (0.972)
  Pallas kernels: 13.1 us -> 7.7 us
    pallas_call x1, Pallas kernels: 13.1 us -> 7.7 us  [kick_call(): pl.pallas_call(kick_kernel, grid=(bunches // KICK_ROWS,), in_specs=[wide,...]
where the time goes in v6:
time: 174 us; the launch traced here: 173 us
  waiting for transfers between devices  48.2 us (28%)
  starting transfers between devices  37.9 us (22%)
  blocking collectives  35.7 us (21%)
  local copies, waits for them, and re-layouts  17.2 us (10%)
  other arithmetic  16.7 us (10%)
  matrix products  8.15 us (5%)
  Pallas kernels  7.7 us (4%)
    all_to_all x4, waiting for transfers between devices, exchange(): lax.all_to_all(sent, axis_name, 0, 0, tiled=True).reshape((count,) + piece)  30 us
    all_to_all x2, blocking collectives, exchange(): lax.all_to_all(sent, axis_name, 0, 0, tiled=True).reshape((count,) + piece)  22.7 us
    all_to_all x4, starting transfers between devices, exchange(): lax.all_to_all(sent, axis_name, 0, 0, tiled=True).reshape((count,) + piece)  18.6 us
    all_to_all x1, blocking collectives, dom_sum(): lax.all_to_all(rows.reshape(domains, -1, 128), 'dom', 0, 0, tiled=True)  13 us
    all_to_all x2, waiting for transfers between devices, dom_sum(): return lax.all_to_all(spread, 'dom', 0, 0, tiled=True).reshape(rows.shape)  11.7 us
    all_to_all x1, starting transfers between devices, dom_sum(): lax.all_to_all(rows.reshape(domains, -1, 128), 'dom', 0, 0, tiled=True)  9.94 us
    all_to_all x2, starting transfers between devices, dom_sum(): return lax.all_to_all(spread, 'dom', 0, 0, tiled=True).reshape(rows.shape)  9.34 us
    dot_general x8, matrix products, contract(): return jnp.einsum(pattern, operand, matrix, precision=highest)  8.15 us
  transfers between devices with their start and end apart: 7, of which 7 were waited for; matrix products, arithmetic and copies ran while one was open for 6% of the time, Pallas kernels for 0%

profile of v6, /device:TPU:2, one launch (start us, length us, event | category | flops | bytes accessed | tf_op | source)
XLA Modules:
  0.0 172.8 jit_solution(2382923588638690451)
XLA Ops:
  0.7 5.7 %fusion.1 = f32[704,32]{1,0:T(8,128)S(1)} fusion(f32[32]{0:T(128)S(1)} %iota_add_fusion.3, f32[704,256]{1,0:T(8,128)} %pos_ref.1), kind=kLoop, calls=%fused_computation.2 | loop fusion | flops 23046144 | bytes 811136 | tf_op jit(solution)/shard_map/reduce_sum | solution.py:142
  6.4 0.8 div.48
  7.2 9.9 %all-to-all-start = ((f32[16,11,128]{2,1,0:T(8,128)}), f32[16,11,128]{2,1,0:T(8,128)S(1)}, u32[]{:S(2)}, u32[]{:S(2)}) async-start(f32[16,11,128]{2,1,0:T(8,128)} %div.48), calls=%async_computation | async-start | bytes 262144 | tf_op jit(solution)/shard_map/all_to_all | solution.py:78
  17.2 0.5 iota_add_fusion.2
  18.0 1.0 fusion.32
  19.0 6.6 %all-to-all-done = f32[16,11,128]{2,1,0:T(8,128)S(1)} async-done(((f32[16,11,128]{2,1,0:T(8,128)}), f32[16,11,128]{2,1,0:T(8,128)S(1)}, u32[]{:S(2)}, u32[]{:S(2)}) %all-to-all-start) | async-done | bytes 90144 | tf_op jit(solution)/shard_map/all_to_all | solution.py:78
  25.6 0.7 broadcast_in_dim.6
  26.3 4.6 %all-to-all-start.1 = ((f32[16,11,128]{2,1,0:T(8,128)}), f32[16,11,128]{2,1,0:T(8,128)S(1)}, u32[]{:S(2)}, u32[]{:S(2)}) async-start(f32[16,11,128]{2,1,0:T(8,128)} %broadcast_in_dim.6), calls=%async_computation.1 | async-start | bytes 262144 | tf_op jit(solution)/shard_map/all_to_all | solution.py:81
  31.1 1.8 %fusion.30 = (f32[256,1,256]{2,0,1:T(8,128)}, f32[256,1,256]{2,0,1:T(8,128)}) fusion(), kind=kLoop, calls=%fused_computation.58 | loop fusion | flops 917504 | bytes 524288 | tf_op jit(solution)/shard_map/sin | solution.py:34
  32.9 6.4 %all-to-all-done.1 = f32[16,11,128]{2,1,0:T(8,128)S(1)} async-done(((f32[16,11,128]{2,1,0:T(8,128)}), f32[16,11,128]{2,1,0:T(8,128)S(1)}, u32[]{:S(2)}, u32[]{:S(2)}) %all-to-all-start.1) | async-done | bytes 90144 | tf_op jit(solution)/shard_map/all_to_all | solution.py:81
  39.5 0.9 fusion.3
  40.5 0.4 copy.93
  40.9 1.1 reshape.706
  42.0 6.1 %all-to-all-start.2 = ((f32[16,8,128]{2,1,0:T(8,128)}), f32[16,8,128]{2,1,0:T(8,128)S(1)}, u32[]{:S(2)}, u32[]{:S(2)}) async-start(f32[16,8,128]{2,1,0:T(8,128)} %reshape.706), calls=%async_computation.2 | async-start | bytes 131072 | tf_op jit(solution)/shard_map/all_to_all | solution.py:67
  48.4 7.4 %all-to-all-done.2 = f32[16,8,128]{2,1,0:T(8,128)S(1)} async-done(((f32[16,8,128]{2,1,0:T(8,128)}), f32[16,8,128]{2,1,0:T(8,128)S(1)}, u32[]{:S(2)}, u32[]{:S(2)}) %all-to-all-start.2) | async-done | bytes 65568 | tf_op jit(solution)/shard_map/all_to_all | solution.py:67
  56.0 0.6 copy.95
  57.4 0.5 copy.97
  57.9 1.0 reshape.709
  58.9 5.5 %all-to-all-start.3 = ((f32[16,16,128]{2,1,0:T(8,128)}), f32[16,16,128]{2,1,0:T(8,128)S(1)}, u32[]{:S(2)}, u32[]{:S(2)}) async-start(f32[16,16,128]{2,1,0:T(8,128)} %reshape.709), calls=%async_computation.3 | async-start | bytes 262144 | tf_op jit(solution)/shard_map/all_to_all | solution.py:67
  64.4 0.9 multiply_multiply_fusion.1
  65.3 8.1 %all-to-all-done.3 = f32[16,16,128]{2,1,0:T(8,128)S(1)} async-done(((f32[16,16,128]{2,1,0:T(8,128)}), f32[16,16,128]{2,1,0:T(8,128)S(1)}, u32[]{:S(2)}, u32[]{:S(2)}) %all-to-all-start.3) | async-done | bytes 131104 | tf_op jit(solution)/shard_map/all_to_all | solution.py:67
  74.7 1.8 %copy.101 = f32[128,2,16,8]{3,2,1,0:T(8,128)S(1)} copy(f32[128,2,16,8]{0,2,3,1:T(8,128)S(1)} %maximum_bitcast_fusion.4) | data formatting | bytes 262144 | tf_op jit(solution)/shard_map/transpose | solution.py:63
  76.6 1.6 reshape.712
  78.2 3.5 %all-to-all-start.4 = ((f32[16,16,128]{2,1,0:T(8,128)}), f32[16,16,128]{2,1,0:T(8,128)S(1)}, u32[]{:S(2)}, u32[]{:S(2)}) async-start(f32[16,16,128]{2,1,0:T(8,128)} %reshape.712), calls=%async_computation.4 | async-start | bytes 262144 | tf_op jit(solution)/shard_map/all_to_all | solution.py:67
  81.7 1.2 maximum_bitcast_fusion
  82.9 0.5 iota_multiply_fusion
  83.4 6.5 %all-to-all-done.4 = f32[16,16,128]{2,1,0:T(8,128)S(1)} async-done(((f32[16,16,128]{2,1,0:T(8,128)}), f32[16,16,128]{2,1,0:T(8,128)S(1)}, u32[]{:S(2)}, u32[]{:S(2)}) %all-to-all-start.4) | async-done | bytes 131104 | tf_op jit(solution)/shard_map/all_to_all | solution.py:67
  90.3 0.4 copy.103
  90.7 0.4 reshape.731
  91.1 0.8 fusion.5
  92.1 0.9 convolution_bitcast_fusion.2
  93.4 1.1 copy.105
  94.5 3.5 %all-to-all-start.5 = ((f32[16,16,128]{2,1,0:T(8,128)}), f32[16,16,128]{2,1,0:T(8,128)S(1)}, u32[]{:S(2)}, u32[]{:S(2)}) async-start(f32[16,16,128]{2,1,0:T(8,128)} %copy.105), calls=%async_computation.5 | async-start | bytes 262144 | tf_op jit(solution)/shard_map/all_to_all | solution.py:67
  98.1 8.1 %all-to-all-done.5 = f32[16,16,128]{2,1,0:T(8,128)S(1)} async-done(((f32[16,16,128]{2,1,0:T(8,128)}), f32[16,16,128]{2,1,0:T(8,128)S(1)}, u32[]{:S(2)}, u32[]{:S(2)}) %all-to-all-start.5) | async-done | bytes 131104 | tf_op jit(solution)/shard_map/all_to_all | solution.py:67
  106.5 1.8 %convolution_bitcast_fusion.1 = f32[2,8,128,16]{2,3,1,0:T(8,128)S(1)} fusion(f32[2,128,2,128,1]{3,1,2,0,4:T(8,128)S(1)} %copy-done.3, f32[2,8,16,8,16]{4,3,1,0,2:T(8,128)S(1)} %bitcast.171), kind=kOutput, calls=%fused_computation.7 | convolution fusion | flops 100663296 | bytes 524288 | tf_op jit(solution)/shard_map/iakb,ikon->oanb/dot_general | solution.py:43
  108.3 0.4 multiply_subtract_fusion.1
  108.7 0.5 copy.110
  109.5 12.4 %all_to_all.50 = f32[16,16,128]{2,1,0:T(8,128)S(1)} all-to-all(f32[16,16,128]{2,1,0:T(8,128)S(1)} %reshape.718), channel_id=1, replica_groups=mesh['grp'=16,'dom'=16] {'dom'}, dimensions={0} | all-to-all | bytes 262144 | tf_op jit(solution)/shard_map/all_to_all | solution.py:67
  122.6 1.8 %fusion.6 = f32[128,8,16]{0,2,1:T(8,128)S(1)} fusion(f32[2,128,8,16]{3,2,1,0:T(8,128)S(1)} %bitcast.170, f32[2,128,2,128]{3,1,2,0:T(8,128)S(1)} %copy-done.6), kind=kOutput, calls=%fused_computation.14 | convolution fusion | flops 50348032 | bytes 1245184 | tf_op jit(solution)/shard_map/ikab,ikn->nab/dot_general | solution.py:43
  124.8 10.2 %all_to_all.51 = f32[16,8,128]{2,1,0:T(8,128)S(1)} all-to-all(f32[16,8,128]{2,1,0:T(8,128)S(1)} %reshape.721), channel_id=1, replica_groups=mesh['grp'=16,'dom'=16] {'grp'}, dimensions={0} | all-to-all | bytes 131072 | tf_op jit(solution)/shard_map/all_to_all | solution.py:67
  135.7 1.4 fusion.2
  137.3 13.0 %all_to_all.52 = f32[16,11,128]{2,1,0:T(8,128)S(1)} all-to-all(f32[16,11,128]{2,1,0:T(8,128)S(1)} %reshape.723), channel_id=1, replica_groups=mesh['grp'=16,'dom'=16] {'dom'}, dimensions={0} | all-to-all | bytes 180224 | tf_op jit(solution)/shard_map/all_to_all | solution.py:78
  150.3 0.7 broadcast_in_dim.7
  151.0 4.8 %all-to-all-start.9 = ((f32[16,11,128]{2,1,0:T(8,128)}), f32[16,11,128]{2,1,0:T(8,128)S(1)}, u32[]{:S(2)}, u32[]{:S(2)}) async-start(f32[16,11,128]{2,1,0:T(8,128)} %broadcast_in_dim.7), calls=%async_computation.9 | async-start | bytes 262144 | tf_op jit(solution)/shard_map/all_to_all | solution.py:81
  155.8 3.2 %multiply_subtract_fusion.drift_ref = f32[704,256]{1,0:T(8,128)} fusion(f32[704,256]{1,0:T(8,128)S(1)} %copy-done.4, f32[704,256]{1,0:T(8,128)S(1)} %copy-done.5), kind=kLoop, calls=%fused_computation.25 | loop fusion | flops 720896 | bytes 2162688 | tf_op jit(solution)/shard_map/sub | solution.py:216
  159.0 5.3 %all-to-all-done.9 = f32[16,11,128]{2,1,0:T(8,128)S(1)} async-done(((f32[16,11,128]{2,1,0:T(8,128)}), f32[16,11,128]{2,1,0:T(8,128)S(1)}, u32[]{:S(2)}, u32[]{:S(2)}) %all-to-all-start.9) | async-done | bytes 90144 | tf_op jit(solution)/shard_map/all_to_all | solution.py:81
  164.2 0.9 reshape.724.volt_ref
  165.1 7.7 %shard_map.130 = (f32[704,256]{1,0:T(8,128)}, f32[704,256]{1,0:T(8,128)}) custom-call(f32[704,256]{1,0:T(8,128)} %pos_ref.1, f32[704,256]{1,0:T(8,128)} %multiply_subtract_fusion.drift_ref, f32[704,32]{1,0:T(8,128)} %reshape.724.volt_ref), custom_call_target="tpu_custom_call" | custom-call | flops 69206016 | bytes 2973696 | tf_op jit(solution)/shard_map/pallas_call | solution.py:113
  (76 shorter events, 7.1 us)
Async XLA Ops:
  0.6 17.0 %copy-start.9 = (s32[704]{0:T(1024)S(1)}, s32[704]{0:T(1024)}, u32[]{:S(2)}) copy-start(s32[704]{0:T(1024)} %param.13) | copy-start | bytes 8452
  7.2 18.4 %all-to-all-start = ((f32[16,11,128]{2,1,0:T(8,128)}), f32[16,11,128]{2,1,0:T(8,128)S(1)}, u32[]{:S(2)}, u32[]{:S(2)}) async-start(f32[16,11,128]{2,1,0:T(8,128)} %div.48), calls=%async_computation | async-start | bytes 262144 | tf_op jit(solution)/shard_map/all_to_all | solution.py:78
  17.2 24.8 %copy-start.7 = (s32[16]{0:T(128)}, s32[16]{0:T(128)S(1)}, u32[]{:S(2)}) copy-start(s32[16]{0:T(128)S(1)} %iota_add_fusion.1) | copy-start | bytes 196
  17.7 24.3 %copy-start.10 = (s32[704]{0:T(1024)}, s32[704]{0:T(1024)S(1)}, u32[]{:S(2)}) copy-start(s32[704]{0:T(1024)S(1)} %fusion.74) | copy-start | bytes 8452
  26.3 13.0 %all-to-all-start.1 = ((f32[16,11,128]{2,1,0:T(8,128)}), f32[16,11,128]{2,1,0:T(8,128)S(1)}, u32[]{:S(2)}, u32[]{:S(2)}) async-start(f32[16,11,128]{2,1,0:T(8,128)} %broadcast_in_dim.6), calls=%async_computation.1 | async-start | bytes 262144 | tf_op jit(solution)/shard_map/all_to_all | solution.py:81
  42.0 13.8 %all-to-all-start.2 = ((f32[16,8,128]{2,1,0:T(8,128)}), f32[16,8,128]{2,1,0:T(8,128)S(1)}, u32[]{:S(2)}, u32[]{:S(2)}) async-start(f32[16,8,128]{2,1,0:T(8,128)} %reshape.706), calls=%async_computation.2 | async-start | bytes 131072 | tf_op jit(solution)/shard_map/all_to_all | solution.py:67
  56.8 7.6 %copy-start.12 = (f32[2]{0:T(128)S(1)}, f32[2]{0:T(128)}, u32[]{:S(2)}) copy-start(f32[2]{0:T(128)} %constant.164.clone) | copy-start | bytes 28
  58.9 14.4 %all-to-all-start.3 = ((f32[16,16,128]{2,1,0:T(8,128)}), f32[16,16,128]{2,1,0:T(8,128)S(1)}, u32[]{:S(2)}, u32[]{:S(2)}) async-start(f32[16,16,128]{2,1,0:T(8,128)} %reshape.709), calls=%async_computation.3 | async-start | bytes 262144 | tf_op jit(solution)/shard_map/all_to_all | solution.py:67
  78.2 11.7 %all-to-all-start.4 = ((f32[16,16,128]{2,1,0:T(8,128)}), f32[16,16,128]{2,1,0:T(8,128)S(1)}, u32[]{:S(2)}, u32[]{:S(2)}) async-start(f32[16,16,128]{2,1,0:T(8,128)} %reshape.712), calls=%async_computation.4 | async-start | bytes 262144 | tf_op jit(solution)/shard_map/all_to_all | solution.py:67
  90.2 1.7 copy-start
  90.6 1.3 copy-start.2
  90.7 1.4 copy-start.13
  91.9 1.5 copy-start.1
  92.1 5.9 %copy-start.8 = (s32[16]{0:T(128)S(1)}, s32[16]{0:T(128)}, u32[]{:S(2)}) copy-start(s32[16]{0:T(128)} %copy-done.7) | copy-start | bytes 196
  92.1 5.9 %copy-start.15 = (s32[128]{0:T(128)S(1)}, s32[128]{0:T(128)}, u32[]{:S(2)}) copy-start(s32[128]{0:T(128)} %iota_multiply_fusion) | copy-start | bytes 1540
  93.0 13.5 %copy-start.3 = (f32[2,128,2,128,1]{3,1,2,0,4:T(8,128)S(1)}, f32[2,128,2,128,1]{3,1,2,0,4:T(8,128)}, u32[]{:S(2)}) copy-start(f32[2,128,2,128,1]{3,1,2,0,4:T(8,128)} %get-tuple-element.8) | copy-start | bytes 786436
  93.4 14.9 %copy-start.14 = (s32[8]{0:T(128)S(1)}, s32[8]{0:T(128)}, u32[]{:S(2)}) copy-start(s32[8]{0:T(128)} %get-tuple-element.30) | copy-start | bytes 100
  94.5 11.7 %all-to-all-start.5 = ((f32[16,16,128]{2,1,0:T(8,128)}), f32[16,16,128]{2,1,0:T(8,128)S(1)}, u32[]{:S(2)}, u32[]{:S(2)}) async-start(f32[16,16,128]{2,1,0:T(8,128)} %copy.105), calls=%async_computation.5 | async-start | bytes 262144 | tf_op jit(solution)/shard_map/all_to_all | solution.py:67
  109.2 13.4 %copy-start.6 = (f32[2,128,2,128]{3,1,2,0:T(8,128)S(1)}, f32[2,128,2,128]{3,1,2,0:T(8,128)}, u32[]{:S(2)}) copy-start(f32[2,128,2,128]{3,1,2,0:T(8,128)} %get-tuple-element.7) | copy-start | bytes 786436
  124.4 11.3 %copy-start.11 = (s32[704]{0:T(1024)S(1)}, s32[704]{0:T(1024)}, u32[]{:S(2)}) copy-start(s32[704]{0:T(1024)} %copy-done.10) | copy-start | bytes 8452
  135.1 20.7 %copy-start.4 = (f32[704,256]{1,0:T(8,128)S(1)}, f32[704,256]{1,0:T(8,128)}, u32[]{:S(2)}) copy-start(f32[704,256]{1,0:T(8,128)} %param.12) | copy-start | bytes 2162692
  135.1 20.7 %copy-start.5 = (f32[704,256]{1,0:T(8,128)S(1)}, f32[704,256]{1,0:T(8,128)}, u32[]{:S(2)}) copy-start(f32[704,256]{1,0:T(8,128)} %pos_ref.1) | copy-start | bytes 2162692
  151.0 13.2 %all-to-all-start.9 = ((f32[16,11,128]{2,1,0:T(8,128)}), f32[16,11,128]{2,1,0:T(8,128)S(1)}, u32[]{:S(2)}, u32[]{:S(2)}) async-start(f32[16,11,128]{2,1,0:T(8,128)} %broadcast_in_dim.7), calls=%async_computation.9 | async-start | bytes 262144 | tf_op jit(solution)/shard_map/all_to_all | solution.py:81

commit v7 on v6

--- a/solution.py
+++ b/solution.py
@@ -83,6 +83,35 @@
 
 KICK_ROWS = 352
 SUB_ROWS = 32
+
+
+def profile_kernel(pos_ref, out_ref):
+    def sub_block(i, carry):
+        rows = pl.ds(pl.multiple_of(i * SUB_ROWS, SUB_ROWS), SUB_ROWS)
+        place = pos_ref[rows, :]
+        for j in range(BINS):
+            offset = place - (j + 0.5)
+            table = jnp.exp(-0.5 * offset * offset)
+            out_ref[rows, j : j + 1] = jnp.sum(table, axis=1, keepdims=True)
+        return carry
+
+    lax.fori_loop(0, KICK_ROWS // SUB_ROWS, sub_block, 0)
+
+
+def profile_call(positions):
+    bunches, width = positions.shape
+    return pl.pallas_call(
+        profile_kernel,
+        grid=(bunches // KICK_ROWS,),
+        in_specs=[pl.BlockSpec((KICK_ROWS, width), lambda i: (i, 0))],
+        out_specs=pl.BlockSpec((KICK_ROWS, BINS), lambda i: (i, 0)),
+        out_shape=jax.ShapeDtypeStruct((bunches, BINS), jnp.float32),
+        cost_estimate=pl.CostEstimate(
+            flops=5 * bunches * width * BINS,
+            transcendentals=bunches * width * BINS,
+            bytes_accessed=4 * bunches * (width + BINS),
+        ),
+    )(positions)
 
 
 def kick_kernel(pos_ref, drift_ref, volt_ref, pos_out, en_out):
@@ -139,7 +168,7 @@
     per_row = N3 // BINS
     row_buckets = second_len * per_row
     own_rows = R2 * per_row
-    partial_value = jnp.sum(kernel_table(positions), axis=2) / float(P_DEV * domains)
+    partial_value = profile_call(positions) / float(P_DEV * domains)
     first_row = bucket // row_buckets
     within = bucket % row_buckets
     owner_dom = within // own_rows

time: 174 us -> 177 us (1.017)
  Pallas kernels: 7.7 us -> 15.3 us
  other arithmetic: 16.7 us -> 9.1 us
  waiting for transfers between devices: 48.2 us -> 51.1 us
    pallas_call x0 -> x1, Pallas kernels: none -> 7.63 us  [profile_call(): pl.pallas_call(profile_kernel, grid=(bunches // KICK_ROWS,), in_specs=[pl...]
    reduce_sum x1 -> x0, other arithmetic: 5.72 us -> none  [on_device(): jnp.sum(kernel_table(positions), axis=2) / float(P_DEV * domains)]
  transfers between devices with their start and end apart: 7 -> 7, of which waited for: 7 -> 7; matrix products, arithmetic and copies ran while one was open for 6% -> 4% of each run, Pallas kernels for 0% -> 0%
where the time goes in v7:
time: 177 us; the launch traced here: 176 us
  waiting for transfers between devices  51.1 us (29%)
  starting transfers between devices  37.9 us (21%)
  blocking collectives  35.7 us (20%)
  local copies, waits for them, and re-layouts  17.5 us (10%)
  Pallas kernels  15.3 us (9%)
  other arithmetic  9.1 us (5%)
  matrix products  8.15 us (5%)
    all_to_all x4, waiting for transfers between devices, exchange(): lax.all_to_all(sent, axis_name, 0, 0, tiled=True).reshape((count,) + piece)  31.6 us
    all_to_all x2, blocking collectives, exchange(): lax.all_to_all(sent, axis_name, 0, 0, tiled=True).reshape((count,) + piece)  22.9 us
    all_to_all x4, starting transfers between devices, exchange(): lax.all_to_all(sent, axis_name, 0, 0, tiled=True).reshape((count,) + piece)  18.6 us
    all_to_all x1, blocking collectives, dom_sum(): lax.all_to_all(rows.reshape(domains, -1, 128), 'dom', 0, 0, tiled=True)  12.8 us
    all_to_all x2, waiting for transfers between devices, dom_sum(): return lax.all_to_all(spread, 'dom', 0, 0, tiled=True).reshape(rows.shape)  12.4 us
    all_to_all x1, starting transfers between devices, dom_sum(): lax.all_to_all(rows.reshape(domains, -1, 128), 'dom', 0, 0, tiled=True)  9.94 us
    all_to_all x2, starting transfers between devices, dom_sum(): return lax.all_to_all(spread, 'dom', 0, 0, tiled=True).reshape(rows.shape)  9.34 us
    dot_general x8, matrix products, contract(): return jnp.einsum(pattern, operand, matrix, precision=highest)  8.15 us
  transfers between devices with their start and end apart: 7, of which 7 were waited for; matrix products, arithmetic and copies ran while one was open for 4% of the time, Pallas kernels for 0%

profile of v7, /device:TPU:2, one launch (start us, length us, event | category | flops | bytes accessed | tf_op | source)
XLA Modules:
  0.0 175.9 jit_solution(9739953740524688550)
XLA Ops:
  0.6 7.6 %shard_map.130 = f32[704,32]{1,0:T(8,128)} custom-call(f32[704,256]{1,0:T(8,128)} %pos_ref.3), custom_call_target="tpu_custom_call" | custom-call | flops 28835840 | bytes 811008 | tf_op jit(solution)/shard_map/pallas_call | solution.py:103
  8.3 1.0 broadcast_multiply_fusion
  9.3 0.8 reshape.698
  10.1 9.9 %all-to-all-start = ((f32[16,11,128]{2,1,0:T(8,128)}), f32[16,11,128]{2,1,0:T(8,128)S(1)}, u32[]{:S(2)}, u32[]{:S(2)}) async-start(f32[16,11,128]{2,1,0:T(8,128)} %reshape.698), calls=%async_computation | async-start | bytes 262144 | tf_op jit(solution)/shard_map/all_to_all | solution.py:78
  20.4 1.0 fusion.30
  21.4 7.1 %all-to-all-done = f32[16,11,128]{2,1,0:T(8,128)S(1)} async-done(((f32[16,11,128]{2,1,0:T(8,128)}), f32[16,11,128]{2,1,0:T(8,128)S(1)}, u32[]{:S(2)}, u32[]{:S(2)}) %all-to-all-start) | async-done | bytes 90144 | tf_op jit(solution)/shard_map/all_to_all | solution.py:78
  28.5 0.7 broadcast_in_dim.6
  29.2 4.6 %all-to-all-start.1 = ((f32[16,11,128]{2,1,0:T(8,128)}), f32[16,11,128]{2,1,0:T(8,128)S(1)}, u32[]{:S(2)}, u32[]{:S(2)}) async-start(f32[16,11,128]{2,1,0:T(8,128)} %broadcast_in_dim.6), calls=%async_computation.1 | async-start | bytes 262144 | tf_op jit(solution)/shard_map/all_to_all | solution.py:81
  34.0 1.0 fusion.28
  35.0 7.2 %all-to-all-done.1 = f32[16,11,128]{2,1,0:T(8,128)S(1)} async-done(((f32[16,11,128]{2,1,0:T(8,128)}), f32[16,11,128]{2,1,0:T(8,128)S(1)}, u32[]{:S(2)}, u32[]{:S(2)}) %all-to-all-start.1) | async-done | bytes 90144 | tf_op jit(solution)/shard_map/all_to_all | solution.py:81
  42.3 0.9 fusion.1
  43.4 0.4 copy.68
  43.8 1.1 reshape.701
  44.9 6.1 %all-to-all-start.2 = ((f32[16,8,128]{2,1,0:T(8,128)}), f32[16,8,128]{2,1,0:T(8,128)S(1)}, u32[]{:S(2)}, u32[]{:S(2)}) async-start(f32[16,8,128]{2,1,0:T(8,128)} %reshape.701), calls=%async_computation.2 | async-start | bytes 131072 | tf_op jit(solution)/shard_map/all_to_all | solution.py:67
  51.3 7.4 %all-to-all-done.2 = f32[16,8,128]{2,1,0:T(8,128)S(1)} async-done(((f32[16,8,128]{2,1,0:T(8,128)}), f32[16,8,128]{2,1,0:T(8,128)S(1)}, u32[]{:S(2)}, u32[]{:S(2)}) %all-to-all-start.2) | async-done | bytes 65568 | tf_op jit(solution)/shard_map/all_to_all | solution.py:67
  58.9 0.6 copy.70
  59.9 0.3 multiply_subtract_fusion.4
  60.3 0.5 copy.72
  60.8 1.0 reshape.704
  61.8 5.3 %all-to-all-start.3 = ((f32[16,16,128]{2,1,0:T(8,128)}), f32[16,16,128]{2,1,0:T(8,128)S(1)}, u32[]{:S(2)}, u32[]{:S(2)}) async-start(f32[16,16,128]{2,1,0:T(8,128)} %reshape.704), calls=%async_computation.3 | async-start | bytes 262144 | tf_op jit(solution)/shard_map/all_to_all | solution.py:67
  67.1 0.9 multiply_multiply_fusion
  68.0 8.1 %all-to-all-done.3 = f32[16,16,128]{2,1,0:T(8,128)S(1)} async-done(((f32[16,16,128]{2,1,0:T(8,128)}), f32[16,16,128]{2,1,0:T(8,128)S(1)}, u32[]{:S(2)}, u32[]{:S(2)}) %all-to-all-start.3) | async-done | bytes 131104 | tf_op jit(solution)/shard_map/all_to_all | solution.py:67
  76.7 0.4 copy.75
  77.4 1.8 %copy.76 = f32[128,2,16,8]{3,2,1,0:T(8,128)S(1)} copy(f32[128,2,16,8]{0,2,3,1:T(8,128)S(1)} %maximum_bitcast_fusion.4) | data formatting | bytes 262144 | tf_op jit(solution)/shard_map/transpose | solution.py:63
  79.3 1.6 reshape.707
  80.9 3.7 %all-to-all-start.4 = ((f32[16,16,128]{2,1,0:T(8,128)}), f32[16,16,128]{2,1,0:T(8,128)S(1)}, u32[]{:S(2)}, u32[]{:S(2)}) async-start(f32[16,16,128]{2,1,0:T(8,128)} %reshape.707), calls=%async_computation.4 | async-start | bytes 262144 | tf_op jit(solution)/shard_map/all_to_all | solution.py:67
  84.7 8.1 %all-to-all-done.4 = f32[16,16,128]{2,1,0:T(8,128)S(1)} async-done(((f32[16,16,128]{2,1,0:T(8,128)}), f32[16,16,128]{2,1,0:T(8,128)S(1)}, u32[]{:S(2)}, u32[]{:S(2)}) %all-to-all-start.4) | async-done | bytes 131104 | tf_op jit(solution)/shard_map/all_to_all | solution.py:67
  93.1 0.4 copy.78
  93.5 0.4 reshape.726
  94.0 0.8 fusion.3
  94.9 0.9 convolution_bitcast_fusion.2
  96.3 1.1 copy.80
  97.3 3.5 %all-to-all-start.5 = ((f32[16,16,128]{2,1,0:T(8,128)}), f32[16,16,128]{2,1,0:T(8,128)S(1)}, u32[]{:S(2)}, u32[]{:S(2)}) async-start(f32[16,16,128]{2,1,0:T(8,128)} %copy.80), calls=%async_computation.5 | async-start | bytes 262144 | tf_op jit(solution)/shard_map/all_to_all | solution.py:67
  100.9 8.1 %all-to-all-done.5 = f32[16,16,128]{2,1,0:T(8,128)S(1)} async-done(((f32[16,16,128]{2,1,0:T(8,128)}), f32[16,16,128]{2,1,0:T(8,128)S(1)}, u32[]{:S(2)}, u32[]{:S(2)}) %all-to-all-start.5) | async-done | bytes 131104 | tf_op jit(solution)/shard_map/all_to_all | solution.py:67
  109.4 1.8 %convolution_bitcast_fusion.1 = f32[2,8,128,16]{2,3,1,0:T(8,128)S(1)} fusion(f32[2,128,2,128,1]{3,1,2,0,4:T(8,128)S(1)} %copy-done.3, f32[2,8,16,8,16]{4,3,1,0,2:T(8,128)S(1)} %bitcast.171), kind=kOutput, calls=%fused_computation.4 | convolution fusion | flops 100663296 | bytes 524288 | tf_op jit(solution)/shard_map/iakb,ikon->oanb/dot_general | solution.py:43
  111.1 0.4 multiply_subtract_fusion.1
  111.5 0.5 copy.85
  112.3 12.6 %all_to_all.50 = f32[16,16,128]{2,1,0:T(8,128)S(1)} all-to-all(f32[16,16,128]{2,1,0:T(8,128)S(1)} %reshape.713), channel_id=1, replica_groups=mesh['grp'=16,'dom'=16] {'dom'}, dimensions={0} | all-to-all | bytes 262144 | tf_op jit(solution)/shard_map/all_to_all | solution.py:67
  125.9 1.8 %fusion.4 = f32[128,8,16]{0,2,1:T(8,128)S(1)} fusion(f32[2,128,8,16]{3,2,1,0:T(8,128)S(1)} %bitcast.170, f32[2,128,2,128]{3,1,2,0:T(8,128)S(1)} %copy-done.6), kind=kOutput, calls=%fused_computation.11 | convolution fusion | flops 50348032 | bytes 1245184 | tf_op jit(solution)/shard_map/ikab,ikn->nab/dot_general | solution.py:43
  128.1 10.2 %all_to_all.51 = f32[16,8,128]{2,1,0:T(8,128)S(1)} all-to-all(f32[16,8,128]{2,1,0:T(8,128)S(1)} %reshape.716), channel_id=1, replica_groups=mesh['grp'=16,'dom'=16] {'grp'}, dimensions={0} | all-to-all | bytes 131072 | tf_op jit(solution)/shard_map/all_to_all | solution.py:67
  139.0 1.4 fusion
  140.6 12.8 %all_to_all.52 = f32[16,11,128]{2,1,0:T(8,128)S(1)} all-to-all(f32[16,11,128]{2,1,0:T(8,128)S(1)} %reshape.718), channel_id=1, replica_groups=mesh['grp'=16,'dom'=16] {'dom'}, dimensions={0} | all-to-all | bytes 180224 | tf_op jit(solution)/shard_map/all_to_all | solution.py:78
  153.4 0.7 broadcast_in_dim.7
  154.1 4.8 %all-to-all-start.9 = ((f32[16,11,128]{2,1,0:T(8,128)}), f32[16,11,128]{2,1,0:T(8,128)S(1)}, u32[]{:S(2)}, u32[]{:S(2)}) async-start(f32[16,11,128]{2,1,0:T(8,128)} %broadcast_in_dim.7), calls=%async_computation.9 | async-start | bytes 262144 | tf_op jit(solution)/shard_map/all_to_all | solution.py:81
  158.9 3.2 %multiply_subtract_fusion.drift_ref = f32[704,256]{1,0:T(8,128)} fusion(f32[704,256]{1,0:T(8,128)S(1)} %copy-done.4, f32[704,256]{1,0:T(8,128)S(1)} %copy-done.5), kind=kLoop, calls=%fused_computation.22 | loop fusion | flops 720896 | bytes 2162688 | tf_op jit(solution)/shard_map/sub | solution.py:245
  162.0 5.3 %all-to-all-done.9 = f32[16,11,128]{2,1,0:T(8,128)S(1)} async-done(((f32[16,11,128]{2,1,0:T(8,128)}), f32[16,11,128]{2,1,0:T(8,128)S(1)}, u32[]{:S(2)}, u32[]{:S(2)}) %all-to-all-start.9) | async-done | bytes 90144 | tf_op jit(solution)/shard_map/all_to_all | solution.py:81
  167.3 0.9 reshape.719.volt_ref
  168.2 7.7 %shard_map.131 = (f32[704,256]{1,0:T(8,128)}, f32[704,256]{1,0:T(8,128)}) custom-call(f32[704,256]{1,0:T(8,128)} %pos_ref.3, f32[704,256]{1,0:T(8,128)} %multiply_subtract_fusion.drift_ref, f32[704,32]{1,0:T(8,128)} %reshape.719.volt_ref), custom_call_target="tpu_custom_call" | custom-call | flops 69206016 | bytes 2973696 | tf_op jit(solution)/shard_map/pallas_call | solution.py:142
  (61 shorter events, 6.7 us)
Async XLA Ops:
  0.6 19.4 %copy-start.7 = (s32[704]{0:T(1024)S(1)}, s32[704]{0:T(1024)}, u32[]{:S(2)}) copy-start(s32[704]{0:T(1024)} %param.13) | copy-start | bytes 8452
  10.1 18.4 %all-to-all-start = ((f32[16,11,128]{2,1,0:T(8,128)}), f32[16,11,128]{2,1,0:T(8,128)S(1)}, u32[]{:S(2)}, u32[]{:S(2)}) async-start(f32[16,11,128]{2,1,0:T(8,128)} %reshape.698), calls=%async_computation | async-start | bytes 262144 | tf_op jit(solution)/shard_map/all_to_all | solution.py:78
  29.2 13.0 %all-to-all-start.1 = ((f32[16,11,128]{2,1,0:T(8,128)}), f32[16,11,128]{2,1,0:T(8,128)S(1)}, u32[]{:S(2)}, u32[]{:S(2)}) async-start(f32[16,11,128]{2,1,0:T(8,128)} %broadcast_in_dim.6), calls=%async_computation.1 | async-start | bytes 262144 | tf_op jit(solution)/shard_map/all_to_all | solution.py:81
  44.9 13.8 %all-to-all-start.2 = ((f32[16,8,128]{2,1,0:T(8,128)}), f32[16,8,128]{2,1,0:T(8,128)S(1)}, u32[]{:S(2)}, u32[]{:S(2)}) async-start(f32[16,8,128]{2,1,0:T(8,128)} %reshape.701), calls=%async_computation.2 | async-start | bytes 131072 | tf_op jit(solution)/shard_map/all_to_all | solution.py:67
  60.3 6.8 %copy-start.8 = (f32[2]{0:T(128)S(1)}, f32[2]{0:T(128)}, u32[]{:S(2)}) copy-start(f32[2]{0:T(128)} %constant.161.clone) | copy-start | bytes 28
  61.8 14.3 %all-to-all-start.3 = ((f32[16,16,128]{2,1,0:T(8,128)}), f32[16,16,128]{2,1,0:T(8,128)S(1)}, u32[]{:S(2)}, u32[]{:S(2)}) async-start(f32[16,16,128]{2,1,0:T(8,128)} %reshape.704), calls=%async_computation.3 | async-start | bytes 262144 | tf_op jit(solution)/shard_map/all_to_all | solution.py:67
  80.9 11.9 %all-to-all-start.4 = ((f32[16,16,128]{2,1,0:T(8,128)}), f32[16,16,128]{2,1,0:T(8,128)S(1)}, u32[]{:S(2)}, u32[]{:S(2)}) async-start(f32[16,16,128]{2,1,0:T(8,128)} %reshape.707), calls=%async_computation.4 | async-start | bytes 262144 | tf_op jit(solution)/shard_map/all_to_all | solution.py:67
  93.5 1.3 copy-start
  93.5 1.3 copy-start.2
  94.8 1.1 copy-start.1
  96.2 13.1 %copy-start.3 = (f32[2,128,2,128,1]{3,1,2,0,4:T(8,128)S(1)}, f32[2,128,2,128,1]{3,1,2,0,4:T(8,128)}, u32[]{:S(2)}) copy-start(f32[2,128,2,128,1]{3,1,2,0,4:T(8,128)} %get-tuple-element.8) | copy-start | bytes 786436
  97.3 11.7 %all-to-all-start.5 = ((f32[16,16,128]{2,1,0:T(8,128)}), f32[16,16,128]{2,1,0:T(8,128)S(1)}, u32[]{:S(2)}, u32[]{:S(2)}) async-start(f32[16,16,128]{2,1,0:T(8,128)} %copy.80), calls=%async_computation.5 | async-start | bytes 262144 | tf_op jit(solution)/shard_map/all_to_all | solution.py:67
  124.9 1.0 copy-start.6
  138.9 20.0 %copy-start.4 = (f32[704,256]{1,0:T(8,128)S(1)}, f32[704,256]{1,0:T(8,128)}, u32[]{:S(2)}) copy-start(f32[704,256]{1,0:T(8,128)} %param.12) | copy-start | bytes 2162692
  138.9 20.0 %copy-start.5 = (f32[704,256]{1,0:T(8,128)S(1)}, f32[704,256]{1,0:T(8,128)}, u32[]{:S(2)}) copy-start(f32[704,256]{1,0:T(8,128)} %pos_ref.3) | copy-start | bytes 2162692
  154.1 13.2 %all-to-all-start.9 = ((f32[16,11,128]{2,1,0:T(8,128)}), f32[16,11,128]{2,1,0:T(8,128)S(1)}, u32[]{:S(2)}, u32[]{:S(2)}) async-start(f32[16,11,128]{2,1,0:T(8,128)} %broadcast_in_dim.7), calls=%async_computation.9 | async-start | bytes 262144 | tf_op jit(solution)/shard_map/all_to_all | solution.py:81

commit v8 on v6

--- a/solution.py
+++ b/solution.py
@@ -102,7 +102,7 @@
         pos_out[rows, :] = place + 0.25 * energy
         return carry
 
-    lax.fori_loop(0, KICK_ROWS // SUB_ROWS, sub_block, 0)
+    lax.fori_loop(0, KICK_ROWS // SUB_ROWS, sub_block, 0, unroll=True)
 
 
 def kick_call(positions, drifted, volt_rows):

time: 174 us -> 173 us (level)
  no operation moved by 1% of the time
where the time goes in v8:
time: 173 us
  waiting for transfers between devices  48.2 us (28%)
  starting transfers between devices  37.9 us (22%)
  blocking collectives  35.7 us (21%)
  local copies, waits for them, and re-layouts  17.2 us (10%)
  other arithmetic  16.7 us (10%)
  matrix products  8.15 us (5%)
  Pallas kernels  7.43 us (4%)
    all_to_all x4, waiting for transfers between devices, exchange(): lax.all_to_all(sent, axis_name, 0, 0, tiled=True).reshape((count,) + piece)  30 us
    all_to_all x2, blocking collectives, exchange(): lax.all_to_all(sent, axis_name, 0, 0, tiled=True).reshape((count,) + piece)  22.7 us
    all_to_all x4, starting transfers between devices, exchange(): lax.all_to_all(sent, axis_name, 0, 0, tiled=True).reshape((count,) + piece)  18.6 us
    all_to_all x1, blocking collectives, dom_sum(): lax.all_to_all(rows.reshape(domains, -1, 128), 'dom', 0, 0, tiled=True)  13 us
    all_to_all x2, waiting for transfers between devices, dom_sum(): return lax.all_to_all(spread, 'dom', 0, 0, tiled=True).reshape(rows.shape)  11.7 us
    all_to_all x1, starting transfers between devices, dom_sum(): lax.all_to_all(rows.reshape(domains, -1, 128), 'dom', 0, 0, tiled=True)  9.94 us
    all_to_all x2, starting transfers between devices, dom_sum(): return lax.all_to_all(spread, 'dom', 0, 0, tiled=True).reshape(rows.shape)  9.34 us
    dot_general x8, matrix products, contract(): return jnp.einsum(pattern, operand, matrix, precision=highest)  8.15 us
  transfers between devices with their start and end apart: 7, of which 7 were waited for; matrix products, arithmetic and copies ran while one was open for 6% of the time, Pallas kernels for 0%

profile of v8, /device:TPU:2, one launch (start us, length us, event | category | flops | bytes accessed | tf_op | source)
XLA Modules:
  0.0 172.6 jit_solution(5175493292492272662)
XLA Ops:
  0.7 5.7 %fusion.1 = f32[704,32]{1,0:T(8,128)S(1)} fusion(f32[32]{0:T(128)S(1)} %iota_add_fusion.3, f32[704,256]{1,0:T(8,128)} %pos_ref.1), kind=kLoop, calls=%fused_computation.2 | loop fusion | flops 23046144 | bytes 811136 | tf_op jit(solution)/shard_map/reduce_sum | solution.py:142
  6.4 0.8 div.48
  7.2 9.9 %all-to-all-start = ((f32[16,11,128]{2,1,0:T(8,128)}), f32[16,11,128]{2,1,0:T(8,128)S(1)}, u32[]{:S(2)}, u32[]{:S(2)}) async-start(f32[16,11,128]{2,1,0:T(8,128)} %div.48), calls=%async_computation | async-start | bytes 262144 | tf_op jit(solution)/shard_map/all_to_all | solution.py:78
  17.2 0.5 iota_add_fusion.2
  18.0 1.0 fusion.32
  19.0 6.6 %all-to-all-done = f32[16,11,128]{2,1,0:T(8,128)S(1)} async-done(((f32[16,11,128]{2,1,0:T(8,128)}), f32[16,11,128]{2,1,0:T(8,128)S(1)}, u32[]{:S(2)}, u32[]{:S(2)}) %all-to-all-start) | async-done | bytes 90144 | tf_op jit(solution)/shard_map/all_to_all | solution.py:78
  25.6 0.7 broadcast_in_dim.6
  26.3 4.6 %all-to-all-start.1 = ((f32[16,11,128]{2,1,0:T(8,128)}), f32[16,11,128]{2,1,0:T(8,128)S(1)}, u32[]{:S(2)}, u32[]{:S(2)}) async-start(f32[16,11,128]{2,1,0:T(8,128)} %broadcast_in_dim.6), calls=%async_computation.1 | async-start | bytes 262144 | tf_op jit(solution)/shard_map/all_to_all | solution.py:81
  31.1 1.8 %fusion.30 = (f32[256,1,256]{2,0,1:T(8,128)}, f32[256,1,256]{2,0,1:T(8,128)}) fusion(), kind=kLoop, calls=%fused_computation.58 | loop fusion | flops 917504 | bytes 524288 | tf_op jit(solution)/shard_map/sin | solution.py:34
  32.9 6.4 %all-to-all-done.1 = f32[16,11,128]{2,1,0:T(8,128)S(1)} async-done(((f32[16,11,128]{2,1,0:T(8,128)}), f32[16,11,128]{2,1,0:T(8,128)S(1)}, u32[]{:S(2)}, u32[]{:S(2)}) %all-to-all-start.1) | async-done | bytes 90144 | tf_op jit(solution)/shard_map/all_to_all | solution.py:81
  39.5 0.9 fusion.3
  40.5 0.4 copy.93
  40.9 1.1 reshape.706
  42.0 6.1 %all-to-all-start.2 = ((f32[16,8,128]{2,1,0:T(8,128)}), f32[16,8,128]{2,1,0:T(8,128)S(1)}, u32[]{:S(2)}, u32[]{:S(2)}) async-start(f32[16,8,128]{2,1,0:T(8,128)} %reshape.706), calls=%async_computation.2 | async-start | bytes 131072 | tf_op jit(solution)/shard_map/all_to_all | solution.py:67
  48.4 7.4 %all-to-all-done.2 = f32[16,8,128]{2,1,0:T(8,128)S(1)} async-done(((f32[16,8,128]{2,1,0:T(8,128)}), f32[16,8,128]{2,1,0:T(8,128)S(1)}, u32[]{:S(2)}, u32[]{:S(2)}) %all-to-all-start.2) | async-done | bytes 65568 | tf_op jit(solution)/shard_map/all_to_all | solution.py:67
  56.0 0.6 copy.95
  57.4 0.5 copy.97
  57.9 1.0 reshape.709
  58.9 5.5 %all-to-all-start.3 = ((f32[16,16,128]{2,1,0:T(8,128)}), f32[16,16,128]{2,1,0:T(8,128)S(1)}, u32[]{:S(2)}, u32[]{:S(2)}) async-start(f32[16,16,128]{2,1,0:T(8,128)} %reshape.709), calls=%async_computation.3 | async-start | bytes 262144 | tf_op jit(solution)/shard_map/all_to_all | solution.py:67
  64.4 0.9 multiply_multiply_fusion.1
  65.3 8.1 %all-to-all-done.3 = f32[16,16,128]{2,1,0:T(8,128)S(1)} async-done(((f32[16,16,128]{2,1,0:T(8,128)}), f32[16,16,128]{2,1,0:T(8,128)S(1)}, u32[]{:S(2)}, u32[]{:S(2)}) %all-to-all-start.3) | async-done | bytes 131104 | tf_op jit(solution)/shard_map/all_to_all | solution.py:67
  74.7 1.8 %copy.101 = f32[128,2,16,8]{3,2,1,0:T(8,128)S(1)} copy(f32[128,2,16,8]{0,2,3,1:T(8,128)S(1)} %maximum_bitcast_fusion.4) | data formatting | bytes 262144 | tf_op jit(solution)/shard_map/transpose | solution.py:63
  76.6 1.6 reshape.712
  78.2 3.5 %all-to-all-start.4 = ((f32[16,16,128]{2,1,0:T(8,128)}), f32[16,16,128]{2,1,0:T(8,128)S(1)}, u32[]{:S(2)}, u32[]{:S(2)}) async-start(f32[16,16,128]{2,1,0:T(8,128)} %reshape.712), calls=%async_computation.4 | async-start | bytes 262144 | tf_op jit(solution)/shard_map/all_to_all | solution.py:67
  81.7 1.2 maximum_bitcast_fusion
  82.9 0.5 iota_multiply_fusion
  83.4 6.5 %all-to-all-done.4 = f32[16,16,128]{2,1,0:T(8,128)S(1)} async-done(((f32[16,16,128]{2,1,0:T(8,128)}), f32[16,16,128]{2,1,0:T(8,128)S(1)}, u32[]{:S(2)}, u32[]{:S(2)}) %all-to-all-start.4) | async-done | bytes 131104 | tf_op jit(solution)/shard_map/all_to_all | solution.py:67
  90.3 0.4 copy.103
  90.7 0.4 reshape.731
  91.1 0.8 fusion.5
  92.1 0.9 convolution_bitcast_fusion.2
  93.4 1.1 copy.105
  94.5 3.5 %all-to-all-start.5 = ((f32[16,16,128]{2,1,0:T(8,128)}), f32[16,16,128]{2,1,0:T(8,128)S(1)}, u32[]{:S(2)}, u32[]{:S(2)}) async-start(f32[16,16,128]{2,1,0:T(8,128)} %copy.105), calls=%async_computation.5 | async-start | bytes 262144 | tf_op jit(solution)/shard_map/all_to_all | solution.py:67
  98.1 8.1 %all-to-all-done.5 = f32[16,16,128]{2,1,0:T(8,128)S(1)} async-done(((f32[16,16,128]{2,1,0:T(8,128)}), f32[16,16,128]{2,1,0:T(8,128)S(1)}, u32[]{:S(2)}, u32[]{:S(2)}) %all-to-all-start.5) | async-done | bytes 131104 | tf_op jit(solution)/shard_map/all_to_all | solution.py:67
  106.5 1.8 %convolution_bitcast_fusion.1 = f32[2,8,128,16]{2,3,1,0:T(8,128)S(1)} fusion(f32[2,128,2,128,1]{3,1,2,0,4:T(8,128)S(1)} %copy-done.3, f32[2,8,16,8,16]{4,3,1,0,2:T(8,128)S(1)} %bitcast.171), kind=kOutput, calls=%fused_computation.7 | convolution fusion | flops 100663296 | bytes 524288 | tf_op jit(solution)/shard_map/iakb,ikon->oanb/dot_general | solution.py:43
  108.3 0.4 multiply_subtract_fusion.1
  108.7 0.5 copy.110
  109.5 12.4 %all_to_all.50 = f32[16,16,128]{2,1,0:T(8,128)S(1)} all-to-all(f32[16,16,128]{2,1,0:T(8,128)S(1)} %reshape.718), channel_id=1, replica_groups=mesh['grp'=16,'dom'=16] {'dom'}, dimensions={0} | all-to-all | bytes 262144 | tf_op jit(solution)/shard_map/all_to_all | solution.py:67
  122.6 1.8 %fusion.6 = f32[128,8,16]{0,2,1:T(8,128)S(1)} fusion(f32[2,128,8,16]{3,2,1,0:T(8,128)S(1)} %bitcast.170, f32[2,128,2,128]{3,1,2,0:T(8,128)S(1)} %copy-done.6), kind=kOutput, calls=%fused_computation.14 | convolution fusion | flops 50348032 | bytes 1245184 | tf_op jit(solution)/shard_map/ikab,ikn->nab/dot_general | solution.py:43
  124.8 10.2 %all_to_all.51 = f32[16,8,128]{2,1,0:T(8,128)S(1)} all-to-all(f32[16,8,128]{2,1,0:T(8,128)S(1)} %reshape.721), channel_id=1, replica_groups=mesh['grp'=16,'dom'=16] {'grp'}, dimensions={0} | all-to-all | bytes 131072 | tf_op jit(solution)/shard_map/all_to_all | solution.py:67
  135.7 1.4 fusion.2
  137.3 13.0 %all_to_all.52 = f32[16,11,128]{2,1,0:T(8,128)S(1)} all-to-all(f32[16,11,128]{2,1,0:T(8,128)S(1)} %reshape.723), channel_id=1, replica_groups=mesh['grp'=16,'dom'=16] {'dom'}, dimensions={0} | all-to-all | bytes 180224 | tf_op jit(solution)/shard_map/all_to_all | solution.py:78
  150.3 0.7 broadcast_in_dim.7
  151.0 4.8 %all-to-all-start.9 = ((f32[16,11,128]{2,1,0:T(8,128)}), f32[16,11,128]{2,1,0:T(8,128)S(1)}, u32[]{:S(2)}, u32[]{:S(2)}) async-start(f32[16,11,128]{2,1,0:T(8,128)} %broadcast_in_dim.7), calls=%async_computation.9 | async-start | bytes 262144 | tf_op jit(solution)/shard_map/all_to_all | solution.py:81
  155.8 3.2 %multiply_subtract_fusion.drift_ref = f32[704,256]{1,0:T(8,128)} fusion(f32[704,256]{1,0:T(8,128)S(1)} %copy-done.4, f32[704,256]{1,0:T(8,128)S(1)} %copy-done.5), kind=kLoop, calls=%fused_computation.25 | loop fusion | flops 720896 | bytes 2162688 | tf_op jit(solution)/shard_map/sub | solution.py:216
  159.0 5.3 %all-to-all-done.9 = f32[16,11,128]{2,1,0:T(8,128)S(1)} async-done(((f32[16,11,128]{2,1,0:T(8,128)}), f32[16,11,128]{2,1,0:T(8,128)S(1)}, u32[]{:S(2)}, u32[]{:S(2)}) %all-to-all-start.9) | async-done | bytes 90144 | tf_op jit(solution)/shard_map/all_to_all | solution.py:81
  164.2 0.9 reshape.724.volt_ref
  165.1 7.4 %shard_map.130 = (f32[704,256]{1,0:T(8,128)}, f32[704,256]{1,0:T(8,128)}) custom-call(f32[704,256]{1,0:T(8,128)} %pos_ref.1, f32[704,256]{1,0:T(8,128)} %multiply_subtract_fusion.drift_ref, f32[704,32]{1,0:T(8,128)} %reshape.724.volt_ref), custom_call_target="tpu_custom_call" | custom-call | flops 69206016 | bytes 2973696 | tf_op jit(solution)/shard_map/pallas_call | solution.py:113
  (76 shorter events, 7.1 us)
Async XLA Ops:
  0.6 17.0 %copy-start.9 = (s32[704]{0:T(1024)S(1)}, s32[704]{0:T(1024)}, u32[]{:S(2)}) copy-start(s32[704]{0:T(1024)} %param.13) | copy-start | bytes 8452
  7.2 18.4 %all-to-all-start = ((f32[16,11,128]{2,1,0:T(8,128)}), f32[16,11,128]{2,1,0:T(8,128)S(1)}, u32[]{:S(2)}, u32[]{:S(2)}) async-start(f32[16,11,128]{2,1,0:T(8,128)} %div.48), calls=%async_computation | async-start | bytes 262144 | tf_op jit(solution)/shard_map/all_to_all | solution.py:78
  17.2 24.8 %copy-start.7 = (s32[16]{0:T(128)}, s32[16]{0:T(128)S(1)}, u32[]{:S(2)}) copy-start(s32[16]{0:T(128)S(1)} %iota_add_fusion.1) | copy-start | bytes 196
  17.7 24.3 %copy-start.10 = (s32[704]{0:T(1024)}, s32[704]{0:T(1024)S(1)}, u32[]{:S(2)}) copy-start(s32[704]{0:T(1024)S(1)} %fusion.74) | copy-start | bytes 8452
  26.3 13.0 %all-to-all-start.1 = ((f32[16,11,128]{2,1,0:T(8,128)}), f32[16,11,128]{2,1,0:T(8,128)S(1)}, u32[]{:S(2)}, u32[]{:S(2)}) async-start(f32[16,11,128]{2,1,0:T(8,128)} %broadcast_in_dim.6), calls=%async_computation.1 | async-start | bytes 262144 | tf_op jit(solution)/shard_map/all_to_all | solution.py:81
  42.0 13.8 %all-to-all-start.2 = ((f32[16,8,128]{2,1,0:T(8,128)}), f32[16,8,128]{2,1,0:T(8,128)S(1)}, u32[]{:S(2)}, u32[]{:S(2)}) async-start(f32[16,8,128]{2,1,0:T(8,128)} %reshape.706), calls=%async_computation.2 | async-start | bytes 131072 | tf_op jit(solution)/shard_map/all_to_all | solution.py:67
  56.8 7.6 %copy-start.12 = (f32[2]{0:T(128)S(1)}, f32[2]{0:T(128)}, u32[]{:S(2)}) copy-start(f32[2]{0:T(128)} %constant.164.clone) | copy-start | bytes 28
  58.9 14.4 %all-to-all-start.3 = ((f32[16,16,128]{2,1,0:T(8,128)}), f32[16,16,128]{2,1,0:T(8,128)S(1)}, u32[]{:S(2)}, u32[]{:S(2)}) async-start(f32[16,16,128]{2,1,0:T(8,128)} %reshape.709), calls=%async_computation.3 | async-start | bytes 262144 | tf_op jit(solution)/shard_map/all_to_all | solution.py:67
  78.2 11.7 %all-to-all-start.4 = ((f32[16,16,128]{2,1,0:T(8,128)}), f32[16,16,128]{2,1,0:T(8,128)S(1)}, u32[]{:S(2)}, u32[]{:S(2)}) async-start(f32[16,16,128]{2,1,0:T(8,128)} %reshape.712), calls=%async_computation.4 | async-start | bytes 262144 | tf_op jit(solution)/shard_map/all_to_all | solution.py:67
  90.2 1.7 copy-start
  90.6 1.3 copy-start.2
  90.7 1.4 copy-start.13
  91.9 1.5 copy-start.1
  92.1 5.9 %copy-start.8 = (s32[16]{0:T(128)S(1)}, s32[16]{0:T(128)}, u32[]{:S(2)}) copy-start(s32[16]{0:T(128)} %copy-done.7) | copy-start | bytes 196
  92.1 5.9 %copy-start.15 = (s32[128]{0:T(128)S(1)}, s32[128]{0:T(128)}, u32[]{:S(2)}) copy-start(s32[128]{0:T(128)} %iota_multiply_fusion) | copy-start | bytes 1540
  93.0 13.5 %copy-start.3 = (f32[2,128,2,128,1]{3,1,2,0,4:T(8,128)S(1)}, f32[2,128,2,128,1]{3,1,2,0,4:T(8,128)}, u32[]{:S(2)}) copy-start(f32[2,128,2,128,1]{3,1,2,0,4:T(8,128)} %get-tuple-element.8) | copy-start | bytes 786436
  93.4 14.9 %copy-start.14 = (s32[8]{0:T(128)S(1)}, s32[8]{0:T(128)}, u32[]{:S(2)}) copy-start(s32[8]{0:T(128)} %get-tuple-element.30) | copy-start | bytes 100
  94.5 11.7 %all-to-all-start.5 = ((f32[16,16,128]{2,1,0:T(8,128)}), f32[16,16,128]{2,1,0:T(8,128)S(1)}, u32[]{:S(2)}, u32[]{:S(2)}) async-start(f32[16,16,128]{2,1,0:T(8,128)} %copy.105), calls=%async_computation.5 | async-start | bytes 262144 | tf_op jit(solution)/shard_map/all_to_all | solution.py:67
  109.2 13.4 %copy-start.6 = (f32[2,128,2,128]{3,1,2,0:T(8,128)S(1)}, f32[2,128,2,128]{3,1,2,0:T(8,128)}, u32[]{:S(2)}) copy-start(f32[2,128,2,128]{3,1,2,0:T(8,128)} %get-tuple-element.7) | copy-start | bytes 786436
  124.4 11.3 %copy-start.11 = (s32[704]{0:T(1024)S(1)}, s32[704]{0:T(1024)}, u32[]{:S(2)}) copy-start(s32[704]{0:T(1024)} %copy-done.10) | copy-start | bytes 8452
  135.1 20.7 %copy-start.4 = (f32[704,256]{1,0:T(8,128)S(1)}, f32[704,256]{1,0:T(8,128)}, u32[]{:S(2)}) copy-start(f32[704,256]{1,0:T(8,128)} %param.12) | copy-start | bytes 2162692
  135.1 20.7 %copy-start.5 = (f32[704,256]{1,0:T(8,128)S(1)}, f32[704,256]{1,0:T(8,128)}, u32[]{:S(2)}) copy-start(f32[704,256]{1,0:T(8,128)} %pos_ref.1) | copy-start | bytes 2162692
  151.0 13.2 %all-to-all-start.9 = ((f32[16,11,128]{2,1,0:T(8,128)}), f32[16,11,128]{2,1,0:T(8,128)S(1)}, u32[]{:S(2)}, u32[]{:S(2)}) async-start(f32[16,11,128]{2,1,0:T(8,128)} %broadcast_in_dim.7), calls=%async_computation.9 | async-start | bytes 262144 | tf_op jit(solution)/shard_map/all_to_all | solution.py:81

commit v9 on v6

--- a/solution.py
+++ b/solution.py
@@ -147,12 +147,25 @@
     slot = jnp.where(owned_here, first_row * own_rows + within - owner_dom * own_rows, -1)
     picker = (slot[None, :] == jnp.arange(R1 * own_rows, dtype=jnp.int32)[:, None]).astype(jnp.float32)
     totals = dom_sum(partial_value, domains)
-    line_slab = contract("sb,bj->sj", picker, totals)
-    density = line_slab.reshape(R1, R2, N3)
+    in_row = within % per_row
+    row_key = jnp.where(owned_here, in_row * R1 + first_row, -1)
+    row_picker = (row_key[None, :] == jnp.arange(per_row * R1, dtype=jnp.int32)[:, None]).astype(jnp.float32)
+    lane_slot = (within - owner_dom * own_rows) // per_row
+    half = BINS // 2
+    lane_match = lane_slot[:, None] == (jnp.arange(128, dtype=jnp.int32) // half)[None, :]
+    halves = [
+        contract(
+            "sb,bl->sl",
+            row_picker,
+            jnp.where(lane_match, jnp.tile(totals[:, h * half : (h + 1) * half], (1, 128 // half)), 0.0),
+        ).reshape(per_row, R1, 128)
+        for h in range(2)
+    ]
+    send = jnp.stack(halves, axis=1).reshape(groups, R1, 128)
     first_table = block_table(first_len)
     second_table = block_table(second_len)
     third_table = block_table(N3)
-    received = exchange(density, "grp", 2, 0)
+    received = lax.all_to_all(send, "grp", 0, 0, tiled=True).reshape(first_len, R2, depth_len)
     rows = contract("nab,nok->oabk", received, first_table[0])
     second_global = domain_index * R2 + jnp.arange(R2, dtype=jnp.int32)
     depth_global = group_index * depth_len + jnp.arange(depth_len, dtype=jnp.int32)

time: 174 us -> 173 us (level)
    all_to_all x4 -> x3, waiting for transfers between devices: 30 us -> 22.6 us  [exchange(): lax.all_to_all(sent, axis_name, 0, 0, tiled=True).reshape((count,) + piece)]
    all_to_all x0 -> x1, waiting for transfers between devices: none -> 7.4 us  [on_device(): lax.all_to_all(send, 'grp', 0, 0, tiled=True)]
    all_to_all x4 -> x3, starting transfers between devices: 18.6 us -> 12.3 us  [exchange(): lax.all_to_all(sent, axis_name, 0, 0, tiled=True).reshape((count,) + piece)]
    all_to_all x0 -> x1, starting transfers between devices: none -> 6.14 us  [on_device(): lax.all_to_all(send, 'grp', 0, 0, tiled=True)]
    reshape x7 -> x6, local copies, waits for them, and re-layouts: 5.54 us -> 4.47 us  [exchange(): sent = front.reshape(count, -1, 128)]
    dot_general x8 -> x9, matrix products: 8.15 us -> 8.2 us  [contract(): return jnp.einsum(pattern, operand, matrix, precision=highest)]
where the time goes in v9:
time: 173 us; the launch traced here: 172 us
  waiting for transfers between devices  47.9 us (28%)
  starting transfers between devices  37.7 us (22%)
  blocking collectives  35.9 us (21%)
  other arithmetic  16.9 us (10%)
  local copies, waits for them, and re-layouts  16.3 us (9%)
  matrix products  8.2 us (5%)
  Pallas kernels  7.7 us (4%)
    all_to_all x2, blocking collectives, exchange(): lax.all_to_all(sent, axis_name, 0, 0, tiled=True).reshape((count,) + piece)  23.1 us
    all_to_all x3, waiting for transfers between devices, exchange(): lax.all_to_all(sent, axis_name, 0, 0, tiled=True).reshape((count,) + piece)  22.6 us
    all_to_all x1, blocking collectives, dom_sum(): lax.all_to_all(rows.reshape(domains, -1, 128), 'dom', 0, 0, tiled=True)  12.8 us
    all_to_all x3, starting transfers between devices, exchange(): lax.all_to_all(sent, axis_name, 0, 0, tiled=True).reshape((count,) + piece)  12.3 us
    all_to_all x2, waiting for transfers between devices, dom_sum(): return lax.all_to_all(spread, 'dom', 0, 0, tiled=True).reshape(rows.shape)  12 us
    all_to_all x1, starting transfers between devices, dom_sum(): lax.all_to_all(rows.reshape(domains, -1, 128), 'dom', 0, 0, tiled=True)  9.94 us
    all_to_all x2, starting transfers between devices, dom_sum(): return lax.all_to_all(spread, 'dom', 0, 0, tiled=True).reshape(rows.shape)  9.34 us
    dot_general x9, matrix products, contract(): return jnp.einsum(pattern, operand, matrix, precision=highest)  8.2 us
  transfers between devices with their start and end apart: 7, of which 7 were waited for; matrix products, arithmetic and copies ran while one was open for 6% of the time, Pallas kernels for 0%

profile of v9, /device:TPU:2, one launch (start us, length us, event | category | flops | bytes accessed | tf_op | source)
XLA Modules:
  0.0 171.8 jit_solution(5733860353054398634)
XLA Ops:
  0.7 5.7 %fusion.1 = f32[704,32]{1,0:T(8,128)S(1)} fusion(f32[32]{0:T(128)S(1)} %iota_add_fusion.3, f32[704,256]{1,0:T(8,128)} %pos_ref.1), kind=kLoop, calls=%fused_computation.2 | loop fusion | flops 23046144 | bytes 811136 | tf_op jit(solution)/shard_map/reduce_sum | solution.py:142
  6.4 0.8 div.75
  7.2 9.9 %all-to-all-start = ((f32[16,11,128]{2,1,0:T(8,128)}), f32[16,11,128]{2,1,0:T(8,128)S(1)}, u32[]{:S(2)}, u32[]{:S(2)}) async-start(f32[16,11,128]{2,1,0:T(8,128)} %div.75), calls=%async_computation | async-start | bytes 262144 | tf_op jit(solution)/shard_map/all_to_all | solution.py:78
  17.3 0.6 subtract_select_fusion
  18.6 1.0 fusion.42
  19.6 6.0 %all-to-all-done = f32[16,11,128]{2,1,0:T(8,128)S(1)} async-done(((f32[16,11,128]{2,1,0:T(8,128)}), f32[16,11,128]{2,1,0:T(8,128)S(1)}, u32[]{:S(2)}, u32[]{:S(2)}) %all-to-all-start) | async-done | bytes 90144 | tf_op jit(solution)/shard_map/all_to_all | solution.py:78
  25.6 0.7 broadcast_in_dim.11
  26.3 4.6 %all-to-all-start.1 = ((f32[16,11,128]{2,1,0:T(8,128)}), f32[16,11,128]{2,1,0:T(8,128)S(1)}, u32[]{:S(2)}, u32[]{:S(2)}) async-start(f32[16,11,128]{2,1,0:T(8,128)} %broadcast_in_dim.11), calls=%async_computation.1 | async-start | bytes 262144 | tf_op jit(solution)/shard_map/all_to_all | solution.py:81
  30.9 1.8 %fusion.40 = (f32[256,1,256]{2,0,1:T(8,128)}, f32[256,1,256]{2,0,1:T(8,128)}) fusion(), kind=kLoop, calls=%fused_computation.70 | loop fusion | flops 917504 | bytes 524288 | tf_op jit(solution)/shard_map/sin | solution.py:34
  32.6 6.7 %all-to-all-done.1 = f32[16,11,128]{2,1,0:T(8,128)S(1)} async-done(((f32[16,11,128]{2,1,0:T(8,128)}), f32[16,11,128]{2,1,0:T(8,128)S(1)}, u32[]{:S(2)}, u32[]{:S(2)}) %all-to-all-start.1) | async-done | bytes 90144 | tf_op jit(solution)/shard_map/all_to_all | solution.py:81
  40.0 0.5 convolution_bitcast_fusion.6
  40.5 0.5 convolution_bitcast_fusion.7
  40.9 0.6 copy.99
  41.6 6.1 %all-to-all-start.2 = ((f32[16,8,128]{2,1,0:T(8,128)}), f32[16,8,128]{2,1,0:T(8,128)S(1)}, u32[]{:S(2)}, u32[]{:S(2)}) async-start(f32[16,8,128]{2,1,0:T(8,128)} %bitcast.22), calls=%async_computation.2 | async-start | bytes 131072 | tf_op jit(solution)/shard_map/all_to_all | solution.py:168
  48.0 7.4 %all-to-all-done.2 = f32[16,8,128]{2,1,0:T(8,128)S(1)} async-done(((f32[16,8,128]{2,1,0:T(8,128)}), f32[16,8,128]{2,1,0:T(8,128)S(1)}, u32[]{:S(2)}, u32[]{:S(2)}) %all-to-all-start.2) | async-done | bytes 65568 | tf_op jit(solution)/shard_map/all_to_all | solution.py:168
  56.4 0.5 copy.101
  56.9 1.0 reshape.804
  57.9 5.3 %all-to-all-start.3 = ((f32[16,16,128]{2,1,0:T(8,128)}), f32[16,16,128]{2,1,0:T(8,128)S(1)}, u32[]{:S(2)}, u32[]{:S(2)}) async-start(f32[16,16,128]{2,1,0:T(8,128)} %reshape.804), calls=%async_computation.3 | async-start | bytes 262144 | tf_op jit(solution)/shard_map/all_to_all | solution.py:67
  63.2 0.9 multiply_multiply_fusion.1
  64.1 8.1 %all-to-all-done.3 = f32[16,16,128]{2,1,0:T(8,128)S(1)} async-done(((f32[16,16,128]{2,1,0:T(8,128)}), f32[16,16,128]{2,1,0:T(8,128)S(1)}, u32[]{:S(2)}, u32[]{:S(2)}) %all-to-all-start.3) | async-done | bytes 131104 | tf_op jit(solution)/shard_map/all_to_all | solution.py:67
  72.8 0.4 copy.104
  73.5 1.8 %copy.105 = f32[128,2,16,8]{3,2,1,0:T(8,128)S(1)} copy(f32[128,2,16,8]{0,2,3,1:T(8,128)S(1)} %maximum_bitcast_fusion.4) | data formatting | bytes 262144 | tf_op jit(solution)/shard_map/transpose | solution.py:63
  75.4 1.6 reshape.807
  77.0 3.5 %all-to-all-start.4 = ((f32[16,16,128]{2,1,0:T(8,128)}), f32[16,16,128]{2,1,0:T(8,128)S(1)}, u32[]{:S(2)}, u32[]{:S(2)}) async-start(f32[16,16,128]{2,1,0:T(8,128)} %reshape.807), calls=%async_computation.4 | async-start | bytes 262144 | tf_op jit(solution)/shard_map/all_to_all | solution.py:67
  80.5 1.2 maximum_bitcast_fusion
  81.7 0.5 iota_multiply_fusion
  82.3 6.4 %all-to-all-done.4 = f32[16,16,128]{2,1,0:T(8,128)S(1)} async-done(((f32[16,16,128]{2,1,0:T(8,128)}), f32[16,16,128]{2,1,0:T(8,128)S(1)}, u32[]{:S(2)}, u32[]{:S(2)}) %all-to-all-start.4) | async-done | bytes 131104 | tf_op jit(solution)/shard_map/all_to_all | solution.py:67
  89.1 0.4 copy.107
  89.5 0.4 reshape.829
  89.9 0.8 fusion.4
  90.9 0.9 convolution_bitcast_fusion.2
  92.2 1.1 copy.109
  93.3 3.5 %all-to-all-start.5 = ((f32[16,16,128]{2,1,0:T(8,128)}), f32[16,16,128]{2,1,0:T(8,128)S(1)}, u32[]{:S(2)}, u32[]{:S(2)}) async-start(f32[16,16,128]{2,1,0:T(8,128)} %copy.109), calls=%async_computation.5 | async-start | bytes 262144 | tf_op jit(solution)/shard_map/all_to_all | solution.py:67
  96.9 8.1 %all-to-all-done.5 = f32[16,16,128]{2,1,0:T(8,128)S(1)} async-done(((f32[16,16,128]{2,1,0:T(8,128)}), f32[16,16,128]{2,1,0:T(8,128)S(1)}, u32[]{:S(2)}, u32[]{:S(2)}) %all-to-all-start.5) | async-done | bytes 131104 | tf_op jit(solution)/shard_map/all_to_all | solution.py:67
  105.3 1.8 %convolution_bitcast_fusion.1 = f32[2,8,128,16]{2,3,1,0:T(8,128)S(1)} fusion(f32[2,128,2,128,1]{3,1,2,0,4:T(8,128)S(1)} %copy-done.3, f32[2,8,16,8,16]{4,3,1,0,2:T(8,128)S(1)} %bitcast.178), kind=kOutput, calls=%fused_computation.6 | convolution fusion | flops 100663296 | bytes 524288 | tf_op jit(solution)/shard_map/iakb,ikon->oanb/dot_general | solution.py:43
  107.1 0.4 multiply_subtract_fusion.1
  107.5 0.5 copy.114
  108.3 12.6 %all_to_all.50 = f32[16,16,128]{2,1,0:T(8,128)S(1)} all-to-all(f32[16,16,128]{2,1,0:T(8,128)S(1)} %reshape.813), channel_id=1, replica_groups=mesh['grp'=16,'dom'=16] {'dom'}, dimensions={0} | all-to-all | bytes 262144 | tf_op jit(solution)/shard_map/all_to_all | solution.py:67
  121.6 1.8 %fusion.5 = f32[128,8,16]{0,2,1:T(8,128)S(1)} fusion(f32[2,128,8,16]{3,2,1,0:T(8,128)S(1)} %bitcast.177, f32[2,128,2,128]{3,1,2,0:T(8,128)S(1)} %copy-done.6), kind=kOutput, calls=%fused_computation.13 | convolution fusion | flops 50348032 | bytes 1245184 | tf_op jit(solution)/shard_map/ikab,ikn->nab/dot_general | solution.py:43
  123.8 10.5 %all_to_all.51 = f32[16,8,128]{2,1,0:T(8,128)S(1)} all-to-all(f32[16,8,128]{2,1,0:T(8,128)S(1)} %reshape.816), channel_id=1, replica_groups=mesh['grp'=16,'dom'=16] {'grp'}, dimensions={0} | all-to-all | bytes 131072 | tf_op jit(solution)/shard_map/all_to_all | solution.py:67
  134.9 1.4 fusion.2
  136.5 12.8 %all_to_all.52 = f32[16,11,128]{2,1,0:T(8,128)S(1)} all-to-all(f32[16,11,128]{2,1,0:T(8,128)S(1)} %reshape.818), channel_id=1, replica_groups=mesh['grp'=16,'dom'=16] {'dom'}, dimensions={0} | all-to-all | bytes 180224 | tf_op jit(solution)/shard_map/all_to_all | solution.py:78
  149.3 0.7 broadcast_in_dim.13
  150.0 4.8 %all-to-all-start.9 = ((f32[16,11,128]{2,1,0:T(8,128)}), f32[16,11,128]{2,1,0:T(8,128)S(1)}, u32[]{:S(2)}, u32[]{:S(2)}) async-start(f32[16,11,128]{2,1,0:T(8,128)} %broadcast_in_dim.13), calls=%async_computation.9 | async-start | bytes 262144 | tf_op jit(solution)/shard_map/all_to_all | solution.py:81
  154.8 3.2 %multiply_subtract_fusion.drift_ref = f32[704,256]{1,0:T(8,128)} fusion(f32[704,256]{1,0:T(8,128)S(1)} %copy-done.4, f32[704,256]{1,0:T(8,128)S(1)} %copy-done.5), kind=kLoop, calls=%fused_computation.25 | loop fusion | flops 720896 | bytes 2162688 | tf_op jit(solution)/shard_map/sub | solution.py:229
  158.0 5.3 %all-to-all-done.9 = f32[16,11,128]{2,1,0:T(8,128)S(1)} async-done(((f32[16,11,128]{2,1,0:T(8,128)}), f32[16,11,128]{2,1,0:T(8,128)S(1)}, u32[]{:S(2)}, u32[]{:S(2)}) %all-to-all-start.9) | async-done | bytes 90144 | tf_op jit(solution)/shard_map/all_to_all | solution.py:81
  163.2 0.9 reshape.819.volt_ref
  164.1 7.7 %shard_map.130 = (f32[704,256]{1,0:T(8,128)}, f32[704,256]{1,0:T(8,128)}) custom-call(f32[704,256]{1,0:T(8,128)} %pos_ref.1, f32[704,256]{1,0:T(8,128)} %multiply_subtract_fusion.drift_ref, f32[704,32]{1,0:T(8,128)} %reshape.819.volt_ref), custom_call_target="tpu_custom_call" | custom-call | flops 69206016 | bytes 2973696 | tf_op jit(solution)/shard_map/pallas_call | solution.py:113
  (83 shorter events, 7.3 us)
Async XLA Ops:
  0.6 16.7 %copy-start.9 = (s32[704]{0:T(1024)S(1)}, s32[704]{0:T(1024)}, u32[]{:S(2)}) copy-start(s32[704]{0:T(1024)} %param.13) | copy-start | bytes 8452
  7.2 18.4 %all-to-all-start = ((f32[16,11,128]{2,1,0:T(8,128)}), f32[16,11,128]{2,1,0:T(8,128)S(1)}, u32[]{:S(2)}, u32[]{:S(2)}) async-start(f32[16,11,128]{2,1,0:T(8,128)} %div.75), calls=%async_computation | async-start | bytes 262144 | tf_op jit(solution)/shard_map/all_to_all | solution.py:78
  18.0 1.6 copy-start.7
  26.3 13.0 %all-to-all-start.1 = ((f32[16,11,128]{2,1,0:T(8,128)}), f32[16,11,128]{2,1,0:T(8,128)S(1)}, u32[]{:S(2)}, u32[]{:S(2)}) async-start(f32[16,11,128]{2,1,0:T(8,128)} %broadcast_in_dim.11), calls=%async_computation.1 | async-start | bytes 262144 | tf_op jit(solution)/shard_map/all_to_all | solution.py:81
  41.6 13.8 %all-to-all-start.2 = ((f32[16,8,128]{2,1,0:T(8,128)}), f32[16,8,128]{2,1,0:T(8,128)S(1)}, u32[]{:S(2)}, u32[]{:S(2)}) async-start(f32[16,8,128]{2,1,0:T(8,128)} %bitcast.22), calls=%async_computation.2 | async-start | bytes 131072 | tf_op jit(solution)/shard_map/all_to_all | solution.py:168
  55.8 7.4 %copy-start.11 = (f32[2]{0:T(128)S(1)}, f32[2]{0:T(128)}, u32[]{:S(2)}) copy-start(f32[2]{0:T(128)} %constant.206.clone) | copy-start | bytes 28
  57.9 14.3 %all-to-all-start.3 = ((f32[16,16,128]{2,1,0:T(8,128)}), f32[16,16,128]{2,1,0:T(8,128)S(1)}, u32[]{:S(2)}, u32[]{:S(2)}) async-start(f32[16,16,128]{2,1,0:T(8,128)} %reshape.804), calls=%async_computation.3 | async-start | bytes 262144 | tf_op jit(solution)/shard_map/all_to_all | solution.py:67
  77.0 11.7 %all-to-all-start.4 = ((f32[16,16,128]{2,1,0:T(8,128)}), f32[16,16,128]{2,1,0:T(8,128)S(1)}, u32[]{:S(2)}, u32[]{:S(2)}) async-start(f32[16,16,128]{2,1,0:T(8,128)} %reshape.807), calls=%async_computation.4 | async-start | bytes 262144 | tf_op jit(solution)/shard_map/all_to_all | solution.py:67
  89.1 1.7 copy-start
  89.5 1.3 copy-start.2
  89.5 1.4 copy-start.12
  90.7 1.5 copy-start.1
  90.9 5.9 %copy-start.8 = (s32[16]{0:T(128)S(1)}, s32[16]{0:T(128)}, u32[]{:S(2)}) copy-start(s32[16]{0:T(128)} %copy-done.7) | copy-start | bytes 196
  90.9 5.9 %copy-start.13 = (s32[128]{0:T(128)S(1)}, s32[128]{0:T(128)}, u32[]{:S(2)}) copy-start(s32[128]{0:T(128)} %iota_multiply_fusion) | copy-start | bytes 1540
  91.9 13.5 %copy-start.3 = (f32[2,128,2,128,1]{3,1,2,0,4:T(8,128)S(1)}, f32[2,128,2,128,1]{3,1,2,0,4:T(8,128)}, u32[]{:S(2)}) copy-start(f32[2,128,2,128,1]{3,1,2,0,4:T(8,128)} %get-tuple-element.10) | copy-start | bytes 786436
  93.3 11.7 %all-to-all-start.5 = ((f32[16,16,128]{2,1,0:T(8,128)}), f32[16,16,128]{2,1,0:T(8,128)S(1)}, u32[]{:S(2)}, u32[]{:S(2)}) async-start(f32[16,16,128]{2,1,0:T(8,128)} %copy.109), calls=%async_computation.5 | async-start | bytes 262144 | tf_op jit(solution)/shard_map/all_to_all | solution.py:67
  108.0 13.6 %copy-start.6 = (f32[2,128,2,128]{3,1,2,0:T(8,128)S(1)}, f32[2,128,2,128]{3,1,2,0:T(8,128)}, u32[]{:S(2)}) copy-start(f32[2,128,2,128]{3,1,2,0:T(8,128)} %get-tuple-element.9) | copy-start | bytes 786436
  123.4 11.6 %copy-start.10 = (s32[704]{0:T(1024)S(1)}, s32[704]{0:T(1024)}, u32[]{:S(2)}) copy-start(s32[704]{0:T(1024)} %get-tuple-element.24) | copy-start | bytes 8452
  134.3 20.5 %copy-start.4 = (f32[704,256]{1,0:T(8,128)S(1)}, f32[704,256]{1,0:T(8,128)}, u32[]{:S(2)}) copy-start(f32[704,256]{1,0:T(8,128)} %param.12) | copy-start | bytes 2162692
  134.3 20.5 %copy-start.5 = (f32[704,256]{1,0:T(8,128)S(1)}, f32[704,256]{1,0:T(8,128)}, u32[]{:S(2)}) copy-start(f32[704,256]{1,0:T(8,128)} %pos_ref.1) | copy-start | bytes 2162692
  150.0 13.2 %all-to-all-start.9 = ((f32[16,11,128]{2,1,0:T(8,128)}), f32[16,11,128]{2,1,0:T(8,128)S(1)}, u32[]{:S(2)}, u32[]{:S(2)}) async-start(f32[16,11,128]{2,1,0:T(8,128)} %broadcast_in_dim.13), calls=%async_computation.9 | async-start | bytes 262144 | tf_op jit(solution)/shard_map/all_to_all | solution.py:81

commit v10 on v9

--- a/solution.py
+++ b/solution.py
@@ -221,10 +221,20 @@
     part = exchange(spin, "dom", 2, 1)
     summed = contract("ikab,ikn->nab", part, conjugate(first_table)[:, :, 0, :])
     volt_part = summed * inverse_factor
-    volt_slab = exchange(volt_part, "grp", 0, 2).reshape(
-        R1 * own_rows, BINS
-    )
-    owned_volts = contract("sb,sj->bj", picker, volt_slab)
+    got = lax.all_to_all(volt_part.reshape(groups, R1, 128), "grp", 0, 0, tiled=True)
+    got = got.reshape(per_row, 2, R1, 128)
+    owned_volts = jnp.concatenate(
+        [
+            jnp.sum(
+                jnp.where(lane_match, contract("sb,sl->bl", row_picker, got[:, h].reshape(-1, 128)), 0.0).reshape(
+                    BUNCH_GRP, 128 // half, half
+                ),
+                axis=1,
+            )
+            for h in range(2)
+        ],
+        axis=1,
+    )
     volt_rows = dom_sum(owned_volts, domains)
     drifted = energies - 0.5 * jnp.sin(two_pi * (positions - 0.5 * BINS) / BINS)
     positions_out, energies_out = kick_call(positions, drifted, volt_rows)

time: 173 us -> 174 us (level)
  blocking collectives: 35.9 us -> 25.4 us
  waiting for transfers between devices: 47.9 us -> 55.5 us
  starting transfers between devices: 37.7 us -> 41.4 us
    all_to_all x2 -> x1, blocking collectives: 23.1 us -> 12.6 us  [exchange(): lax.all_to_all(sent, axis_name, 0, 0, tiled=True).reshape((count,) + piece)]
    all_to_all x0 -> x1, waiting for transfers between devices: none -> 7.61 us  [on_device(): lax.all_to_all(volt_part.reshape(groups, R1, 128), 'grp', 0, 0, tiled=True)]
    all_to_all x0 -> x1, starting transfers between devices: none -> 3.72 us  [on_device(): lax.all_to_all(volt_part.reshape(groups, R1, 128), 'grp', 0, 0, tiled=True)]
    dot_general x9 -> x10, matrix products: 8.2 us -> 7.57 us  [contract(): return jnp.einsum(pattern, operand, matrix, precision=highest)]
    reshape x6 -> x5, local copies, waits for them, and re-layouts: 4.47 us -> 4.28 us  [exchange(): sent = front.reshape(count, -1, 128)]
  transfers between devices with their start and end apart: 7 -> 8, of which waited for: 7 -> 8; matrix products, arithmetic and copies ran while one was open for 6% -> 6% of each run, Pallas kernels for 0% -> 0%
where the time goes in v10:
time: 174 us; the launch traced here: 173 us
  waiting for transfers between devices  55.5 us (32%)
  starting transfers between devices  41.4 us (24%)
  blocking collectives  25.4 us (15%)
  local copies, waits for them, and re-layouts  17.1 us (10%)
  other arithmetic  17 us (10%)
  Pallas kernels  7.7 us (4%)
  matrix products  7.57 us (4%)
    all_to_all x3, waiting for transfers between devices, exchange(): lax.all_to_all(sent, axis_name, 0, 0, tiled=True).reshape((count,) + piece)  22.5 us
    all_to_all x1, blocking collectives, dom_sum(): lax.all_to_all(rows.reshape(domains, -1, 128), 'dom', 0, 0, tiled=True)  12.8 us
    all_to_all x1, blocking collectives, exchange(): lax.all_to_all(sent, axis_name, 0, 0, tiled=True).reshape((count,) + piece)  12.6 us
    all_to_all x3, starting transfers between devices, exchange(): lax.all_to_all(sent, axis_name, 0, 0, tiled=True).reshape((count,) + piece)  12.3 us
    all_to_all x2, waiting for transfers between devices, dom_sum(): return lax.all_to_all(spread, 'dom', 0, 0, tiled=True).reshape(rows.shape)  12 us
    all_to_all x1, starting transfers between devices, dom_sum(): lax.all_to_all(rows.reshape(domains, -1, 128), 'dom', 0, 0, tiled=True)  9.94 us
    all_to_all x2, starting transfers between devices, dom_sum(): return lax.all_to_all(spread, 'dom', 0, 0, tiled=True).reshape(rows.shape)  9.34 us
    pallas_call x1, Pallas kernels, kick_call(): pl.pallas_call(kick_kernel, grid=(bunches // KICK_ROWS,), in_specs=[wide,...  7.7 us
  transfers between devices with their start and end apart: 8, of which 8 were waited for; matrix products, arithmetic and copies ran while one was open for 6% of the time, Pallas kernels for 0%

profile of v10, /device:TPU:2, one launch (start us, length us, event | category | flops | bytes accessed | tf_op | source)
XLA Modules:
  0.0 173.0 jit_solution(8063134065639643289)
XLA Ops:
  0.7 5.7 %fusion.1 = f32[704,32]{1,0:T(8,128)S(1)} fusion(f32[32]{0:T(128)S(1)} %iota_add_fusion.3, f32[704,256]{1,0:T(8,128)} %pos_ref.1), kind=kLoop, calls=%fused_computation.2 | loop fusion | flops 23046144 | bytes 811136 | tf_op jit(solution)/shard_map/reduce_sum | solution.py:142
  6.4 0.8 div.81
  7.2 9.9 %all-to-all-start = ((f32[16,11,128]{2,1,0:T(8,128)}), f32[16,11,128]{2,1,0:T(8,128)S(1)}, u32[]{:S(2)}, u32[]{:S(2)}) async-start(f32[16,11,128]{2,1,0:T(8,128)} %div.81), calls=%async_computation | async-start | bytes 262144 | tf_op jit(solution)/shard_map/all_to_all | solution.py:78
  17.6 0.7 fusion.90
  18.6 1.0 fusion.40
  19.6 6.0 %all-to-all-done = f32[16,11,128]{2,1,0:T(8,128)S(1)} async-done(((f32[16,11,128]{2,1,0:T(8,128)}), f32[16,11,128]{2,1,0:T(8,128)S(1)}, u32[]{:S(2)}, u32[]{:S(2)}) %all-to-all-start) | async-done | bytes 90144 | tf_op jit(solution)/shard_map/all_to_all | solution.py:78
  25.6 0.7 broadcast_in_dim.12
  26.3 4.6 %all-to-all-start.1 = ((f32[16,11,128]{2,1,0:T(8,128)}), f32[16,11,128]{2,1,0:T(8,128)S(1)}, u32[]{:S(2)}, u32[]{:S(2)}) async-start(f32[16,11,128]{2,1,0:T(8,128)} %broadcast_in_dim.12), calls=%async_computation.1 | async-start | bytes 262144 | tf_op jit(solution)/shard_map/all_to_all | solution.py:81
  30.9 1.8 %fusion.38 = (f32[256,1,256]{2,0,1:T(8,128)}, f32[256,1,256]{2,0,1:T(8,128)}) fusion(), kind=kLoop, calls=%fused_computation.69 | loop fusion | flops 917504 | bytes 524288 | tf_op jit(solution)/shard_map/sin | solution.py:34
  32.6 6.7 %all-to-all-done.1 = f32[16,11,128]{2,1,0:T(8,128)S(1)} async-done(((f32[16,11,128]{2,1,0:T(8,128)}), f32[16,11,128]{2,1,0:T(8,128)S(1)}, u32[]{:S(2)}, u32[]{:S(2)}) %all-to-all-start.1) | async-done | bytes 90144 | tf_op jit(solution)/shard_map/all_to_all | solution.py:81
  40.3 0.4 convolution_bitcast_fusion.6
  41.1 0.6 copy.107
  41.8 6.1 %all-to-all-start.2 = ((f32[16,8,128]{2,1,0:T(8,128)}), f32[16,8,128]{2,1,0:T(8,128)S(1)}, u32[]{:S(2)}, u32[]{:S(2)}) async-start(f32[16,8,128]{2,1,0:T(8,128)} %bitcast.22), calls=%async_computation.2 | async-start | bytes 131072 | tf_op jit(solution)/shard_map/all_to_all | solution.py:168
  48.2 7.4 %all-to-all-done.2 = f32[16,8,128]{2,1,0:T(8,128)S(1)} async-done(((f32[16,8,128]{2,1,0:T(8,128)}), f32[16,8,128]{2,1,0:T(8,128)S(1)}, u32[]{:S(2)}, u32[]{:S(2)}) %all-to-all-start.2) | async-done | bytes 65568 | tf_op jit(solution)/shard_map/all_to_all | solution.py:168
  56.6 0.5 copy.109
  57.1 1.0 reshape.808
  58.1 5.3 %all-to-all-start.3 = ((f32[16,16,128]{2,1,0:T(8,128)}), f32[16,16,128]{2,1,0:T(8,128)S(1)}, u32[]{:S(2)}, u32[]{:S(2)}) async-start(f32[16,16,128]{2,1,0:T(8,128)} %reshape.808), calls=%async_computation.3 | async-start | bytes 262144 | tf_op jit(solution)/shard_map/all_to_all | solution.py:67
  63.4 0.9 multiply_multiply_fusion.1
  64.3 8.1 %all-to-all-done.3 = f32[16,16,128]{2,1,0:T(8,128)S(1)} async-done(((f32[16,16,128]{2,1,0:T(8,128)}), f32[16,16,128]{2,1,0:T(8,128)S(1)}, u32[]{:S(2)}, u32[]{:S(2)}) %all-to-all-start.3) | async-done | bytes 131104 | tf_op jit(solution)/shard_map/all_to_all | solution.py:67
  73.7 1.8 %copy.113 = f32[128,2,16,8]{3,2,1,0:T(8,128)S(1)} copy(f32[128,2,16,8]{0,2,3,1:T(8,128)S(1)} %maximum_bitcast_fusion.4) | data formatting | bytes 262144 | tf_op jit(solution)/shard_map/transpose | solution.py:63
  75.6 1.6 reshape.811
  77.2 3.5 %all-to-all-start.4 = ((f32[16,16,128]{2,1,0:T(8,128)}), f32[16,16,128]{2,1,0:T(8,128)S(1)}, u32[]{:S(2)}, u32[]{:S(2)}) async-start(f32[16,16,128]{2,1,0:T(8,128)} %reshape.811), calls=%async_computation.4 | async-start | bytes 262144 | tf_op jit(solution)/shard_map/all_to_all | solution.py:67
  80.7 1.2 maximum_bitcast_fusion
  81.9 0.6 iota_multiply_fusion
  82.5 6.4 %all-to-all-done.4 = f32[16,16,128]{2,1,0:T(8,128)S(1)} async-done(((f32[16,16,128]{2,1,0:T(8,128)}), f32[16,16,128]{2,1,0:T(8,128)S(1)}, u32[]{:S(2)}, u32[]{:S(2)}) %all-to-all-start.4) | async-done | bytes 131104 | tf_op jit(solution)/shard_map/all_to_all | solution.py:67
  89.2 0.4 copy.115
  89.7 0.4 reshape.835
  90.1 0.8 fusion.3
  91.1 0.9 convolution_bitcast_fusion.2
  92.4 1.1 copy.117
  93.5 3.5 %all-to-all-start.5 = ((f32[16,16,128]{2,1,0:T(8,128)}), f32[16,16,128]{2,1,0:T(8,128)S(1)}, u32[]{:S(2)}, u32[]{:S(2)}) async-start(f32[16,16,128]{2,1,0:T(8,128)} %copy.117), calls=%async_computation.5 | async-start | bytes 262144 | tf_op jit(solution)/shard_map/all_to_all | solution.py:67
  97.1 8.1 %all-to-all-done.5 = f32[16,16,128]{2,1,0:T(8,128)S(1)} async-done(((f32[16,16,128]{2,1,0:T(8,128)}), f32[16,16,128]{2,1,0:T(8,128)S(1)}, u32[]{:S(2)}, u32[]{:S(2)}) %all-to-all-start.5) | async-done | bytes 131104 | tf_op jit(solution)/shard_map/all_to_all | solution.py:67
  105.5 1.8 %convolution_bitcast_fusion.1 = f32[2,8,128,16]{2,3,1,0:T(8,128)S(1)} fusion(f32[2,128,2,128,1]{3,1,2,0,4:T(8,128)S(1)} %copy-done.3, f32[2,8,16,8,16]{4,3,1,0,2:T(8,128)S(1)} %bitcast.185), kind=kOutput, calls=%fused_computation.6 | convolution fusion | flops 100663296 | bytes 524288 | tf_op jit(solution)/shard_map/iakb,ikon->oanb/dot_general | solution.py:43
  107.7 0.5 copy.122
  108.5 12.6 %all_to_all.50 = f32[16,16,128]{2,1,0:T(8,128)S(1)} all-to-all(f32[16,16,128]{2,1,0:T(8,128)S(1)} %reshape.817), channel_id=1, replica_groups=mesh['grp'=16,'dom'=16] {'dom'}, dimensions={0} | all-to-all | bytes 262144 | tf_op jit(solution)/shard_map/all_to_all | solution.py:67
  121.8 1.8 %fusion.4 = f32[128,8,16]{0,2,1:T(8,128)S(1)} fusion(f32[2,128,8,16]{3,2,1,0:T(8,128)S(1)} %bitcast.184, f32[2,128,2,128]{3,1,2,0:T(8,128)S(1)} %copy-done.6), kind=kOutput, calls=%fused_computation.13 | convolution fusion | flops 50348032 | bytes 1245184 | tf_op jit(solution)/shard_map/ikab,ikn->nab/dot_general | solution.py:43
  123.8 0.8 reshape.820
  124.6 3.7 %all-to-all-start.7 = ((f32[16,8,128]{2,1,0:T(8,128)}), f32[16,8,128]{2,1,0:T(8,128)S(1)}, u32[]{:S(2)}, u32[]{:S(2)}) async-start(f32[16,8,128]{2,1,0:T(8,128)} %reshape.820), calls=%async_computation.7 | async-start | bytes 131072 | tf_op jit(solution)/shard_map/all_to_all | solution.py:224
  128.4 7.6 %all-to-all-done.7 = f32[16,8,128]{2,1,0:T(8,128)S(1)} async-done(((f32[16,8,128]{2,1,0:T(8,128)}), f32[16,8,128]{2,1,0:T(8,128)S(1)}, u32[]{:S(2)}, u32[]{:S(2)}) %all-to-all-start.7) | async-done | bytes 65568 | tf_op jit(solution)/shard_map/all_to_all | solution.py:224
  136.0 0.5 convolution_select_fusion.1
  136.5 0.5 convolution_select_fusion
  137.7 12.8 %all_to_all.51 = f32[16,11,128]{2,1,0:T(8,128)S(1)} all-to-all(f32[16,11,128]{2,1,0:T(8,128)S(1)} %reshape.824), channel_id=1, replica_groups=mesh['grp'=16,'dom'=16] {'dom'}, dimensions={0} | all-to-all | bytes 180224 | tf_op jit(solution)/shard_map/all_to_all | solution.py:78
  150.5 0.7 broadcast_in_dim.15
  151.2 4.8 %all-to-all-start.9 = ((f32[16,11,128]{2,1,0:T(8,128)}), f32[16,11,128]{2,1,0:T(8,128)S(1)}, u32[]{:S(2)}, u32[]{:S(2)}) async-start(f32[16,11,128]{2,1,0:T(8,128)} %broadcast_in_dim.15), calls=%async_computation.9 | async-start | bytes 262144 | tf_op jit(solution)/shard_map/all_to_all | solution.py:81
  156.0 3.2 %multiply_subtract_fusion.drift_ref = f32[704,256]{1,0:T(8,128)} fusion(f32[704,256]{1,0:T(8,128)S(1)} %copy-done.4, f32[704,256]{1,0:T(8,128)S(1)} %copy-done.5), kind=kLoop, calls=%fused_computation.24 | loop fusion | flops 720896 | bytes 2162688 | tf_op jit(solution)/shard_map/sub | solution.py:239
  159.1 5.3 %all-to-all-done.9 = f32[16,11,128]{2,1,0:T(8,128)S(1)} async-done(((f32[16,11,128]{2,1,0:T(8,128)}), f32[16,11,128]{2,1,0:T(8,128)S(1)}, u32[]{:S(2)}, u32[]{:S(2)}) %all-to-all-start.9) | async-done | bytes 90144 | tf_op jit(solution)/shard_map/all_to_all | solution.py:81
  164.4 0.9 reshape.825.volt_ref
  165.3 7.7 %shard_map.130 = (f32[704,256]{1,0:T(8,128)}, f32[704,256]{1,0:T(8,128)}) custom-call(f32[704,256]{1,0:T(8,128)} %pos_ref.1, f32[704,256]{1,0:T(8,128)} %multiply_subtract_fusion.drift_ref, f32[704,32]{1,0:T(8,128)} %reshape.825.volt_ref), custom_call_target="tpu_custom_call" | custom-call | flops 69206016 | bytes 2973696 | tf_op jit(solution)/shard_map/pallas_call | solution.py:113
  (91 shorter events, 8.3 us)
Async XLA Ops:
  0.6 16.7 %copy-start.10 = (s32[704]{0:T(1024)S(1)}, s32[704]{0:T(1024)}, u32[]{:S(2)}) copy-start(s32[704]{0:T(1024)} %param.13) | copy-start | bytes 8452
  7.2 18.4 %all-to-all-start = ((f32[16,11,128]{2,1,0:T(8,128)}), f32[16,11,128]{2,1,0:T(8,128)S(1)}, u32[]{:S(2)}, u32[]{:S(2)}) async-start(f32[16,11,128]{2,1,0:T(8,128)} %div.81), calls=%async_computation | async-start | bytes 262144 | tf_op jit(solution)/shard_map/all_to_all | solution.py:78
  17.4 22.4 %copy-start.8 = (s32[16]{0:T(128)}, s32[16]{0:T(128)S(1)}, u32[]{:S(2)}) copy-start(s32[16]{0:T(128)S(1)} %iota_add_fusion.1) | copy-start | bytes 196
  26.3 13.0 %all-to-all-start.1 = ((f32[16,11,128]{2,1,0:T(8,128)}), f32[16,11,128]{2,1,0:T(8,128)S(1)}, u32[]{:S(2)}, u32[]{:S(2)}) async-start(f32[16,11,128]{2,1,0:T(8,128)} %broadcast_in_dim.12), calls=%async_computation.1 | async-start | bytes 262144 | tf_op jit(solution)/shard_map/all_to_all | solution.py:81
  41.8 13.8 %all-to-all-start.2 = ((f32[16,8,128]{2,1,0:T(8,128)}), f32[16,8,128]{2,1,0:T(8,128)S(1)}, u32[]{:S(2)}, u32[]{:S(2)}) async-start(f32[16,8,128]{2,1,0:T(8,128)} %bitcast.22), calls=%async_computation.2 | async-start | bytes 131072 | tf_op jit(solution)/shard_map/all_to_all | solution.py:168
  55.9 7.4 %copy-start.11 = (f32[2]{0:T(128)S(1)}, f32[2]{0:T(128)}, u32[]{:S(2)}) copy-start(f32[2]{0:T(128)} %constant.206.clone) | copy-start | bytes 28
  58.1 14.3 %all-to-all-start.3 = ((f32[16,16,128]{2,1,0:T(8,128)}), f32[16,16,128]{2,1,0:T(8,128)S(1)}, u32[]{:S(2)}, u32[]{:S(2)}) async-start(f32[16,16,128]{2,1,0:T(8,128)} %reshape.808), calls=%async_computation.3 | async-start | bytes 262144 | tf_op jit(solution)/shard_map/all_to_all | solution.py:67
  77.2 11.7 %all-to-all-start.4 = ((f32[16,16,128]{2,1,0:T(8,128)}), f32[16,16,128]{2,1,0:T(8,128)S(1)}, u32[]{:S(2)}, u32[]{:S(2)}) async-start(f32[16,16,128]{2,1,0:T(8,128)} %reshape.811), calls=%async_computation.4 | async-start | bytes 262144 | tf_op jit(solution)/shard_map/all_to_all | solution.py:67
  89.2 1.7 copy-start
  89.6 1.3 copy-start.2
  89.6 1.4 copy-start.12
  90.1 1.9 %copy-start.7 = (f32[8,256]{1,0:T(8,128)S(1)}, f32[8,256]{1,0:T(8,128)}, u32[]{:S(2)}) copy-start(f32[8,256]{1,0:T(8,128)} %get-tuple-element.27) | copy-start | bytes 24580
  90.9 1.5 copy-start.1
  91.0 6.0 %copy-start.9 = (s32[16]{0:T(128)S(1)}, s32[16]{0:T(128)}, u32[]{:S(2)}) copy-start(s32[16]{0:T(128)} %copy-done.8) | copy-start | bytes 196
  91.1 6.0 %copy-start.13 = (s32[128]{0:T(128)S(1)}, s32[128]{0:T(128)}, u32[]{:S(2)}) copy-start(s32[128]{0:T(128)} %iota_multiply_fusion) | copy-start | bytes 1540
  92.0 13.5 %copy-start.3 = (f32[2,128,2,128,1]{3,1,2,0,4:T(8,128)S(1)}, f32[2,128,2,128,1]{3,1,2,0,4:T(8,128)}, u32[]{:S(2)}) copy-start(f32[2,128,2,128,1]{3,1,2,0,4:T(8,128)} %get-tuple-element.10) | copy-start | bytes 786436
  93.5 11.7 %all-to-all-start.5 = ((f32[16,16,128]{2,1,0:T(8,128)}), f32[16,16,128]{2,1,0:T(8,128)S(1)}, u32[]{:S(2)}, u32[]{:S(2)}) async-start(f32[16,16,128]{2,1,0:T(8,128)} %copy.117), calls=%async_computation.5 | async-start | bytes 262144 | tf_op jit(solution)/shard_map/all_to_all | solution.py:67
  108.2 13.6 %copy-start.6 = (f32[2,128,2,128]{3,1,2,0:T(8,128)S(1)}, f32[2,128,2,128]{3,1,2,0:T(8,128)}, u32[]{:S(2)}) copy-start(f32[2,128,2,128]{3,1,2,0:T(8,128)} %get-tuple-element.9) | copy-start | bytes 786436
  124.6 11.3 %all-to-all-start.7 = ((f32[16,8,128]{2,1,0:T(8,128)}), f32[16,8,128]{2,1,0:T(8,128)S(1)}, u32[]{:S(2)}, u32[]{:S(2)}) async-start(f32[16,8,128]{2,1,0:T(8,128)} %reshape.820), calls=%async_computation.7 | async-start | bytes 131072 | tf_op jit(solution)/shard_map/all_to_all | solution.py:224
  136.9 19.0 %copy-start.4 = (f32[704,256]{1,0:T(8,128)S(1)}, f32[704,256]{1,0:T(8,128)}, u32[]{:S(2)}) copy-start(f32[704,256]{1,0:T(8,128)} %param.12) | copy-start | bytes 2162692
  137.0 19.0 %copy-start.5 = (f32[704,256]{1,0:T(8,128)S(1)}, f32[704,256]{1,0:T(8,128)}, u32[]{:S(2)}) copy-start(f32[704,256]{1,0:T(8,128)} %pos_ref.1) | copy-start | bytes 2162692
  151.2 13.2 %all-to-all-start.9 = ((f32[16,11,128]{2,1,0:T(8,128)}), f32[16,11,128]{2,1,0:T(8,128)S(1)}, u32[]{:S(2)}, u32[]{:S(2)}) async-start(f32[16,11,128]{2,1,0:T(8,128)} %broadcast_in_dim.15), calls=%async_computation.9 | async-start | bytes 262144 | tf_op jit(solution)/shard_map/all_to_all | solution.py:81

commit v11 on v9

--- a/solution.py
+++ b/solution.py
@@ -183,27 +183,24 @@
         depth_global[:, None, None] * second_freq[None, None, :], plane_len
     )
     turned = turn(cols, cos_turn, -sin_turn)
+    past_real = impedance[1, 0] * history[0, 0] - impedance[1, 1] * history[0, 1]
+    past_imag = impedance[1, 0] * history[0, 1] + impedance[1, 1] * history[0, 0]
+    for earlier in range(1, HIST):
+        past_real = past_real + (
+            impedance[earlier + 1, 0] * history[earlier, 0] - impedance[earlier + 1, 1] * history[earlier, 1]
+        )
+        past_imag = past_imag + (
+            impedance[earlier + 1, 0] * history[earlier, 1] + impedance[earlier + 1, 1] * history[earlier, 0]
+        )
+    past_real, past_imag, turned = lax.optimization_barrier((past_real, past_imag, turned))
     part = exchange(turned, "grp", 3, 1)
     full = contract("inac,inok->oack", part, third_table)
     norm_factor = 1.0 / math.sqrt(BUNCH_GRP * groups)
     spectrum = full * norm_factor
     spec_real = spectrum[0]
     spec_imag = spectrum[1]
-    volt_real = impedance[0, 0] * spec_real - impedance[0, 1] * spec_imag
-    volt_imag = impedance[0, 0] * spec_imag + impedance[0, 1] * spec_real
-    for earlier in range(HIST):
-        past_real = history[earlier, 0]
-        past_imag = history[earlier, 1]
-        volt_real = (
-            volt_real
-            + impedance[earlier + 1, 0] * past_real
-            - impedance[earlier + 1, 1] * past_imag
-        )
-        volt_imag = (
-            volt_imag
-            + impedance[earlier + 1, 0] * past_imag
-            + impedance[earlier + 1, 1] * past_real
-        )
+    volt_real = impedance[0, 0] * spec_real - impedance[0, 1] * spec_imag + past_real
+    volt_imag = impedance[0, 0] * spec_imag + impedance[0, 1] * spec_real + past_imag
     back = contract("iack,ikon->oacn", jnp.stack([volt_real, volt_imag]), conjugate(third_table))
     second_own = group_index * second_part + jnp.arange(second_part, dtype=jnp.int32)
     depth_all = jnp.arange(N3, dtype=jnp.int32)

time: 173 us -> 174 us (level)
  waiting for transfers between devices: 47.9 us -> 49.7 us
  transfers between devices with their start and end apart: 7 -> 7, of which waited for: 7 -> 7; matrix products, arithmetic and copies ran while one was open for 6% -> 5% of each run, Pallas kernels for 0% -> 0%
where the time goes in v11:
time: 174 us; the launch traced here: 173 us
  waiting for transfers between devices  49.7 us (29%)
  starting transfers between devices  37.7 us (22%)
  blocking collectives  35.9 us (21%)
  local copies, waits for them, and re-layouts  16.3 us (9%)
  other arithmetic  16 us (9%)
  matrix products  8.19 us (5%)
  Pallas kernels  7.7 us (4%)
    all_to_all x3, waiting for transfers between devices, exchange(): lax.all_to_all(sent, axis_name, 0, 0, tiled=True).reshape((count,) + piece)  23.6 us
    all_to_all x2, blocking collectives, exchange(): lax.all_to_all(sent, axis_name, 0, 0, tiled=True).reshape((count,) + piece)  23.1 us
    all_to_all x1, blocking collectives, dom_sum(): lax.all_to_all(rows.reshape(domains, -1, 128), 'dom', 0, 0, tiled=True)  12.8 us
    all_to_all x2, waiting for transfers between devices, dom_sum(): return lax.all_to_all(spread, 'dom', 0, 0, tiled=True).reshape(rows.shape)  12.7 us
    all_to_all x3, starting transfers between devices, exchange(): lax.all_to_all(sent, axis_name, 0, 0, tiled=True).reshape((count,) + piece)  12.3 us
    all_to_all x1, starting transfers between devices, dom_sum(): lax.all_to_all(rows.reshape(domains, -1, 128), 'dom', 0, 0, tiled=True)  9.94 us
    all_to_all x2, starting transfers between devices, dom_sum(): return lax.all_to_all(spread, 'dom', 0, 0, tiled=True).reshape(rows.shape)  9.34 us
    dot_general x9, matrix products, contract(): return jnp.einsum(pattern, operand, matrix, precision=highest)  8.19 us
  transfers between devices with their start and end apart: 7, of which 7 were waited for; matrix products, arithmetic and copies ran while one was open for 5% of the time, Pallas kernels for 0%

profile of v11, /device:TPU:2, one launch (start us, length us, event | category | flops | bytes accessed | tf_op | source)
XLA Modules:
  0.0 172.7 jit_solution(3743934398432539972)
XLA Ops:
  0.7 5.8 %fusion.1 = f32[704,32]{1,0:T(8,128)S(1)} fusion(f32[32]{0:T(128)S(1)} %iota_add_fusion.3, f32[704,256]{1,0:T(8,128)} %pos_ref.1), kind=kLoop, calls=%fused_computation.2 | loop fusion | flops 23046144 | bytes 811136 | tf_op jit(solution)/shard_map/reduce_sum | solution.py:142
  6.5 0.8 div.75
  7.3 9.9 %all-to-all-start = ((f32[16,11,128]{2,1,0:T(8,128)}), f32[16,11,128]{2,1,0:T(8,128)S(1)}, u32[]{:S(2)}, u32[]{:S(2)}) async-start(f32[16,11,128]{2,1,0:T(8,128)} %div.75), calls=%async_computation | async-start | bytes 262144 | tf_op jit(solution)/shard_map/all_to_all | solution.py:78
  17.4 0.6 subtract_select_fusion
  18.8 1.0 fusion.42
  19.8 5.9 %all-to-all-done = f32[16,11,128]{2,1,0:T(8,128)S(1)} async-done(((f32[16,11,128]{2,1,0:T(8,128)}), f32[16,11,128]{2,1,0:T(8,128)S(1)}, u32[]{:S(2)}, u32[]{:S(2)}) %all-to-all-start) | async-done | bytes 90144 | tf_op jit(solution)/shard_map/all_to_all | solution.py:78
  25.7 0.7 broadcast_in_dim.11
  26.4 4.6 %all-to-all-start.1 = ((f32[16,11,128]{2,1,0:T(8,128)}), f32[16,11,128]{2,1,0:T(8,128)S(1)}, u32[]{:S(2)}, u32[]{:S(2)}) async-start(f32[16,11,128]{2,1,0:T(8,128)} %broadcast_in_dim.11), calls=%async_computation.1 | async-start | bytes 262144 | tf_op jit(solution)/shard_map/all_to_all | solution.py:81
  30.9 1.0 fusion.40
  32.0 7.4 %all-to-all-done.1 = f32[16,11,128]{2,1,0:T(8,128)S(1)} async-done(((f32[16,11,128]{2,1,0:T(8,128)}), f32[16,11,128]{2,1,0:T(8,128)S(1)}, u32[]{:S(2)}, u32[]{:S(2)}) %all-to-all-start.1) | async-done | bytes 90144 | tf_op jit(solution)/shard_map/all_to_all | solution.py:81
  40.0 0.5 convolution_bitcast_fusion.6
  40.5 0.5 convolution_bitcast_fusion.7
  41.0 0.6 copy.99
  41.7 6.1 %all-to-all-start.2 = ((f32[16,8,128]{2,1,0:T(8,128)}), f32[16,8,128]{2,1,0:T(8,128)S(1)}, u32[]{:S(2)}, u32[]{:S(2)}) async-start(f32[16,8,128]{2,1,0:T(8,128)} %bitcast.24), calls=%async_computation.2 | async-start | bytes 131072 | tf_op jit(solution)/shard_map/all_to_all | solution.py:168
  48.1 7.4 %all-to-all-done.2 = f32[16,8,128]{2,1,0:T(8,128)S(1)} async-done(((f32[16,8,128]{2,1,0:T(8,128)}), f32[16,8,128]{2,1,0:T(8,128)S(1)}, u32[]{:S(2)}, u32[]{:S(2)}) %all-to-all-start.2) | async-done | bytes 65568 | tf_op jit(solution)/shard_map/all_to_all | solution.py:168
  56.5 0.5 copy.101
  57.0 1.0 reshape.670
  58.0 5.3 %all-to-all-start.3 = ((f32[16,16,128]{2,1,0:T(8,128)}), f32[16,16,128]{2,1,0:T(8,128)S(1)}, u32[]{:S(2)}, u32[]{:S(2)}) async-start(f32[16,16,128]{2,1,0:T(8,128)} %reshape.670), calls=%async_computation.3 | async-start | bytes 262144 | tf_op jit(solution)/shard_map/all_to_all | solution.py:67
  63.3 0.9 multiply_multiply_fusion.1
  64.2 8.1 %all-to-all-done.3 = f32[16,16,128]{2,1,0:T(8,128)S(1)} async-done(((f32[16,16,128]{2,1,0:T(8,128)}), f32[16,16,128]{2,1,0:T(8,128)S(1)}, u32[]{:S(2)}, u32[]{:S(2)}) %all-to-all-start.3) | async-done | bytes 131104 | tf_op jit(solution)/shard_map/all_to_all | solution.py:67
  72.9 0.4 copy.104
  73.6 1.8 %copy.105 = f32[128,2,16,8]{3,2,1,0:T(8,128)S(1)} copy(f32[128,2,16,8]{0,2,3,1:T(8,128)S(1)} %bitcast.181) | data formatting | bytes 262144 | tf_op jit(solution)/shard_map/transpose | solution.py:63
  75.5 1.6 reshape.673
  77.1 3.5 %all-to-all-start.4 = ((f32[16,16,128]{2,1,0:T(8,128)}), f32[16,16,128]{2,1,0:T(8,128)S(1)}, u32[]{:S(2)}, u32[]{:S(2)}) async-start(f32[16,16,128]{2,1,0:T(8,128)} %reshape.673), calls=%async_computation.4 | async-start | bytes 262144 | tf_op jit(solution)/shard_map/all_to_all | solution.py:67
  80.7 0.6 iota_multiply_fusion
  81.3 7.5 %all-to-all-done.4 = f32[16,16,128]{2,1,0:T(8,128)S(1)} async-done(((f32[16,16,128]{2,1,0:T(8,128)}), f32[16,16,128]{2,1,0:T(8,128)S(1)}, u32[]{:S(2)}, u32[]{:S(2)}) %all-to-all-start.4) | async-done | bytes 131104 | tf_op jit(solution)/shard_map/all_to_all | solution.py:67
  89.1 0.4 copy.107
  89.5 0.4 reshape.695
  90.0 0.8 fusion.4
  90.8 0.9 fusion.59
  91.8 0.9 convolution_bitcast_fusion.2
  93.1 1.1 copy.109
  94.1 3.5 %all-to-all-start.5 = ((f32[16,16,128]{2,1,0:T(8,128)}), f32[16,16,128]{2,1,0:T(8,128)S(1)}, u32[]{:S(2)}, u32[]{:S(2)}) async-start(f32[16,16,128]{2,1,0:T(8,128)} %copy.109), calls=%async_computation.5 | async-start | bytes 262144 | tf_op jit(solution)/shard_map/all_to_all | solution.py:67
  97.8 8.1 %all-to-all-done.5 = f32[16,16,128]{2,1,0:T(8,128)S(1)} async-done(((f32[16,16,128]{2,1,0:T(8,128)}), f32[16,16,128]{2,1,0:T(8,128)S(1)}, u32[]{:S(2)}, u32[]{:S(2)}) %all-to-all-start.5) | async-done | bytes 131104 | tf_op jit(solution)/shard_map/all_to_all | solution.py:67
  106.2 1.8 %convolution_bitcast_fusion.1 = f32[2,8,128,16]{2,3,1,0:T(8,128)S(1)} fusion(f32[2,128,2,128,1]{3,1,2,0,4:T(8,128)S(1)} %copy-done, f32[2,8,16,8,16]{4,3,1,0,2:T(8,128)S(1)} %bitcast.173), kind=kOutput, calls=%fused_computation.6 | convolution fusion | flops 100663296 | bytes 524288 | tf_op jit(solution)/shard_map/iakb,ikon->oanb/dot_general | solution.py:43
  108.0 0.4 multiply_subtract_fusion.1
  108.3 0.5 copy.114
  109.2 12.6 %all_to_all.50 = f32[16,16,128]{2,1,0:T(8,128)S(1)} all-to-all(f32[16,16,128]{2,1,0:T(8,128)S(1)} %reshape.679), channel_id=1, replica_groups=mesh['grp'=16,'dom'=16] {'dom'}, dimensions={0} | all-to-all | bytes 262144 | tf_op jit(solution)/shard_map/all_to_all | solution.py:67
  122.5 1.8 %fusion.5 = f32[128,8,16]{0,2,1:T(8,128)S(1)} fusion(f32[2,128,8,16]{3,2,1,0:T(8,128)S(1)} %bitcast.172, f32[2,128,2,128]{3,1,2,0:T(8,128)S(1)} %copy-done.3), kind=kOutput, calls=%fused_computation.13 | convolution fusion | flops 50348032 | bytes 1245184 | tf_op jit(solution)/shard_map/ikab,ikn->nab/dot_general | solution.py:43
  124.7 10.5 %all_to_all.51 = f32[16,8,128]{2,1,0:T(8,128)S(1)} all-to-all(f32[16,8,128]{2,1,0:T(8,128)S(1)} %reshape.682), channel_id=1, replica_groups=mesh['grp'=16,'dom'=16] {'grp'}, dimensions={0} | all-to-all | bytes 131072 | tf_op jit(solution)/shard_map/all_to_all | solution.py:67
  135.8 1.4 fusion.2
  137.4 12.8 %all_to_all.52 = f32[16,11,128]{2,1,0:T(8,128)S(1)} all-to-all(f32[16,11,128]{2,1,0:T(8,128)S(1)} %reshape.684), channel_id=1, replica_groups=mesh['grp'=16,'dom'=16] {'dom'}, dimensions={0} | all-to-all | bytes 180224 | tf_op jit(solution)/shard_map/all_to_all | solution.py:78
  150.2 0.7 broadcast_in_dim.13
  150.8 4.8 %all-to-all-start.9 = ((f32[16,11,128]{2,1,0:T(8,128)}), f32[16,11,128]{2,1,0:T(8,128)S(1)}, u32[]{:S(2)}, u32[]{:S(2)}) async-start(f32[16,11,128]{2,1,0:T(8,128)} %broadcast_in_dim.13), calls=%async_computation.9 | async-start | bytes 262144 | tf_op jit(solution)/shard_map/all_to_all | solution.py:81
  155.6 3.2 %multiply_subtract_fusion.drift_ref = f32[704,256]{1,0:T(8,128)} fusion(f32[704,256]{1,0:T(8,128)S(1)} %copy-done.1, f32[704,256]{1,0:T(8,128)S(1)} %copy-done.2), kind=kLoop, calls=%fused_computation.25 | loop fusion | flops 720896 | bytes 2162688 | tf_op jit(solution)/shard_map/sub | solution.py:226
  158.8 5.3 %all-to-all-done.9 = f32[16,11,128]{2,1,0:T(8,128)S(1)} async-done(((f32[16,11,128]{2,1,0:T(8,128)}), f32[16,11,128]{2,1,0:T(8,128)S(1)}, u32[]{:S(2)}, u32[]{:S(2)}) %all-to-all-start.9) | async-done | bytes 90144 | tf_op jit(solution)/shard_map/all_to_all | solution.py:81
  164.1 0.9 reshape.685.volt_ref
  165.0 7.7 %shard_map.130 = (f32[704,256]{1,0:T(8,128)}, f32[704,256]{1,0:T(8,128)}) custom-call(f32[704,256]{1,0:T(8,128)} %pos_ref.1, f32[704,256]{1,0:T(8,128)} %multiply_subtract_fusion.drift_ref, f32[704,32]{1,0:T(8,128)} %reshape.685.volt_ref), custom_call_target="tpu_custom_call" | custom-call | flops 69206016 | bytes 2973696 | tf_op jit(solution)/shard_map/pallas_call | solution.py:113
  (83 shorter events, 7.3 us)
Async XLA Ops:
  0.6 16.8 %copy-start.9 = (s32[704]{0:T(1024)S(1)}, s32[704]{0:T(1024)}, u32[]{:S(2)}) copy-start(s32[704]{0:T(1024)} %param.13) | copy-start | bytes 8452
  0.7 17.8 %copy-start.5 = (f32[3,2,8,8,256]{4,3,2,1,0:T(8,128)S(1)}, f32[3,2,8,8,256]{4,3,2,1,0:T(8,128)}, u32[]{:S(2)}) copy-start(f32[3,2,8,8,256]{4,3,2,1,0:T(8,128)} %param.14) | copy-start | bytes 1179652
  0.7 17.8 %copy-start.6 = (f32[2,2,8,8,256]{4,3,2,1,0:T(8,128)S(1)}, f32[2,2,8,8,256]{4,3,2,1,0:T(8,128)}, u32[]{:S(2)}) copy-start(f32[2,2,8,8,256]{4,3,2,1,0:T(8,128)} %param.15) | copy-start | bytes 786436
  7.3 18.4 %all-to-all-start = ((f32[16,11,128]{2,1,0:T(8,128)}), f32[16,11,128]{2,1,0:T(8,128)S(1)}, u32[]{:S(2)}, u32[]{:S(2)}) async-start(f32[16,11,128]{2,1,0:T(8,128)} %div.75), calls=%async_computation | async-start | bytes 262144 | tf_op jit(solution)/shard_map/all_to_all | solution.py:78
  18.0 1.7 copy-start.7
  26.4 13.0 %all-to-all-start.1 = ((f32[16,11,128]{2,1,0:T(8,128)}), f32[16,11,128]{2,1,0:T(8,128)S(1)}, u32[]{:S(2)}, u32[]{:S(2)}) async-start(f32[16,11,128]{2,1,0:T(8,128)} %broadcast_in_dim.11), calls=%async_computation.1 | async-start | bytes 262144 | tf_op jit(solution)/shard_map/all_to_all | solution.py:81
  41.7 13.8 %all-to-all-start.2 = ((f32[16,8,128]{2,1,0:T(8,128)}), f32[16,8,128]{2,1,0:T(8,128)S(1)}, u32[]{:S(2)}, u32[]{:S(2)}) async-start(f32[16,8,128]{2,1,0:T(8,128)} %bitcast.24), calls=%async_computation.2 | async-start | bytes 131072 | tf_op jit(solution)/shard_map/all_to_all | solution.py:168
  55.8 7.4 %copy-start.11 = (f32[2]{0:T(128)S(1)}, f32[2]{0:T(128)}, u32[]{:S(2)}) copy-start(f32[2]{0:T(128)} %constant.206.clone) | copy-start | bytes 28
  58.0 14.3 %all-to-all-start.3 = ((f32[16,16,128]{2,1,0:T(8,128)}), f32[16,16,128]{2,1,0:T(8,128)S(1)}, u32[]{:S(2)}, u32[]{:S(2)}) async-start(f32[16,16,128]{2,1,0:T(8,128)} %reshape.670), calls=%async_computation.3 | async-start | bytes 262144 | tf_op jit(solution)/shard_map/all_to_all | solution.py:67
  77.1 11.7 %all-to-all-start.4 = ((f32[16,16,128]{2,1,0:T(8,128)}), f32[16,16,128]{2,1,0:T(8,128)S(1)}, u32[]{:S(2)}, u32[]{:S(2)}) async-start(f32[16,16,128]{2,1,0:T(8,128)} %reshape.673), calls=%async_computation.4 | async-start | bytes 262144 | tf_op jit(solution)/shard_map/all_to_all | solution.py:67
  89.1 2.6 %copy-start.12 = (f32[2]{0:T(128)S(1)}, f32[2]{0:T(128)}, u32[]{:S(2)}) copy-start(f32[2]{0:T(128)} %constant.206.clone) | copy-start | bytes 28
  90.8 3.4 %copy-start.4 = (f32[2,8,8,256]{3,2,1,0:T(8,128)}, f32[2,8,8,256]{3,2,1,0:T(8,128)S(1)}, u32[]{:S(2)}) copy-start(f32[2,8,8,256]{3,2,1,0:T(8,128)S(1)} %fusion.4) | copy-start | bytes 393220
  91.7 5.9 %copy-start.8 = (s32[16]{0:T(128)S(1)}, s32[16]{0:T(128)}, u32[]{:S(2)}) copy-start(s32[16]{0:T(128)} %copy-done.7) | copy-start | bytes 196
  91.8 5.9 %copy-start.13 = (s32[128]{0:T(128)S(1)}, s32[128]{0:T(128)}, u32[]{:S(2)}) copy-start(s32[128]{0:T(128)} %iota_multiply_fusion) | copy-start | bytes 1540
  92.7 13.5 %copy-start = (f32[2,128,2,128,1]{3,1,2,0,4:T(8,128)S(1)}, f32[2,128,2,128,1]{3,1,2,0,4:T(8,128)}, u32[]{:S(2)}) copy-start(f32[2,128,2,128,1]{3,1,2,0,4:T(8,128)} %get-tuple-element.20) | copy-start | bytes 786436
  94.1 11.7 %all-to-all-start.5 = ((f32[16,16,128]{2,1,0:T(8,128)}), f32[16,16,128]{2,1,0:T(8,128)S(1)}, u32[]{:S(2)}, u32[]{:S(2)}) async-start(f32[16,16,128]{2,1,0:T(8,128)} %copy.109), calls=%async_computation.5 | async-start | bytes 262144 | tf_op jit(solution)/shard_map/all_to_all | solution.py:67
  108.8 13.6 %copy-start.3 = (f32[2,128,2,128]{3,1,2,0:T(8,128)S(1)}, f32[2,128,2,128]{3,1,2,0:T(8,128)}, u32[]{:S(2)}) copy-start(f32[2,128,2,128]{3,1,2,0:T(8,128)} %get-tuple-element.19) | copy-start | bytes 786436
  124.2 11.6 %copy-start.10 = (s32[704]{0:T(1024)S(1)}, s32[704]{0:T(1024)}, u32[]{:S(2)}) copy-start(s32[704]{0:T(1024)} %get-tuple-element.34) | copy-start | bytes 8452
  135.1 20.5 %copy-start.1 = (f32[704,256]{1,0:T(8,128)S(1)}, f32[704,256]{1,0:T(8,128)}, u32[]{:S(2)}) copy-start(f32[704,256]{1,0:T(8,128)} %param.12) | copy-start | bytes 2162692
  135.1 20.5 %copy-start.2 = (f32[704,256]{1,0:T(8,128)S(1)}, f32[704,256]{1,0:T(8,128)}, u32[]{:S(2)}) copy-start(f32[704,256]{1,0:T(8,128)} %pos_ref.1) | copy-start | bytes 2162692
  150.8 13.2 %all-to-all-start.9 = ((f32[16,11,128]{2,1,0:T(8,128)}), f32[16,11,128]{2,1,0:T(8,128)S(1)}, u32[]{:S(2)}, u32[]{:S(2)}) async-start(f32[16,11,128]{2,1,0:T(8,128)} %broadcast_in_dim.13), calls=%async_computation.9 | async-start | bytes 262144 | tf_op jit(solution)/shard_map/all_to_all | solution.py:81
